TPU v7x, 256 devices: a whole 4x4x8 slice. The times are simulated.
256 devices in a mesh: dp: 32 (over z, y), tensor: 8 (over x, core).
Axes of the slice: x: 4, y: 4, z: 8, core: 2. Of those that a mesh axis runs over, the one named last changes fastest.
Arguments:
- tokens: bfloat16 [4096, 4096], P('dp', 'tensor'), may hold values from -6 to 6
- grad_out: bfloat16 [4096, 4096], P('dp', 'tensor'), may hold values from -6 to 6
- gate_blocks: int32 [8, 32], P('tensor'), may hold values from -1 to 447, as said below
- gate_values: bfloat16 [8, 32, 128, 128], P('tensor'), may hold values from -0.375 to 0.375
- up_blocks: int32 [8, 32], P('tensor'), may hold values from -1 to 447, as said below
- up_values: bfloat16 [8, 32, 128, 128], P('tensor'), may hold values from -0.375 to 0.375
- down_blocks: int32 [8, 32], P('tensor'), may hold values from -1 to 447, as said below
- down_values: bfloat16 [8, 32, 128, 128], P('tensor'), may hold values from -0.1875 to 0.1875
Outputs:
- mixed: bfloat16 [4096, 4096], P('dp', 'tensor')
- grad_tokens: bfloat16 [4096, 4096], P('dp', 'tensor')
- grad_gate: float32 [8, 32, 128, 128], P('tensor', 'dp')
- grad_up: float32 [8, 32, 128, 128], P('tensor', 'dp')
- grad_down: float32 [8, 32, 128, 128], P('tensor', 'dp')
Inputs may be any that keep to these rules, and one draw needn't show every extreme that they name: `gate_blocks`: each row lists distinct block numbers of one tensor shard in its first slots and -1 in the rest; a row has 16 to 32 listed blocks, one row has exactly 32 and another exactly 16. `up_blocks`: as for gate_blocks, drawn apart. `down_blocks`: as for gate_blocks, drawn apart.
All inputs are finite; a program needn't handle non-finite values.
Results may differ from a plain program's by a relative error of at most 0.015.
Values may be sent and summed in bfloat16 or wider, within the bound.
No kernel may reach another device: no remote copies, remote signals or barrier semaphores. Data moves between devices by JAX's collectives and lax.ppermute only.
A program may use at most 64 MiB of HBM per device.

v0:
```python
import jax
import jax.numpy as jnp
from jax import lax
from jax.experimental import pallas as pl
from jax.experimental.pallas import tpu as pltpu
from jax.sharding import Mesh
from jax.sharding import PartitionSpec as P

FF = 14336

NT = (((1,), (1,)), ((), ()))


def _dot(a, b, dims=(((1,), (0,)), ((), ()))):
    return lax.dot_general(a, b, dims, preferred_element_type=jnp.float32)


def _front_kernel(gate_at, up_at, down_at, xb, dyb, xt, dyt, wg, wu, wd,
                  terms, hid, gdel, udel, gpre, upre, hgrad):
    inner = terms.shape[0]
    feature_count = xb.shape[0]
    slots = wg.shape[0]
    gpre[...] = jnp.zeros(gpre.shape, jnp.float32)
    upre[...] = jnp.zeros(upre.shape, jnp.float32)
    hgrad[...] = jnp.zeros(hgrad.shape, jnp.float32)

    @pl.loop(0, slots)
    def _(s):
        bg = gate_at[s]

        @pl.when(bg >= 0)
        def _():
            r, c = bg % feature_count, bg // feature_count
            gpre[c] += _dot(xb[r], wg[s])

        bu = up_at[s]

        @pl.when(bu >= 0)
        def _():
            r, c = bu % feature_count, bu // feature_count
            upre[c] += _dot(xb[r], wu[s])

        bd = down_at[s]

        @pl.when(bd >= 0)
        def _():
            r, c = bd % feature_count, bd // feature_count
            hgrad[c] += _dot(dyb[r], wd[s], NT)

    g = gpre[...]
    u = upre[...]
    hg = hgrad[...]
    sig = 1.0 / (1.0 + jnp.exp(-g))
    act = g * sig
    hid[...] = (act * u).astype(hid.dtype)
    gdel[...] = (hg * u * sig * (1.0 + g * (1.0 - sig))).astype(gdel.dtype)
    udel[...] = (hg * act).astype(udel.dtype)

    @pl.loop(0, slots)
    def _(s):
        bg = gate_at[s]

        @pl.when(bg >= 0)
        def _():
            r, c = bg % feature_count, bg // feature_count
            terms[s % inner, s // inner, 0] = _dot(xt[r], gdel[c]).astype(terms.dtype)

        @pl.when(bg < 0)
        def _():
            terms[s % inner, s // inner, 0] = jnp.zeros(terms.shape[3:], terms.dtype)

        bu = up_at[s]

        @pl.when(bu >= 0)
        def _():
            r, c = bu % feature_count, bu // feature_count
            terms[s % inner, s // inner, 1] = _dot(xt[r], udel[c]).astype(terms.dtype)

        @pl.when(bu < 0)
        def _():
            terms[s % inner, s // inner, 1] = jnp.zeros(terms.shape[3:], terms.dtype)

        bd = down_at[s]

        @pl.when(bd >= 0)
        def _():
            r, c = bd % feature_count, bd // feature_count
            terms[s % inner, s // inner, 2] = _dot(dyt[r], hid[c]).astype(terms.dtype)

        @pl.when(bd < 0)
        def _():
            terms[s % inner, s // inner, 2] = jnp.zeros(terms.shape[3:], terms.dtype)


def _back_kernel(gate_at, up_at, down_at, hid, gdel, udel, wg, wu, wd,
                 mixed, grads, macc, iacc):
    feature_count = mixed.shape[0]
    slots = wg.shape[0]
    macc[...] = jnp.zeros(macc.shape, jnp.float32)
    iacc[...] = jnp.zeros(iacc.shape, jnp.float32)

    @pl.loop(0, slots)
    def _(s):
        bd = down_at[s]

        @pl.when(bd >= 0)
        def _():
            r, c = bd % feature_count, bd // feature_count
            macc[r] += _dot(hid[c], wd[s])

        bg = gate_at[s]

        @pl.when(bg >= 0)
        def _():
            r, c = bg % feature_count, bg // feature_count
            iacc[r] += _dot(gdel[c], wg[s], NT)

        bu = up_at[s]

        @pl.when(bu >= 0)
        def _():
            r, c = bu % feature_count, bu // feature_count
            iacc[r] += _dot(udel[c], wu[s], NT)

    mixed[...] = macc[...].astype(mixed.dtype)
    grads[...] = iacc[...].astype(grads.dtype)


def _specs(n_smem, n_vmem):
    return [pl.BlockSpec(memory_space=pltpu.SMEM)] * n_smem + [
        pl.BlockSpec(memory_space=pltpu.VMEM)
    ] * n_vmem


def front(gate_at, up_at, down_at, xb, dyb, xt, dyt, wg, wu, wd, hidden_count, inner,
          interpret=False):
    feature_count, rows, size = xb.shape
    slots = wg.shape[0]
    hshape = (hidden_count, rows, size)
    return pl.pallas_call(
        _front_kernel,
        out_shape=(
            jax.ShapeDtypeStruct((inner, slots // inner, 3, size, size), jnp.bfloat16),
            jax.ShapeDtypeStruct(hshape, jnp.bfloat16),
            jax.ShapeDtypeStruct(hshape, jnp.bfloat16),
            jax.ShapeDtypeStruct(hshape, jnp.bfloat16),
        ),
        in_specs=_specs(3, 7),
        out_specs=tuple(_specs(0, 4)),
        scratch_shapes=[pltpu.VMEM(hshape, jnp.float32)] * 3,
        cost_estimate=pl.CostEstimate(
            flops=6 * slots * 2 * size**3,
            transcendentals=hidden_count * rows * size,
            bytes_accessed=(4 * feature_count * rows + 6 * slots * size + 3 * hidden_count * rows)
            * size * 2,
        ),
        interpret=interpret,
    )(gate_at, up_at, down_at, xb, dyb, xt, dyt, wg, wu, wd)


def back(gate_at, up_at, down_at, hid, gdel, udel, wg, wu, wd, feature_count, interpret=False):
    _, rows, size = hid.shape
    fshape = (feature_count, rows, size)
    return pl.pallas_call(
        _back_kernel,
        out_shape=(
            jax.ShapeDtypeStruct(fshape, jnp.bfloat16),
            jax.ShapeDtypeStruct(fshape, jnp.bfloat16),
        ),
        in_specs=_specs(3, 6),
        out_specs=tuple(_specs(0, 2)),
        scratch_shapes=[pltpu.VMEM(fshape, jnp.float32)] * 2,
        cost_estimate=pl.CostEstimate(
            flops=3 * wg.shape[0] * 2 * size**3,
            transcendentals=0,
            bytes_accessed=(3 * hid.shape[0] * rows + 3 * wg.shape[0] * size + 2 * feature_count * rows)
            * size * 2,
        ),
        interpret=interpret,
    )(gate_at, up_at, down_at, hid, gdel, udel, wg, wu, wd)


def gather_blocks(parts, axis, block_size):
    count = lax.axis_size(axis)
    spread_out = jnp.broadcast_to(parts[None], (count,) + parts.shape)
    pieces = lax.all_to_all(spread_out, axis, 0, 0, tiled=True)
    kinds, rows, width = parts.shape
    pieces = pieces.reshape(count, kinds, rows, width // block_size, block_size)
    blocks = pieces.transpose(1, 0, 3, 2, 4).reshape(kinds, -1, rows, block_size)
    flipped = pieces.transpose(1, 0, 3, 4, 2).reshape(kinds, -1, block_size, rows)
    return blocks, flipped


def scatter_blocks(full, axis):
    count = lax.axis_size(axis)
    own = lax.axis_index(axis)
    pieces = full.reshape((count, -1) + full.shape[1:])
    total = lax.dynamic_index_in_dim(pieces, own, 0, keepdims=False).astype(jnp.float32)
    for shift in range(1, count):
        outgoing = lax.dynamic_index_in_dim(pieces, (own + shift) % count, 0, keepdims=False)
        pairs = [(source, (source + shift) % count) for source in range(count)]
        total = total + lax.ppermute(outgoing, axis, pairs).astype(jnp.float32)
    return total.astype(jnp.bfloat16).transpose(1, 0, 2).reshape(full.shape[1], -1)


def reduce_inner(grid, inner):
    count = lax.axis_size(inner)
    own = lax.axis_index(inner)
    total = lax.dynamic_index_in_dim(grid, own, 0, keepdims=False).astype(jnp.float32)
    for shift in range(1, count):
        outgoing = lax.dynamic_index_in_dim(grid, (own + shift) % count, 0, keepdims=False)
        pairs = [(source, (source + shift) % count) for source in range(count)]
        total = total + lax.ppermute(outgoing, inner, pairs).astype(jnp.float32)
    return total.astype(jnp.bfloat16)


def reduce_outer(grid, outer):
    grid = lax.all_to_all(grid, outer, 0, 0, tiled=True)
    return grid.astype(jnp.float32).sum(0)


def layer(
    tokens, grad_out, gate_blocks, gate_values, up_blocks, up_values, down_blocks, down_values
):
    block_size = gate_values.shape[-1]
    tensor_count = lax.axis_size("tensor")
    feature_count = tokens.shape[1] * tensor_count // block_size
    hidden_count = FF // (block_size * tensor_count)
    (inputs, upstream), (inputs_t, upstream_t) = gather_blocks(
        jnp.stack([tokens, grad_out]), "tensor", block_size
    )
    gate_at, up_at, down_at = gate_blocks[0], up_blocks[0], down_blocks[0]
    weights = (gate_values[0], up_values[0], down_values[0])
    stacked, hidden, gate_delta, up_delta = front(
        gate_at, up_at, down_at, inputs, upstream, inputs_t, upstream_t, *weights, hidden_count,
        lax.axis_size("y"),
    )
    partial = reduce_inner(stacked, "y")
    mixed_part, input_part = back(
        gate_at, up_at, down_at, hidden, gate_delta, up_delta, *weights, feature_count
    )
    mixed = scatter_blocks(mixed_part, "tensor")
    grad_tokens = scatter_blocks(input_part, "tensor")
    combined = reduce_outer(partial, "z")[None]
    grad_gate = combined[None, :, 0]
    grad_up = combined[None, :, 1]
    grad_down = combined[None, :, 2].swapaxes(-1, -2)
    return (mixed, grad_tokens, grad_gate, grad_up, grad_down)


def solution(mesh):
    dp_count, tensor_count = mesh.devices.shape
    y_count = len({device.coords[1] for device in mesh.devices[:, 0]})
    split_mesh = Mesh(
        mesh.devices.reshape(dp_count // y_count, y_count, tensor_count), ("z", "y", "tensor")
    )
    dp = ("z", "y")
    in_specs = (
        P(dp, "tensor"),
        P(dp, "tensor"),
        P("tensor", None),
        P("tensor", None, None, None),
        P("tensor", None),
        P("tensor", None, None, None),
        P("tensor", None),
        P("tensor", None, None, None),
    )
    out_specs = (
        P(dp, "tensor"),
        P(dp, "tensor"),
        P("tensor", dp, None, None),
        P("tensor", dp, None, None),
        P("tensor", dp, None, None),
    )
    return jax.shard_map(
        layer, mesh=split_mesh, in_specs=in_specs, out_specs=out_specs, check_vma=False
    )
```

profile of v0, /device:TPU:8, one launch (start us, length us, event | category | flops | bytes accessed | tf_op | source)
XLA Modules:
  0.0 174.2 jit_solution(360159063986199720)
XLA Ops:
  0.6 1.0 pad_maximum_fusion
  1.6 0.2 copy.20
  1.8 1.8 %broadcast_in_dim.4 = bf16[8,2,128,512]{2,3,1,0:T(8,128)(2,1)} broadcast(bf16[2,128,512]{1,2,0:T(8,128)(2,1)S(1)} %copy.20), dimensions={1,2,3} | broadcast | bytes 2359296 | tf_op jit(solution)/shard_map/broadcast_in_dim | solution.py:185
  3.6 4.3 %all-to-all-start = ((bf16[8,2,128,512]{2,3,1,0:T(8,128)(2,1)}), bf16[8,2,128,512]{2,3,1,0:T(8,128)(2,1)S(1)}, u32[]{:S(2)}, u32[]{:S(2)}) async-start(bf16[8,2,128,512]{2,3,1,0:T(8,128)(2,1)} %broadcast_in_dim.4), calls=%async_computation | async-start | bytes 4194304 | tf_op jit(solution)/shard_map/all_to_all | solution.py:186
  7.9 27.2 %all-to-all-done = bf16[8,2,128,512]{2,3,1,0:T(8,128)(2,1)S(1)} async-done(((bf16[8,2,128,512]{2,3,1,0:T(8,128)(2,1)}), bf16[8,2,128,512]{2,3,1,0:T(8,128)(2,1)S(1)}, u32[]{:S(2)}, u32[]{:S(2)}) %all-to-all-start) | async-done | bytes 2097184 | tf_op jit(solution)/shard_map/all_to_all | solution.py:186
  35.0 2.6 %copy.21 = bf16[8,2,128,4,128]{4,2,3,0,1:T(8,128)(2,1)} copy(bf16[8,2,128,4,128]{2,4,3,1,0:T(8,128)(2,1)S(1)} %bitcast.79) | data formatting | bytes 4194304 | tf_op jit(solution)/shard_map/reshape | solution.py:188
  37.6 0.1 copy.31
  37.8 1.4 copy-done
  39.2 1.5 fusion.20
  40.7 1.5 fusion.19
  42.2 26.1 %shard_map.119 = (bf16[4,8,3,128,128]{4,3,2,1,0:T(8,128)(2,1)}, bf16[14,128,128]{2,1,0:T(8,128)(2,1)}, bf16[14,128,128]{2,1,0:T(8,128)(2,1)}, bf16[14,128,128]{2,1,0:T(8,128)(2,1)}) custom-call(s32[32]{0:T(128)} %bitcast.100, s32[32]{0:T(128)} %bitcast.102, s32[32]{0:T(128)} %bitcast.104, bf16[32,128,128]{2,1,0:T(8,128)(2,1)} %bitcast.90, ...), custom_call_target="tpu_custom_call" | custom-call | flops 805306368 | bytes 11862016 | tf_op jit(solution)/shard_map/pallas_call | solution.py:140
  68.3 3.0 %dynamic-slice_bitcast_fusion.2 = (bf16[8,3,128,128]{3,2,1,0:T(8,128)(2,1)S(1)}, bf16[8,3,128,128]{3,2,1,0:T(8,128)(2,1)}, bf16[8,3,128,128]{3,2,1,0:T(8,128)(2,1)}) fusion(bf16[4,8,3,128,128]{4,3,2,1,0:T(8,128)(2,1)} %get-tuple-element.16, s32[]{:T(128)S(6)} %select_n.120, s32[]{:T(128)S(6)} %select_n.124, s32[]{:T(128)S(6)} %select_n.122), kind=kLoop, calls=%fused_computation.8 | loop fusion | bytes 4718604 | tf_op jit(solution)/shard_map/jit(dynamic_index_in_dim)/squeeze | solution.py:211
  71.4 1.4 collective-permute-start.16
  72.8 1.6 collective-permute-start.15
  74.4 1.9 %collective-permute-start.14 = (bf16[8,3,128,128]{3,2,1,0:T(8,128)(2,1)S(1)}, bf16[8,3,128,128]{3,2,1,0:T(8,128)(2,1)S(1)}, u32[]{:S(2)}, u32[]{:S(2)}) collective-permute-start(bf16[8,3,128,128]{3,2,1,0:T(8,128)(2,1)S(1)} %get-tuple-element.27), channel_id=1, source_target_pairs={{0,8},{8,16},{16,24},{24,0},{1,9},{9,17},{17,25},{25,1},{2,10},{10... | collective-permute-start | bytes 2359304 | tf_op jit(solution)/shard_map/ppermute | solution.py:213
  76.3 14.7 %collective-permute-done.16 = bf16[8,3,128,128]{3,2,1,0:T(8,128)(2,1)S(1)} collective-permute-done((bf16[8,3,128,128]{3,2,1,0:T(8,128)(2,1)}, bf16[8,3,128,128]{3,2,1,0:T(8,128)(2,1)S(1)}, u32[]{:S(2)}, u32[]{:S(2)}) %collective-permute-start.16) | collective-permute-done | bytes 786464 | tf_op jit(solution)/shard_map/ppermute | solution.py:213
  91.0 17.9 %collective-permute-done.15 = bf16[8,3,128,128]{3,2,1,0:T(8,128)(2,1)S(1)} collective-permute-done((bf16[8,3,128,128]{3,2,1,0:T(8,128)(2,1)}, bf16[8,3,128,128]{3,2,1,0:T(8,128)(2,1)S(1)}, u32[]{:S(2)}, u32[]{:S(2)}) %collective-permute-start.15) | collective-permute-done | bytes 786464 | tf_op jit(solution)/shard_map/ppermute | solution.py:213
  108.9 1.4 collective-permute-done.14
  110.2 2.5 %fusion.2 = bf16[8,3,128,128]{3,2,1,0:T(8,128)(2,1)} fusion(bf16[8,3,128,128]{3,2,1,0:T(8,128)(2,1)S(1)} %collective-permute-done.16, bf16[8,3,128,128]{3,2,1,0:T(8,128)(2,1)S(1)} %collective-permute-done.15, bf16[8,3,128,128]{3,2,1,0:T(8,128)(2,1)S(1)} %collective-permute-done.14, bf16[4,8,3,128,128]{4,3,2,1,0:T(8,128)(2,1)} %get-tuple-element.16, ...), kind=kLoop, calls=%fused_computation.4 | loop fusion | flops 3145728 | bytes 3932164 | tf_op jit(solution)/shard_map/convert_element_type | solution.py:214
  112.8 8.5 %all-to-all-start.1 = ((bf16[8,3,128,128]{3,2,1,0:T(8,128)(2,1)}), bf16[8,3,128,128]{3,2,1,0:T(8,128)(2,1)S(1)}, u32[]{:S(2)}, u32[]{:S(2)}) async-start(bf16[8,3,128,128]{3,2,1,0:T(8,128)(2,1)} %fusion.2), calls=%async_computation.1 | async-start | bytes 1572864 | tf_op jit(solution)/shard_map/all_to_all | solution.py:218
  121.2 14.5 %shard_map.120 = (bf16[32,128,128]{2,1,0:T(8,128)(2,1)}, bf16[32,128,128]{2,1,0:T(8,128)(2,1)}) custom-call(s32[32]{0:T(128)} %bitcast.101, s32[32]{0:T(128)} %bitcast.103, s32[32]{0:T(128)} %bitcast.105, bf16[14,128,128]{2,1,0:T(8,128)(2,1)} %get-tuple-element.11.hid, bf16[14,128,128]{2,1,0:T(8,128)(2,1)} %get-tuple-element.12.gdel, ...), custom_call_target="tpu_custom_call" | custom-call | flops 402653184 | bytes 6619136 | tf_op jit(solution)/shard_map/pallas_call | solution.py:164
  135.7 2.1 %dynamic-slice_bitcast_fusion.16 = (bf16[4,128,128]{2,1,0:T(8,128)(2,1)S(1)}, bf16[4,128,128]{2,1,0:T(8,128)(2,1)S(1)}, bf16[4,128,128]{2,1,0:T(8,128)(2,1)S(1)}...) fusion(bf16[8,4,128,128]{3,2,1,0:T(8,128)(2,1)} %bitcast.95, ...), kind=kLoop, calls=%fused_computation.43 | loop fusion | bytes 1835036 | tf_op jit(solution)/shard_map/jit(dynamic_index_in_dim)/squeeze | solution.py:200
  137.8 1.5 collective-permute-start.5
  139.2 3.7 %collective-permute-start.3 = (bf16[4,128,128]{2,1,0:T(8,128)(2,1)S(1)}, bf16[4,128,128]{2,1,0:T(8,128)(2,1)S(1)}, u32[]{:S(2)}, u32[]{:S(2)}) collective-permute-start(bf16[4,128,128]{2,1,0:T(8,128)(2,1)S(1)} %get-tuple-element.45), channel_id=1, source_target_pairs={{0,4},{1,5},{2,6},{3,7},{4,0},{5,1},{6,2},{7,3},{8,12},{9,13},{10,... | collective-permute-start | bytes 393224 | tf_op jit(solution)/shard_map/ppermute | solution.py:202
  143.0 0.9 collective-permute-start.2
  143.8 0.8 dynamic-slice_bitcast_fusion.9
  144.6 0.0 collective-permute-done.6
  144.6 0.3 collective-permute-start.1
  144.9 3.1 %collective-permute-done.5 = bf16[4,128,128]{2,1,0:T(8,128)(2,1)S(1)} collective-permute-done((bf16[4,128,128]{2,1,0:T(8,128)(2,1)S(1)}, bf16[4,128,128]{2,1,0:T(8,128)(2,1)S(1)}, u32[]{:S(2)}, u32[]{:S(2)}) %collective-permute-start.5) | collective-permute-done | bytes 131104 | tf_op jit(solution)/shard_map/ppermute | solution.py:202
  148.0 5.2 %collective-permute-start.13 = (bf16[4,128,128]{2,1,0:T(8,128)(2,1)}, bf16[4,128,128]{2,1,0:T(8,128)(2,1)S(1)}, u32[]{:S(2)}, u32[]{:S(2)}) collective-permute-start(bf16[4,128,128]{2,1,0:T(8,128)(2,1)} %get-tuple-element.35), channel_id=1, source_target_pairs={{0,7},{1,0},{2,1},{3,2},{4,3},{5,4},{6,5},{7,6},{8,15},{9,8},{10,9... | collective-permute-start | bytes 393224 | tf_op jit(solution)/shard_map/ppermute | solution.py:202
  153.2 0.0 collective-permute-done.3
  153.2 3.1 %collective-permute-start.12 = (bf16[4,128,128]{2,1,0:T(8,128)(2,1)}, bf16[4,128,128]{2,1,0:T(8,128)(2,1)}, u32[]{:S(2)}, u32[]{:S(2)}) collective-permute-start(bf16[4,128,128]{2,1,0:T(8,128)(2,1)} %get-tuple-element.36), channel_id=1, source_target_pairs={{0,6},{1,7},{2,0},{3,1},{4,2},{5,3},{6,4},{7,5},{8,14},{9,15},{10,... | collective-permute-start | bytes 393224 | tf_op jit(solution)/shard_map/ppermute | solution.py:202
  156.3 0.0 collective-permute-done.2
  156.3 0.0 collective-permute-start.11
  156.3 0.0 collective-permute-done.1
  156.3 0.7 collective-permute-start.10
  157.0 1.2 collective-permute-start.9
  158.2 0.0 collective-permute-done.13
  158.2 1.1 collective-permute-start.8
  159.3 6.1 %collective-permute-done.12 = bf16[4,128,128]{2,1,0:T(8,128)(2,1)} collective-permute-done((bf16[4,128,128]{2,1,0:T(8,128)(2,1)}, bf16[4,128,128]{2,1,0:T(8,128)(2,1)}, u32[]{:S(2)}, u32[]{:S(2)}) %collective-permute-start.12) | collective-permute-done | bytes 131104 | tf_op jit(solution)/shard_map/ppermute | solution.py:202
  165.4 0.0 collective-permute-start.7
  165.4 1.8 %copy_bitcast_fusion.2 = bf16[128,512]{1,0:T(8,128)(2,1)} fusion(bf16[4,128,128]{2,1,0:T(8,128)(2,1)S(1)} %collective-permute-done.6, bf16[4,128,128]{2,1,0:T(8,128)(2,1)S(1)} %collective-permute-done.5, bf16[4,128,128]{2,1,0:T(8,128)(2,1)S(1)} %collective-permute-done.4, bf16[4,128,128]{2,1,0:T(8,128)(2,1)S(1)} %collective-permute-done.3, ...), kind=kLoop, calls=%fused_computation.29 | loop fusion | flops 1048576 | bytes 1179652 | tf_op jit(solution)/shard_map/reshape | solution.py:203
  167.2 1.7 collective-permute-done.8
  169.0 2.0 %collective-permute-done.7 = bf16[4,128,128]{2,1,0:T(8,128)(2,1)S(1)} collective-permute-done((bf16[4,128,128]{2,1,0:T(8,128)(2,1)S(1)}, bf16[4,128,128]{2,1,0:T(8,128)(2,1)S(1)}, u32[]{:S(2)}, u32[]{:S(2)}) %collective-permute-start.7) | collective-permute-done | bytes 131104 | tf_op jit(solution)/shard_map/ppermute | solution.py:202
  171.0 1.7 copy_bitcast_fusion.1
  172.7 0.1 convert_reduce_fusion
  172.8 0.7 slice_bitcast_fusion
  173.5 0.7 copy.25
  (12 shorter events, 0.0 us)
Async XLA Ops:
  3.6 31.5 %all-to-all-start = ((bf16[8,2,128,512]{2,3,1,0:T(8,128)(2,1)}), bf16[8,2,128,512]{2,3,1,0:T(8,128)(2,1)S(1)}, u32[]{:S(2)}, u32[]{:S(2)}) async-start(bf16[8,2,128,512]{2,3,1,0:T(8,128)(2,1)} %broadcast_in_dim.4), calls=%async_computation | async-start | bytes 4194304 | tf_op jit(solution)/shard_map/all_to_all | solution.py:186
  37.6 1.6 copy-start
  71.4 19.6 %collective-permute-start.16 = (bf16[8,3,128,128]{3,2,1,0:T(8,128)(2,1)}, bf16[8,3,128,128]{3,2,1,0:T(8,128)(2,1)S(1)}, u32[]{:S(2)}, u32[]{:S(2)}) collective-permute-start(bf16[8,3,128,128]{3,2,1,0:T(8,128)(2,1)} %get-tuple-element.28), channel_id=1, source_target_pairs={{0,24},{8,0},{16,8},{24,16},{1,25},{9,1},{17,9},{25,17},{2,26},{10... | collective-permute-start | bytes 2359304 | tf_op jit(solution)/shard_map/ppermute | solution.py:213
  72.8 36.1 %collective-permute-start.15 = (bf16[8,3,128,128]{3,2,1,0:T(8,128)(2,1)}, bf16[8,3,128,128]{3,2,1,0:T(8,128)(2,1)S(1)}, u32[]{:S(2)}, u32[]{:S(2)}) collective-permute-start(bf16[8,3,128,128]{3,2,1,0:T(8,128)(2,1)} %get-tuple-element.29), channel_id=1, source_target_pairs={{0,16},{8,24},{16,0},{24,8},{1,17},{9,25},{17,1},{25,9},{2,18},{10... | collective-permute-start | bytes 2359304 | tf_op jit(solution)/shard_map/ppermute | solution.py:213
  74.4 35.8 %collective-permute-start.14 = (bf16[8,3,128,128]{3,2,1,0:T(8,128)(2,1)S(1)}, bf16[8,3,128,128]{3,2,1,0:T(8,128)(2,1)S(1)}, u32[]{:S(2)}, u32[]{:S(2)}) collective-permute-start(bf16[8,3,128,128]{3,2,1,0:T(8,128)(2,1)S(1)} %get-tuple-element.27), channel_id=1, source_target_pairs={{0,8},{8,16},{16,24},{24,0},{1,9},{9,17},{17,25},{25,1},{2,10},{10... | collective-permute-start | bytes 2359304 | tf_op jit(solution)/shard_map/ppermute | solution.py:213
  112.8 60.0 %all-to-all-start.1 = ((bf16[8,3,128,128]{3,2,1,0:T(8,128)(2,1)}), bf16[8,3,128,128]{3,2,1,0:T(8,128)(2,1)S(1)}, u32[]{:S(2)}, u32[]{:S(2)}) async-start(bf16[8,3,128,128]{3,2,1,0:T(8,128)(2,1)} %fusion.2), calls=%async_computation.1 | async-start | bytes 1572864 | tf_op jit(solution)/shard_map/all_to_all | solution.py:218
  135.7 8.1 %copy-start.1 = (bf16[32,128,128]{2,1,0:T(8,128)(2,1)S(1)}, bf16[32,128,128]{2,1,0:T(8,128)(2,1)}, u32[]{:S(2)}) copy-start(bf16[32,128,128]{2,1,0:T(8,128)(2,1)} %get-tuple-element.15) | copy-start | bytes 3145732
  137.8 6.9 %collective-permute-start.6 = (bf16[4,128,128]{2,1,0:T(8,128)(2,1)S(1)}, bf16[4,128,128]{2,1,0:T(8,128)(2,1)S(1)}, u32[]{:S(2)}, u32[]{:S(2)}) collective-permute-start(bf16[4,128,128]{2,1,0:T(8,128)(2,1)S(1)} %get-tuple-element.42), channel_id=1, source_target_pairs={{0,7},{1,0},{2,1},{3,2},{4,3},{5,4},{6,5},{7,6},{8,15},{9,8},{10,9... | collective-permute-start | bytes 393224 | tf_op jit(solution)/shard_map/ppermute | solution.py:202
  137.8 10.3 %collective-permute-start.5 = (bf16[4,128,128]{2,1,0:T(8,128)(2,1)S(1)}, bf16[4,128,128]{2,1,0:T(8,128)(2,1)S(1)}, u32[]{:S(2)}, u32[]{:S(2)}) collective-permute-start(bf16[4,128,128]{2,1,0:T(8,128)(2,1)S(1)} %get-tuple-element.43), channel_id=1, source_target_pairs={{0,6},{1,7},{2,0},{3,1},{4,2},{5,3},{6,4},{7,5},{8,14},{9,15},{10,... | collective-permute-start | bytes 393224 | tf_op jit(solution)/shard_map/ppermute | solution.py:202
  139.2 8.8 %collective-permute-start.4 = (bf16[4,128,128]{2,1,0:T(8,128)(2,1)S(1)}, bf16[4,128,128]{2,1,0:T(8,128)(2,1)S(1)}, u32[]{:S(2)}, u32[]{:S(2)}) collective-permute-start(bf16[4,128,128]{2,1,0:T(8,128)(2,1)S(1)} %get-tuple-element.44), channel_id=1, source_target_pairs={{0,5},{1,6},{2,7},{3,0},{4,1},{5,2},{6,3},{7,4},{8,13},{9,14},{10,... | collective-permute-start | bytes 393224 | tf_op jit(solution)/shard_map/ppermute | solution.py:202
  139.2 14.0 %collective-permute-start.3 = (bf16[4,128,128]{2,1,0:T(8,128)(2,1)S(1)}, bf16[4,128,128]{2,1,0:T(8,128)(2,1)S(1)}, u32[]{:S(2)}, u32[]{:S(2)}) collective-permute-start(bf16[4,128,128]{2,1,0:T(8,128)(2,1)S(1)} %get-tuple-element.45), channel_id=1, source_target_pairs={{0,4},{1,5},{2,6},{3,7},{4,0},{5,1},{6,2},{7,3},{8,12},{9,13},{10,... | collective-permute-start | bytes 393224 | tf_op jit(solution)/shard_map/ppermute | solution.py:202
  143.0 13.4 %collective-permute-start.2 = (bf16[4,128,128]{2,1,0:T(8,128)(2,1)}, bf16[4,128,128]{2,1,0:T(8,128)(2,1)S(1)}, u32[]{:S(2)}, u32[]{:S(2)}) collective-permute-start(bf16[4,128,128]{2,1,0:T(8,128)(2,1)} %get-tuple-element.46), channel_id=1, source_target_pairs={{0,3},{1,4},{2,5},{3,6},{4,7},{5,0},{6,1},{7,2},{8,11},{9,12},{10,... | collective-permute-start | bytes 393224 | tf_op jit(solution)/shard_map/ppermute | solution.py:202
  144.6 11.7 %collective-permute-start.1 = (bf16[4,128,128]{2,1,0:T(8,128)(2,1)S(1)}, bf16[4,128,128]{2,1,0:T(8,128)(2,1)}, u32[]{:S(2)}, u32[]{:S(2)}) collective-permute-start(bf16[4,128,128]{2,1,0:T(8,128)(2,1)S(1)} %get-tuple-element.47), channel_id=1, source_target_pairs={{0,2},{1,3},{2,4},{3,5},{4,6},{5,7},{6,0},{7,1},{8,10},{9,11},{10,... | collective-permute-start | bytes 393224 | tf_op jit(solution)/shard_map/ppermute | solution.py:202
  148.0 9.0 %collective-permute-start = (bf16[4,128,128]{2,1,0:T(8,128)(2,1)S(1)}, bf16[4,128,128]{2,1,0:T(8,128)(2,1)}, u32[]{:S(2)}, u32[]{:S(2)}) collective-permute-start(bf16[4,128,128]{2,1,0:T(8,128)(2,1)S(1)} %get-tuple-element.41), channel_id=1, source_target_pairs={{0,1},{1,2},{2,3},{3,4},{4,5},{5,6},{6,7},{7,0},{8,9},{9,10},{10,1... | collective-permute-start | bytes 393224 | tf_op jit(solution)/shard_map/ppermute | solution.py:202
  148.0 10.1 %collective-permute-start.13 = (bf16[4,128,128]{2,1,0:T(8,128)(2,1)}, bf16[4,128,128]{2,1,0:T(8,128)(2,1)S(1)}, u32[]{:S(2)}, u32[]{:S(2)}) collective-permute-start(bf16[4,128,128]{2,1,0:T(8,128)(2,1)} %get-tuple-element.35), channel_id=1, source_target_pairs={{0,7},{1,0},{2,1},{3,2},{4,3},{5,4},{6,5},{7,6},{8,15},{9,8},{10,9... | collective-permute-start | bytes 393224 | tf_op jit(solution)/shard_map/ppermute | solution.py:202
  153.2 12.2 %collective-permute-start.12 = (bf16[4,128,128]{2,1,0:T(8,128)(2,1)}, bf16[4,128,128]{2,1,0:T(8,128)(2,1)}, u32[]{:S(2)}, u32[]{:S(2)}) collective-permute-start(bf16[4,128,128]{2,1,0:T(8,128)(2,1)} %get-tuple-element.36), channel_id=1, source_target_pairs={{0,6},{1,7},{2,0},{3,1},{4,2},{5,3},{6,4},{7,5},{8,14},{9,15},{10,... | collective-permute-start | bytes 393224 | tf_op jit(solution)/shard_map/ppermute | solution.py:202
  156.3 10.9 %collective-permute-start.11 = (bf16[4,128,128]{2,1,0:T(8,128)(2,1)S(1)}, bf16[4,128,128]{2,1,0:T(8,128)(2,1)S(1)}, u32[]{:S(2)}, u32[]{:S(2)}) collective-permute-start(bf16[4,128,128]{2,1,0:T(8,128)(2,1)S(1)} %get-tuple-element.37), channel_id=1, source_target_pairs={{0,5},{1,6},{2,7},{3,0},{4,1},{5,2},{6,3},{7,4},{8,13},{9,14},{10,... | collective-permute-start | bytes 393224 | tf_op jit(solution)/shard_map/ppermute | solution.py:202
  156.3 10.9 %collective-permute-start.10 = (bf16[4,128,128]{2,1,0:T(8,128)(2,1)S(1)}, bf16[4,128,128]{2,1,0:T(8,128)(2,1)S(1)}, u32[]{:S(2)}, u32[]{:S(2)}) collective-permute-start(bf16[4,128,128]{2,1,0:T(8,128)(2,1)S(1)} %get-tuple-element.38), channel_id=1, source_target_pairs={{0,4},{1,5},{2,6},{3,7},{4,0},{5,1},{6,2},{7,3},{8,12},{9,13},{10,... | collective-permute-start | bytes 393224 | tf_op jit(solution)/shard_map/ppermute | solution.py:202
  157.0 10.2 %collective-permute-start.9 = (bf16[4,128,128]{2,1,0:T(8,128)(2,1)S(1)}, bf16[4,128,128]{2,1,0:T(8,128)(2,1)S(1)}, u32[]{:S(2)}, u32[]{:S(2)}) collective-permute-start(bf16[4,128,128]{2,1,0:T(8,128)(2,1)S(1)} %get-tuple-element.39), channel_id=1, source_target_pairs={{0,3},{1,4},{2,5},{3,6},{4,7},{5,0},{6,1},{7,2},{8,11},{9,12},{10,... | collective-permute-start | bytes 393224 | tf_op jit(solution)/shard_map/ppermute | solution.py:202
  158.2 10.8 %collective-permute-start.8 = (bf16[4,128,128]{2,1,0:T(8,128)(2,1)S(1)}, bf16[4,128,128]{2,1,0:T(8,128)(2,1)S(1)}, u32[]{:S(2)}, u32[]{:S(2)}) collective-permute-start(bf16[4,128,128]{2,1,0:T(8,128)(2,1)S(1)} %get-tuple-element.40), channel_id=1, source_target_pairs={{0,2},{1,3},{2,4},{3,5},{4,6},{5,7},{6,0},{7,1},{8,10},{9,11},{10,... | collective-permute-start | bytes 393224 | tf_op jit(solution)/shard_map/ppermute | solution.py:202
  165.4 5.6 %collective-permute-start.7 = (bf16[4,128,128]{2,1,0:T(8,128)(2,1)S(1)}, bf16[4,128,128]{2,1,0:T(8,128)(2,1)S(1)}, u32[]{:S(2)}, u32[]{:S(2)}) collective-permute-start(bf16[4,128,128]{2,1,0:T(8,128)(2,1)S(1)} %get-tuple-element.34), channel_id=1, source_target_pairs={{0,1},{1,2},{2,3},{3,4},{4,5},{5,6},{6,7},{7,0},{8,9},{9,10},{10,1... | collective-permute-start | bytes 393224 | tf_op jit(solution)/shard_map/ppermute | solution.py:202
where the time goes:
time: 177 us; the launch traced here: 174 us
  waiting for transfers between devices  74.1 us (42%)
  Pallas kernels  40.6 us (23%)
  starting transfers between devices  35.3 us (20%)
  local copies, waits for them, and re-layouts  16.4 us (9%)
  other arithmetic  7.14 us (4%)
    ppermute x3, waiting for transfers between devices, reduce_inner(): total = total + lax.ppermute(outgoing, inner, pairs).astype(jnp.float32)  33.9 us
    all_to_all x1, waiting for transfers between devices, gather_blocks(): pieces = lax.all_to_all(spread_out, axis, 0, 0, tiled=True)  27.2 us
    pallas_call x1, Pallas kernels, front(): pl.pallas_call(_front_kernel, out_shape=(jax.ShapeDtypeStruct((inner, slo...  26.1 us
    ppermute x14, starting transfers between devices, scatter_blocks(): total = total + lax.ppermute(outgoing, axis, pairs).astype(jnp.float32)  17.6 us
    pallas_call x1, Pallas kernels, back(): pl.pallas_call(_back_kernel, out_shape=(jax.ShapeDtypeStruct(fshape, jnp....  14.5 us
    ppermute x14, waiting for transfers between devices, scatter_blocks(): total = total + lax.ppermute(outgoing, axis, pairs).astype(jnp.float32)  13 us
    all_to_all x1, starting transfers between devices, reduce_outer(): grid = lax.all_to_all(grid, outer, 0, 0, tiled=True)  8.47 us
    ppermute x3, starting transfers between devices, reduce_inner(): total = total + lax.ppermute(outgoing, inner, pairs).astype(jnp.float32)  4.93 us
  transfers between devices with their start and end apart: 19, of which 8 were waited for; matrix products, arithmetic and copies ran while one was open for 4% of the time, Pallas kernels for 8%

commit v1 on v0

--- a/solution.py
+++ b/solution.py
@@ -235,13 +235,16 @@
         gate_at, up_at, down_at, inputs, upstream, inputs_t, upstream_t, *weights, hidden_count,
         lax.axis_size("y"),
     )
-    partial = reduce_inner(stacked, "y")
+    half = stacked.shape[-2] // 2
+    partial = reduce_inner(stacked[..., :half, :], "y")
+    later = reduce_inner(stacked[..., half:, :], "y")
     mixed_part, input_part = back(
         gate_at, up_at, down_at, hidden, gate_delta, up_delta, *weights, feature_count
     )
     mixed = scatter_blocks(mixed_part, "tensor")
     grad_tokens = scatter_blocks(input_part, "tensor")
-    combined = reduce_outer(partial, "z")[None]
+    combined = reduce_outer(partial, "z")
+    combined = jnp.concatenate([combined, reduce_outer(later, "z")], axis=-2)[None]
     grad_gate = combined[None, :, 0]
     grad_up = combined[None, :, 1]
     grad_down = combined[None, :, 2].swapaxes(-1, -2)

time: 177 us -> 175 us (0.989)
  waiting for transfers between devices: 74.1 us -> 50.8 us
  starting transfers between devices: 35.3 us -> 51.6 us
  other arithmetic: 7.14 us -> 9.35 us
  local copies, waits for them, and re-layouts: 16.4 us -> 18.5 us
    ppermute x3 -> x6, waiting for transfers between devices: 33.9 us -> 12.6 us  [reduce_inner(): total = total + lax.ppermute(outgoing, inner, pairs).astype(jnp.float32)]
    all_to_all x1 -> x2, starting transfers between devices: 8.47 us -> 15.7 us  [reduce_outer(): grid = lax.all_to_all(grid, outer, 0, 0, tiled=True)]
    ppermute x14, starting transfers between devices: 17.6 us -> 23.1 us  [scatter_blocks(): total = total + lax.ppermute(outgoing, axis, pairs).astype(jnp.float32)]
    ppermute x3 -> x6, starting transfers between devices: 4.93 us -> 8.52 us  [reduce_inner(): total = total + lax.ppermute(outgoing, inner, pairs).astype(jnp.float32)]
    slice x0 -> x1, local copies, waits for them, and re-layouts: none -> 3.05 us  [layer(): partial = reduce_inner(stacked[..., :half, :], 'y')]
    convert_element_type x1 -> x2, other arithmetic: 2.52 us -> 4.48 us  [reduce_inner(): return total.astype(jnp.bfloat16)]
    ppermute x14, waiting for transfers between devices: 13 us -> 11.1 us  [scatter_blocks(): total = total + lax.ppermute(outgoing, axis, pairs).astype(jnp.float32)]
  transfers between devices with their start and end apart: 19 -> 23, of which waited for: 8 -> 8; matrix products, arithmetic and copies ran while one was open for 4% -> 7% of each run, Pallas kernels for 8% -> 8%
where the time goes in v1:
time: 175 us; the launch traced here: 172 us
  starting transfers between devices  51.6 us (29%)
  waiting for transfers between devices  50.8 us (29%)
  Pallas kernels  40.6 us (23%)
  local copies, waits for them, and re-layouts  18.5 us (11%)
  other arithmetic  9.35 us (5%)
    all_to_all x1, waiting for transfers between devices, gather_blocks(): pieces = lax.all_to_all(spread_out, axis, 0, 0, tiled=True)  27.2 us
    pallas_call x1, Pallas kernels, front(): pl.pallas_call(_front_kernel, out_shape=(jax.ShapeDtypeStruct((inner, slo...  26.1 us
    ppermute x14, starting transfers between devices, scatter_blocks(): total = total + lax.ppermute(outgoing, axis, pairs).astype(jnp.float32)  23.1 us
    all_to_all x2, starting transfers between devices, reduce_outer(): grid = lax.all_to_all(grid, outer, 0, 0, tiled=True)  15.7 us
    pallas_call x1, Pallas kernels, back(): pl.pallas_call(_back_kernel, out_shape=(jax.ShapeDtypeStruct(fshape, jnp....  14.5 us
    ppermute x6, waiting for transfers between devices, reduce_inner(): total = total + lax.ppermute(outgoing, inner, pairs).astype(jnp.float32)  12.6 us
    ppermute x14, waiting for transfers between devices, scatter_blocks(): total = total + lax.ppermute(outgoing, axis, pairs).astype(jnp.float32)  11.1 us
    ppermute x6, starting transfers between devices, reduce_inner(): total = total + lax.ppermute(outgoing, inner, pairs).astype(jnp.float32)  8.52 us
  transfers between devices with their start and end apart: 23, of which 8 were waited for; matrix products, arithmetic and copies ran while one was open for 7% of the time, Pallas kernels for 8%

profile of v1, /device:TPU:8, one launch (start us, length us, event | category | flops | bytes accessed | tf_op | source)
XLA Modules:
  0.0 171.7 jit_solution(12204826655836987111)
XLA Ops:
  0.6 1.0 pad_maximum_fusion
  1.6 0.2 copy.20
  1.8 1.8 %broadcast_in_dim.4 = bf16[8,2,128,512]{2,3,1,0:T(8,128)(2,1)} broadcast(bf16[2,128,512]{1,2,0:T(8,128)(2,1)S(1)} %copy.20), dimensions={1,2,3} | broadcast | bytes 2359296 | tf_op jit(solution)/shard_map/broadcast_in_dim | solution.py:185
  3.6 4.3 %all-to-all-start = ((bf16[8,2,128,512]{2,3,1,0:T(8,128)(2,1)}), bf16[8,2,128,512]{2,3,1,0:T(8,128)(2,1)S(1)}, u32[]{:S(2)}, u32[]{:S(2)}) async-start(bf16[8,2,128,512]{2,3,1,0:T(8,128)(2,1)} %broadcast_in_dim.4), calls=%async_computation | async-start | bytes 4194304 | tf_op jit(solution)/shard_map/all_to_all | solution.py:186
  7.9 27.2 %all-to-all-done = bf16[8,2,128,512]{2,3,1,0:T(8,128)(2,1)S(1)} async-done(((bf16[8,2,128,512]{2,3,1,0:T(8,128)(2,1)}), bf16[8,2,128,512]{2,3,1,0:T(8,128)(2,1)S(1)}, u32[]{:S(2)}, u32[]{:S(2)}) %all-to-all-start) | async-done | bytes 2097184 | tf_op jit(solution)/shard_map/all_to_all | solution.py:186
  35.0 2.6 %copy.21 = bf16[8,2,128,4,128]{4,2,3,0,1:T(8,128)(2,1)} copy(bf16[8,2,128,4,128]{2,4,3,1,0:T(8,128)(2,1)S(1)} %bitcast.89) | data formatting | bytes 4194304 | tf_op jit(solution)/shard_map/reshape | solution.py:188
  37.8 1.4 copy-done
  39.2 1.5 fusion.24
  40.7 1.5 fusion.23
  42.2 26.1 %shard_map.119 = (bf16[4,8,3,128,128]{4,3,2,1,0:T(8,128)(2,1)}, bf16[14,128,128]{2,1,0:T(8,128)(2,1)}, bf16[14,128,128]{2,1,0:T(8,128)(2,1)}, bf16[14,128,128]{2,1,0:T(8,128)(2,1)}) custom-call(s32[32]{0:T(128)} %bitcast.109, s32[32]{0:T(128)} %bitcast.111, s32[32]{0:T(128)} %bitcast.113, bf16[32,128,128]{2,1,0:T(8,128)(2,1)} %bitcast.100, ...), custom_call_target="tpu_custom_call" | custom-call | flops 805306368 | bytes 11862016 | tf_op jit(solution)/shard_map/pallas_call | solution.py:140
  68.3 3.1 %fusion.22 = (bf16[4,8,3,64,128]{4,3,2,1,0:T(8,128)(2,1)S(1)}, bf16[4,8,3,64,128]{4,3,2,1,0:T(8,128)(2,1)S(1)}) fusion(bf16[4,8,3,128,128]{4,3,2,1,0:T(8,128)(2,1)} %get-tuple-element.16), kind=kLoop, calls=%fused_computation.54 | loop fusion | bytes 6291456 | tf_op jit(solution)/shard_map/slice | solution.py:239
  71.4 1.0 dynamic-slice_bitcast_fusion.2
  72.4 1.4 collective-permute-start.19
  73.8 1.6 collective-permute-start.18
  75.4 1.9 %collective-permute-start.17 = (bf16[8,3,64,128]{3,2,1,0:T(8,128)(2,1)S(1)}, bf16[8,3,64,128]{3,2,1,0:T(8,128)(2,1)}, u32[]{:S(2)}, u32[]{:S(2)}) collective-permute-start(bf16[8,3,64,128]{3,2,1,0:T(8,128)(2,1)S(1)} %get-tuple-element.36), channel_id=1, source_target_pairs={{0,8},{8,16},{16,24},{24,0},{1,9},{9,17},{17,25},{25,1},{2,10},{10... | collective-permute-start | bytes 1179656 | tf_op jit(solution)/shard_map/ppermute | solution.py:213
  77.3 1.0 dynamic-slice_bitcast_fusion.5
  78.5 1.9 %collective-permute-start.15 = (bf16[8,3,64,128]{3,2,1,0:T(8,128)(2,1)}, bf16[8,3,64,128]{3,2,1,0:T(8,128)(2,1)}, u32[]{:S(2)}, u32[]{:S(2)}) collective-permute-start(bf16[8,3,64,128]{3,2,1,0:T(8,128)(2,1)} %get-tuple-element.35), channel_id=1, source_target_pairs={{0,16},{8,24},{16,0},{24,8},{1,17},{9,25},{17,1},{25,9},{2,18},{10... | collective-permute-start | bytes 1179656 | tf_op jit(solution)/shard_map/ppermute | solution.py:213
  80.4 3.3 %collective-permute-done.19 = bf16[8,3,64,128]{3,2,1,0:T(8,128)(2,1)} collective-permute-done((bf16[8,3,64,128]{3,2,1,0:T(8,128)(2,1)}, bf16[8,3,64,128]{3,2,1,0:T(8,128)(2,1)}, u32[]{:S(2)}, u32[]{:S(2)}) %collective-permute-start.19) | collective-permute-done | bytes 393248 | tf_op jit(solution)/shard_map/ppermute | solution.py:213
  83.7 1.6 collective-permute-start.14
  85.3 8.0 %collective-permute-done.18 = bf16[8,3,64,128]{3,2,1,0:T(8,128)(2,1)} collective-permute-done((bf16[8,3,64,128]{3,2,1,0:T(8,128)(2,1)}, bf16[8,3,64,128]{3,2,1,0:T(8,128)(2,1)}, u32[]{:S(2)}, u32[]{:S(2)}) %collective-permute-start.18) | collective-permute-done | bytes 393248 | tf_op jit(solution)/shard_map/ppermute | solution.py:213
  93.2 1.3 collective-permute-done.17
  94.5 2.2 %fusion.2 = bf16[8,3,64,128]{3,2,1,0:T(8,128)(2,1)} fusion(bf16[8,3,64,128]{3,2,1,0:T(8,128)(2,1)} %collective-permute-done.19, bf16[8,3,64,128]{3,2,1,0:T(8,128)(2,1)} %collective-permute-done.18, bf16[8,3,64,128]{3,2,1,0:T(8,128)(2,1)} %collective-permute-done.17, bf16[4,8,3,64,128]{4,3,2,1,0:T(8,128)(2,1)S(1)} %get-tuple-element.28, s32[]{:T(128)S(6)} %select_n.128), kind=kLoop, calls=%fused_computation.4 | loop fusion | flops 1572864 | bytes 1966084 | tf_op jit(solution)/shard_map/convert_element_type | solution.py:214
  96.7 8.5 %all-to-all-start.2 = ((bf16[8,3,64,128]{3,2,1,0:T(8,128)(2,1)}), bf16[8,3,64,128]{3,2,1,0:T(8,128)(2,1)S(1)}, u32[]{:S(2)}, u32[]{:S(2)}) async-start(bf16[8,3,64,128]{3,2,1,0:T(8,128)(2,1)} %fusion.2), calls=%async_computation.2 | async-start | bytes 786432 | tf_op jit(solution)/shard_map/all_to_all | solution.py:218
  105.2 14.5 %shard_map.120 = (bf16[32,128,128]{2,1,0:T(8,128)(2,1)}, bf16[32,128,128]{2,1,0:T(8,128)(2,1)}) custom-call(s32[32]{0:T(128)} %bitcast.110, s32[32]{0:T(128)} %bitcast.112, s32[32]{0:T(128)} %bitcast.114, bf16[14,128,128]{2,1,0:T(8,128)(2,1)} %get-tuple-element.11.hid, bf16[14,128,128]{2,1,0:T(8,128)(2,1)} %get-tuple-element.12.gdel, ...), custom_call_target="tpu_custom_call" | custom-call | flops 402653184 | bytes 6619136 | tf_op jit(solution)/shard_map/pallas_call | solution.py:164
  119.7 2.1 %dynamic-slice_bitcast_fusion.19 = (bf16[4,128,128]{2,1,0:T(8,128)(2,1)}, bf16[4,128,128]{2,1,0:T(8,128)(2,1)S(1)}, bf16[4,128,128]{2,1,0:T(8,128)(2,1)S(1)}, bf...) fusion(bf16[8,4,128,128]{3,2,1,0:T(8,128)(2,1)} %bitcast.105, ...), kind=kLoop, calls=%fused_computation.52 | loop fusion | bytes 1835036 | tf_op jit(solution)/shard_map/jit(dynamic_index_in_dim)/squeeze | solution.py:200
  121.8 1.6 collective-permute-start.6
  123.4 3.5 %collective-permute-start.5 = (bf16[4,128,128]{2,1,0:T(8,128)(2,1)S(1)}, bf16[4,128,128]{2,1,0:T(8,128)(2,1)S(1)}, u32[]{:S(2)}, u32[]{:S(2)}) collective-permute-start(bf16[4,128,128]{2,1,0:T(8,128)(2,1)S(1)} %get-tuple-element.48), channel_id=1, source_target_pairs={{0,6},{1,7},{2,0},{3,1},{4,2},{5,3},{6,4},{7,5},{8,14},{9,15},{10,... | collective-permute-start | bytes 393224 | tf_op jit(solution)/shard_map/ppermute | solution.py:202
  126.9 5.6 %collective-permute-start.4 = (bf16[4,128,128]{2,1,0:T(8,128)(2,1)S(1)}, bf16[4,128,128]{2,1,0:T(8,128)(2,1)}, u32[]{:S(2)}, u32[]{:S(2)}) collective-permute-start(bf16[4,128,128]{2,1,0:T(8,128)(2,1)S(1)} %get-tuple-element.49), channel_id=1, source_target_pairs={{0,5},{1,6},{2,7},{3,0},{4,1},{5,2},{6,3},{7,4},{8,13},{9,14},{10,... | collective-permute-start | bytes 393224 | tf_op jit(solution)/shard_map/ppermute | solution.py:202
  132.6 2.8 %collective-permute-start.3 = (bf16[4,128,128]{2,1,0:T(8,128)(2,1)S(1)}, bf16[4,128,128]{2,1,0:T(8,128)(2,1)S(1)}, u32[]{:S(2)}, u32[]{:S(2)}) collective-permute-start(bf16[4,128,128]{2,1,0:T(8,128)(2,1)S(1)} %get-tuple-element.50), channel_id=1, source_target_pairs={{0,4},{1,5},{2,6},{3,7},{4,0},{5,1},{6,2},{7,3},{8,12},{9,13},{10,... | collective-permute-start | bytes 393224 | tf_op jit(solution)/shard_map/ppermute | solution.py:202
  135.4 0.8 dynamic-slice_bitcast_fusion.12
  136.2 0.3 collective-permute-start.2
  136.6 2.5 %collective-permute-done.3 = bf16[4,128,128]{2,1,0:T(8,128)(2,1)S(1)} collective-permute-done((bf16[4,128,128]{2,1,0:T(8,128)(2,1)S(1)}, bf16[4,128,128]{2,1,0:T(8,128)(2,1)S(1)}, u32[]{:S(2)}, u32[]{:S(2)}) %collective-permute-start.3) | collective-permute-done | bytes 131104 | tf_op jit(solution)/shard_map/ppermute | solution.py:202
  139.1 0.7 collective-permute-start.1
  139.8 3.0 %collective-permute-start.13 = (bf16[4,128,128]{2,1,0:T(8,128)(2,1)}, bf16[4,128,128]{2,1,0:T(8,128)(2,1)}, u32[]{:S(2)}, u32[]{:S(2)}) collective-permute-start(bf16[4,128,128]{2,1,0:T(8,128)(2,1)} %get-tuple-element.40), channel_id=1, source_target_pairs={{0,7},{1,0},{2,1},{3,2},{4,3},{5,4},{6,5},{7,6},{8,15},{9,8},{10,9... | collective-permute-start | bytes 393224 | tf_op jit(solution)/shard_map/ppermute | solution.py:202
  142.7 1.3 collective-permute-start.12
  144.1 2.2 %fusion.5 = bf16[8,3,64,128]{3,2,1,0:T(8,128)(2,1)} fusion(bf16[8,3,64,128]{3,2,1,0:T(8,128)(2,1)} %collective-permute-done.16, bf16[8,3,64,128]{3,2,1,0:T(8,128)(2,1)} %collective-permute-done.15, bf16[8,3,64,128]{3,2,1,0:T(8,128)(2,1)} %collective-permute-done.14, bf16[4,8,3,64,128]{4,3,2,1,0:T(8,128)(2,1)S(1)} %get-tuple-element.27, s32[]{:T(128)S(6)} %select_n.128), kind=kLoop, calls=%fused_computation.8 | loop fusion | flops 1572864 | bytes 1966084 | tf_op jit(solution)/shard_map/convert_element_type | solution.py:214
  146.3 7.2 %all-to-all-start.1 = ((bf16[8,3,64,128]{3,2,1,0:T(8,128)(2,1)}), bf16[8,3,64,128]{3,2,1,0:T(8,128)(2,1)S(1)}, u32[]{:S(2)}, u32[]{:S(2)}) async-start(bf16[8,3,64,128]{3,2,1,0:T(8,128)(2,1)} %fusion.5), calls=%async_computation.1 | async-start | bytes 786432 | tf_op jit(solution)/shard_map/all_to_all | solution.py:218
  153.6 1.9 %collective-permute-start.10 = (bf16[4,128,128]{2,1,0:T(8,128)(2,1)}, bf16[4,128,128]{2,1,0:T(8,128)(2,1)S(1)}, u32[]{:S(2)}, u32[]{:S(2)}) collective-permute-start(bf16[4,128,128]{2,1,0:T(8,128)(2,1)} %get-tuple-element.43), channel_id=1, source_target_pairs={{0,4},{1,5},{2,6},{3,7},{4,0},{5,1},{6,2},{7,3},{8,12},{9,13},{10,... | collective-permute-start | bytes 393224 | tf_op jit(solution)/shard_map/ppermute | solution.py:202
  155.5 0.8 collective-permute-start.9
  156.2 0.6 collective-permute-start.8
  156.9 0.9 collective-permute-start.7
  157.8 2.0 %copy_bitcast_fusion.2 = bf16[128,512]{1,0:T(8,128)(2,1)} fusion(bf16[4,128,128]{2,1,0:T(8,128)(2,1)S(1)} %collective-permute-done.6, bf16[4,128,128]{2,1,0:T(8,128)(2,1)S(1)} %collective-permute-done.5, bf16[4,128,128]{2,1,0:T(8,128)(2,1)} %collective-permute-done.4, bf16[4,128,128]{2,1,0:T(8,128)(2,1)} %copy-done.2, ...), kind=kLoop, calls=%fused_computation.38 | loop fusion | flops 1048576 | bytes 1179652 | tf_op jit(solution)/shard_map/reshape | solution.py:203
  159.8 2.1 %collective-permute-done.10 = bf16[4,128,128]{2,1,0:T(8,128)(2,1)S(1)} collective-permute-done((bf16[4,128,128]{2,1,0:T(8,128)(2,1)}, bf16[4,128,128]{2,1,0:T(8,128)(2,1)S(1)}, u32[]{:S(2)}, u32[]{:S(2)}) %collective-permute-start.10) | collective-permute-done | bytes 131104 | tf_op jit(solution)/shard_map/ppermute | solution.py:202
  161.9 1.8 %collective-permute-done.9 = bf16[4,128,128]{2,1,0:T(8,128)(2,1)S(1)} collective-permute-done((bf16[4,128,128]{2,1,0:T(8,128)(2,1)}, bf16[4,128,128]{2,1,0:T(8,128)(2,1)S(1)}, u32[]{:S(2)}, u32[]{:S(2)}) %collective-permute-start.9) | collective-permute-done | bytes 131104 | tf_op jit(solution)/shard_map/ppermute | solution.py:202
  163.7 4.6 %collective-permute-done.8 = bf16[4,128,128]{2,1,0:T(8,128)(2,1)S(1)} collective-permute-done((bf16[4,128,128]{2,1,0:T(8,128)(2,1)S(1)}, bf16[4,128,128]{2,1,0:T(8,128)(2,1)S(1)}, u32[]{:S(2)}, u32[]{:S(2)}) %collective-permute-start.8) | collective-permute-done | bytes 131104 | tf_op jit(solution)/shard_map/ppermute | solution.py:202
  168.4 1.8 %copy_bitcast_fusion.1 = bf16[128,512]{1,0:T(8,128)(2,1)} fusion(bf16[4,128,128]{2,1,0:T(8,128)(2,1)} %collective-permute-done.13, bf16[4,128,128]{2,1,0:T(8,128)(2,1)} %collective-permute-done.12, bf16[4,128,128]{2,1,0:T(8,128)(2,1)S(1)} %collective-permute-done.11, bf16[4,128,128]{2,1,0:T(8,128)(2,1)S(1)} %collective-permute-done.10, ...), kind=kLoop, calls=%fused_computation.37 | loop fusion | flops 1048576 | bytes 1179652 | tf_op jit(solution)/shard_map/reshape | solution.py:203
  170.3 0.7 slice_bitcast_fusion
  170.9 0.7 copy.25
  (27 shorter events, 0.6 us)
Async XLA Ops:
  3.6 31.5 %all-to-all-start = ((bf16[8,2,128,512]{2,3,1,0:T(8,128)(2,1)}), bf16[8,2,128,512]{2,3,1,0:T(8,128)(2,1)S(1)}, u32[]{:S(2)}, u32[]{:S(2)}) async-start(bf16[8,2,128,512]{2,3,1,0:T(8,128)(2,1)} %broadcast_in_dim.4), calls=%async_computation | async-start | bytes 4194304 | tf_op jit(solution)/shard_map/all_to_all | solution.py:186
  37.6 1.6 copy-start
  72.4 11.3 %collective-permute-start.19 = (bf16[8,3,64,128]{3,2,1,0:T(8,128)(2,1)}, bf16[8,3,64,128]{3,2,1,0:T(8,128)(2,1)}, u32[]{:S(2)}, u32[]{:S(2)}) collective-permute-start(bf16[8,3,64,128]{3,2,1,0:T(8,128)(2,1)} %get-tuple-element.37), channel_id=1, source_target_pairs={{0,24},{8,0},{16,8},{24,16},{1,25},{9,1},{17,9},{25,17},{2,26},{10... | collective-permute-start | bytes 1179656 | tf_op jit(solution)/shard_map/ppermute | solution.py:213
  73.8 19.4 %collective-permute-start.18 = (bf16[8,3,64,128]{3,2,1,0:T(8,128)(2,1)}, bf16[8,3,64,128]{3,2,1,0:T(8,128)(2,1)}, u32[]{:S(2)}, u32[]{:S(2)}) collective-permute-start(bf16[8,3,64,128]{3,2,1,0:T(8,128)(2,1)} %get-tuple-element.38), channel_id=1, source_target_pairs={{0,16},{8,24},{16,0},{24,8},{1,17},{9,25},{17,1},{25,9},{2,18},{10... | collective-permute-start | bytes 1179656 | tf_op jit(solution)/shard_map/ppermute | solution.py:213
  75.4 19.1 %collective-permute-start.17 = (bf16[8,3,64,128]{3,2,1,0:T(8,128)(2,1)S(1)}, bf16[8,3,64,128]{3,2,1,0:T(8,128)(2,1)}, u32[]{:S(2)}, u32[]{:S(2)}) collective-permute-start(bf16[8,3,64,128]{3,2,1,0:T(8,128)(2,1)S(1)} %get-tuple-element.36), channel_id=1, source_target_pairs={{0,8},{8,16},{16,24},{24,0},{1,9},{9,17},{17,25},{25,1},{2,10},{10... | collective-permute-start | bytes 1179656 | tf_op jit(solution)/shard_map/ppermute | solution.py:213
  78.3 61.4 %collective-permute-start.16 = (bf16[8,3,64,128]{3,2,1,0:T(8,128)(2,1)}, bf16[8,3,64,128]{3,2,1,0:T(8,128)(2,1)}, u32[]{:S(2)}, u32[]{:S(2)}) collective-permute-start(bf16[8,3,64,128]{3,2,1,0:T(8,128)(2,1)} %get-tuple-element.34), channel_id=1, source_target_pairs={{0,24},{8,0},{16,8},{24,16},{1,25},{9,1},{17,9},{25,17},{2,26},{10... | collective-permute-start | bytes 1179656 | tf_op jit(solution)/shard_map/ppermute | solution.py:213
  78.5 61.3 %collective-permute-start.15 = (bf16[8,3,64,128]{3,2,1,0:T(8,128)(2,1)}, bf16[8,3,64,128]{3,2,1,0:T(8,128)(2,1)}, u32[]{:S(2)}, u32[]{:S(2)}) collective-permute-start(bf16[8,3,64,128]{3,2,1,0:T(8,128)(2,1)} %get-tuple-element.35), channel_id=1, source_target_pairs={{0,16},{8,24},{16,0},{24,8},{1,17},{9,25},{17,1},{25,9},{2,18},{10... | collective-permute-start | bytes 1179656 | tf_op jit(solution)/shard_map/ppermute | solution.py:213
  83.7 59.1 %collective-permute-start.14 = (bf16[8,3,64,128]{3,2,1,0:T(8,128)(2,1)}, bf16[8,3,64,128]{3,2,1,0:T(8,128)(2,1)}, u32[]{:S(2)}, u32[]{:S(2)}) collective-permute-start(bf16[8,3,64,128]{3,2,1,0:T(8,128)(2,1)} %get-tuple-element.33), channel_id=1, source_target_pairs={{0,8},{8,16},{16,24},{24,0},{1,9},{9,17},{17,25},{25,1},{2,10},{10... | collective-permute-start | bytes 1179656 | tf_op jit(solution)/shard_map/ppermute | solution.py:213
  96.7 49.6 %all-to-all-start.2 = ((bf16[8,3,64,128]{3,2,1,0:T(8,128)(2,1)}), bf16[8,3,64,128]{3,2,1,0:T(8,128)(2,1)S(1)}, u32[]{:S(2)}, u32[]{:S(2)}) async-start(bf16[8,3,64,128]{3,2,1,0:T(8,128)(2,1)} %fusion.2), calls=%async_computation.2 | async-start | bytes 786432 | tf_op jit(solution)/shard_map/all_to_all | solution.py:218
  119.7 15.7 %copy-start.1 = (bf16[32,128,128]{2,1,0:T(8,128)(2,1)S(1)}, bf16[32,128,128]{2,1,0:T(8,128)(2,1)}, u32[]{:S(2)}) copy-start(bf16[32,128,128]{2,1,0:T(8,128)(2,1)} %get-tuple-element.15) | copy-start | bytes 3145732
  121.8 5.1 %collective-permute-start.6 = (bf16[4,128,128]{2,1,0:T(8,128)(2,1)S(1)}, bf16[4,128,128]{2,1,0:T(8,128)(2,1)S(1)}, u32[]{:S(2)}, u32[]{:S(2)}) collective-permute-start(bf16[4,128,128]{2,1,0:T(8,128)(2,1)S(1)} %get-tuple-element.47), channel_id=1, source_target_pairs={{0,7},{1,0},{2,1},{3,2},{4,3},{5,4},{6,5},{7,6},{8,15},{9,8},{10,9... | collective-permute-start | bytes 393224 | tf_op jit(solution)/shard_map/ppermute | solution.py:202
  123.4 9.2 %collective-permute-start.5 = (bf16[4,128,128]{2,1,0:T(8,128)(2,1)S(1)}, bf16[4,128,128]{2,1,0:T(8,128)(2,1)S(1)}, u32[]{:S(2)}, u32[]{:S(2)}) collective-permute-start(bf16[4,128,128]{2,1,0:T(8,128)(2,1)S(1)} %get-tuple-element.48), channel_id=1, source_target_pairs={{0,6},{1,7},{2,0},{3,1},{4,2},{5,3},{6,4},{7,5},{8,14},{9,15},{10,... | collective-permute-start | bytes 393224 | tf_op jit(solution)/shard_map/ppermute | solution.py:202
  126.9 9.3 %collective-permute-start.4 = (bf16[4,128,128]{2,1,0:T(8,128)(2,1)S(1)}, bf16[4,128,128]{2,1,0:T(8,128)(2,1)}, u32[]{:S(2)}, u32[]{:S(2)}) collective-permute-start(bf16[4,128,128]{2,1,0:T(8,128)(2,1)S(1)} %get-tuple-element.49), channel_id=1, source_target_pairs={{0,5},{1,6},{2,7},{3,0},{4,1},{5,2},{6,3},{7,4},{8,13},{9,14},{10,... | collective-permute-start | bytes 393224 | tf_op jit(solution)/shard_map/ppermute | solution.py:202
  132.6 6.5 %collective-permute-start.3 = (bf16[4,128,128]{2,1,0:T(8,128)(2,1)S(1)}, bf16[4,128,128]{2,1,0:T(8,128)(2,1)S(1)}, u32[]{:S(2)}, u32[]{:S(2)}) collective-permute-start(bf16[4,128,128]{2,1,0:T(8,128)(2,1)S(1)} %get-tuple-element.50), channel_id=1, source_target_pairs={{0,4},{1,5},{2,6},{3,7},{4,0},{5,1},{6,2},{7,3},{8,12},{9,13},{10,... | collective-permute-start | bytes 393224 | tf_op jit(solution)/shard_map/ppermute | solution.py:202
  136.2 17.3 %collective-permute-start.2 = (bf16[4,128,128]{2,1,0:T(8,128)(2,1)}, bf16[4,128,128]{2,1,0:T(8,128)(2,1)}, u32[]{:S(2)}, u32[]{:S(2)}) collective-permute-start(bf16[4,128,128]{2,1,0:T(8,128)(2,1)} %get-tuple-element.51), channel_id=1, source_target_pairs={{0,3},{1,4},{2,5},{3,6},{4,7},{5,0},{6,1},{7,2},{8,11},{9,12},{10,... | collective-permute-start | bytes 393224 | tf_op jit(solution)/shard_map/ppermute | solution.py:202
  139.0 5.0 %copy-start.2 = (bf16[4,128,128]{2,1,0:T(8,128)(2,1)}, bf16[4,128,128]{2,1,0:T(8,128)(2,1)S(1)}, u32[]{:S(2)}) copy-start(bf16[4,128,128]{2,1,0:T(8,128)(2,1)S(1)} %collective-permute-done.3) | copy-start | bytes 393220
  139.1 14.5 %collective-permute-start.1 = (bf16[4,128,128]{2,1,0:T(8,128)(2,1)}, bf16[4,128,128]{2,1,0:T(8,128)(2,1)}, u32[]{:S(2)}, u32[]{:S(2)}) collective-permute-start(bf16[4,128,128]{2,1,0:T(8,128)(2,1)} %get-tuple-element.52), channel_id=1, source_target_pairs={{0,2},{1,3},{2,4},{3,5},{4,6},{5,7},{6,0},{7,1},{8,10},{9,11},{10,... | collective-permute-start | bytes 393224 | tf_op jit(solution)/shard_map/ppermute | solution.py:202
  139.8 15.7 %collective-permute-start = (bf16[4,128,128]{2,1,0:T(8,128)(2,1)}, bf16[4,128,128]{2,1,0:T(8,128)(2,1)}, u32[]{:S(2)}, u32[]{:S(2)}) collective-permute-start(bf16[4,128,128]{2,1,0:T(8,128)(2,1)} %get-tuple-element.46), channel_id=1, source_target_pairs={{0,1},{1,2},{2,3},{3,4},{4,5},{5,6},{6,7},{7,0},{8,9},{9,10},{10,1... | collective-permute-start | bytes 393224 | tf_op jit(solution)/shard_map/ppermute | solution.py:202
  139.8 16.5 %collective-permute-start.13 = (bf16[4,128,128]{2,1,0:T(8,128)(2,1)}, bf16[4,128,128]{2,1,0:T(8,128)(2,1)}, u32[]{:S(2)}, u32[]{:S(2)}) collective-permute-start(bf16[4,128,128]{2,1,0:T(8,128)(2,1)} %get-tuple-element.40), channel_id=1, source_target_pairs={{0,7},{1,0},{2,1},{3,2},{4,3},{5,4},{6,5},{7,6},{8,15},{9,8},{10,9... | collective-permute-start | bytes 393224 | tf_op jit(solution)/shard_map/ppermute | solution.py:202
  142.7 14.1 %collective-permute-start.12 = (bf16[4,128,128]{2,1,0:T(8,128)(2,1)}, bf16[4,128,128]{2,1,0:T(8,128)(2,1)}, u32[]{:S(2)}, u32[]{:S(2)}) collective-permute-start(bf16[4,128,128]{2,1,0:T(8,128)(2,1)} %get-tuple-element.41), channel_id=1, source_target_pairs={{0,6},{1,7},{2,0},{3,1},{4,2},{5,3},{6,4},{7,5},{8,14},{9,15},{10,... | collective-permute-start | bytes 393224 | tf_op jit(solution)/shard_map/ppermute | solution.py:202
  146.3 23.9 %all-to-all-start.1 = ((bf16[8,3,64,128]{3,2,1,0:T(8,128)(2,1)}), bf16[8,3,64,128]{3,2,1,0:T(8,128)(2,1)S(1)}, u32[]{:S(2)}, u32[]{:S(2)}) async-start(bf16[8,3,64,128]{3,2,1,0:T(8,128)(2,1)} %fusion.5), calls=%async_computation.1 | async-start | bytes 786432 | tf_op jit(solution)/shard_map/all_to_all | solution.py:218
  153.5 6.3 %collective-permute-start.11 = (bf16[4,128,128]{2,1,0:T(8,128)(2,1)}, bf16[4,128,128]{2,1,0:T(8,128)(2,1)S(1)}, u32[]{:S(2)}, u32[]{:S(2)}) collective-permute-start(bf16[4,128,128]{2,1,0:T(8,128)(2,1)} %get-tuple-element.42), channel_id=1, source_target_pairs={{0,5},{1,6},{2,7},{3,0},{4,1},{5,2},{6,3},{7,4},{8,13},{9,14},{10,... | collective-permute-start | bytes 393224 | tf_op jit(solution)/shard_map/ppermute | solution.py:202
  153.6 8.3 %collective-permute-start.10 = (bf16[4,128,128]{2,1,0:T(8,128)(2,1)}, bf16[4,128,128]{2,1,0:T(8,128)(2,1)S(1)}, u32[]{:S(2)}, u32[]{:S(2)}) collective-permute-start(bf16[4,128,128]{2,1,0:T(8,128)(2,1)} %get-tuple-element.43), channel_id=1, source_target_pairs={{0,4},{1,5},{2,6},{3,7},{4,0},{5,1},{6,2},{7,3},{8,12},{9,13},{10,... | collective-permute-start | bytes 393224 | tf_op jit(solution)/shard_map/ppermute | solution.py:202
  155.5 8.2 %collective-permute-start.9 = (bf16[4,128,128]{2,1,0:T(8,128)(2,1)}, bf16[4,128,128]{2,1,0:T(8,128)(2,1)S(1)}, u32[]{:S(2)}, u32[]{:S(2)}) collective-permute-start(bf16[4,128,128]{2,1,0:T(8,128)(2,1)} %get-tuple-element.44), channel_id=1, source_target_pairs={{0,3},{1,4},{2,5},{3,6},{4,7},{5,0},{6,1},{7,2},{8,11},{9,12},{10,... | collective-permute-start | bytes 393224 | tf_op jit(solution)/shard_map/ppermute | solution.py:202
  156.2 12.1 %collective-permute-start.8 = (bf16[4,128,128]{2,1,0:T(8,128)(2,1)S(1)}, bf16[4,128,128]{2,1,0:T(8,128)(2,1)S(1)}, u32[]{:S(2)}, u32[]{:S(2)}) collective-permute-start(bf16[4,128,128]{2,1,0:T(8,128)(2,1)S(1)} %get-tuple-element.45), channel_id=1, source_target_pairs={{0,2},{1,3},{2,4},{3,5},{4,6},{5,7},{6,0},{7,1},{8,10},{9,11},{10,... | collective-permute-start | bytes 393224 | tf_op jit(solution)/shard_map/ppermute | solution.py:202
  156.9 11.5 %collective-permute-start.7 = (bf16[4,128,128]{2,1,0:T(8,128)(2,1)S(1)}, bf16[4,128,128]{2,1,0:T(8,128)(2,1)S(1)}, u32[]{:S(2)}, u32[]{:S(2)}) collective-permute-start(bf16[4,128,128]{2,1,0:T(8,128)(2,1)S(1)} %get-tuple-element.39), channel_id=1, source_target_pairs={{0,1},{1,2},{2,3},{3,4},{4,5},{5,6},{6,7},{7,0},{8,9},{9,10},{10,1... | collective-permute-start | bytes 393224 | tf_op jit(solution)/shard_map/ppermute | solution.py:202

commit v2 on v0

--- a/solution.py
+++ b/solution.py
@@ -15,9 +15,10 @@
     return lax.dot_general(a, b, dims, preferred_element_type=jnp.float32)
 
 
-def _front_kernel(gate_at, up_at, down_at, xb, dyb, xt, dyt, wg, wu, wd,
+def _front_kernel(turn, gate_at, up_at, down_at, xb, dyb, xt, dyt, wg, wu, wd,
                   terms, hid, gdel, udel, gpre, upre, hgrad):
     inner = terms.shape[0]
+    own = turn[0]
     feature_count = xb.shape[0]
     slots = wg.shape[0]
     gpre[...] = jnp.zeros(gpre.shape, jnp.float32)
@@ -63,38 +64,38 @@
         @pl.when(bg >= 0)
         def _():
             r, c = bg % feature_count, bg // feature_count
-            terms[s % inner, s // inner, 0] = _dot(xt[r], gdel[c]).astype(terms.dtype)
+            terms[(s % inner + inner - own) % inner, s // inner, 0] = _dot(xt[r], gdel[c]).astype(terms.dtype)
 
         @pl.when(bg < 0)
         def _():
-            terms[s % inner, s // inner, 0] = jnp.zeros(terms.shape[3:], terms.dtype)
+            terms[(s % inner + inner - own) % inner, s // inner, 0] = jnp.zeros(terms.shape[3:], terms.dtype)
 
         bu = up_at[s]
 
         @pl.when(bu >= 0)
         def _():
             r, c = bu % feature_count, bu // feature_count
-            terms[s % inner, s // inner, 1] = _dot(xt[r], udel[c]).astype(terms.dtype)
+            terms[(s % inner + inner - own) % inner, s // inner, 1] = _dot(xt[r], udel[c]).astype(terms.dtype)
 
         @pl.when(bu < 0)
         def _():
-            terms[s % inner, s // inner, 1] = jnp.zeros(terms.shape[3:], terms.dtype)
+            terms[(s % inner + inner - own) % inner, s // inner, 1] = jnp.zeros(terms.shape[3:], terms.dtype)
 
         bd = down_at[s]
 
         @pl.when(bd >= 0)
         def _():
             r, c = bd % feature_count, bd // feature_count
-            terms[s % inner, s // inner, 2] = _dot(dyt[r], hid[c]).astype(terms.dtype)
+            terms[(s % inner + inner - own) % inner, s // inner, 2] = _dot(dyt[r], hid[c]).astype(terms.dtype)
 
         @pl.when(bd < 0)
         def _():
-            terms[s % inner, s // inner, 2] = jnp.zeros(terms.shape[3:], terms.dtype)
-
-
-def _back_kernel(gate_at, up_at, down_at, hid, gdel, udel, wg, wu, wd,
+            terms[(s % inner + inner - own) % inner, s // inner, 2] = jnp.zeros(terms.shape[3:], terms.dtype)
+
+
+def _back_kernel(turn, gate_at, up_at, down_at, hid, gdel, udel, wg, wu, wd,
                  mixed, grads, macc, iacc):
-    feature_count = mixed.shape[0]
+    feature_count = macc.shape[0]
     slots = wg.shape[0]
     macc[...] = jnp.zeros(macc.shape, jnp.float32)
     iacc[...] = jnp.zeros(iacc.shape, jnp.float32)
@@ -122,8 +123,11 @@
             r, c = bu % feature_count, bu // feature_count
             iacc[r] += _dot(udel[c], wu[s], NT)
 
-    mixed[...] = macc[...].astype(mixed.dtype)
-    grads[...] = iacc[...].astype(grads.dtype)
+    count, per = mixed.shape[:2]
+    for piece in range(count):
+        at = (piece + count - turn[0]) % count
+        mixed[at] = macc[piece * per:(piece + 1) * per].astype(mixed.dtype)
+        grads[at] = iacc[piece * per:(piece + 1) * per].astype(grads.dtype)
 
 
 def _specs(n_smem, n_vmem):
@@ -132,7 +136,7 @@
     ] * n_vmem
 
 
-def front(gate_at, up_at, down_at, xb, dyb, xt, dyt, wg, wu, wd, hidden_count, inner,
+def front(turn, gate_at, up_at, down_at, xb, dyb, xt, dyt, wg, wu, wd, hidden_count, inner,
           interpret=False):
     feature_count, rows, size = xb.shape
     slots = wg.shape[0]
@@ -145,7 +149,7 @@
             jax.ShapeDtypeStruct(hshape, jnp.bfloat16),
             jax.ShapeDtypeStruct(hshape, jnp.bfloat16),
         ),
-        in_specs=_specs(3, 7),
+        in_specs=_specs(4, 7),
         out_specs=tuple(_specs(0, 4)),
         scratch_shapes=[pltpu.VMEM(hshape, jnp.float32)] * 3,
         cost_estimate=pl.CostEstimate(
@@ -155,19 +159,21 @@
             * size * 2,
         ),
         interpret=interpret,
-    )(gate_at, up_at, down_at, xb, dyb, xt, dyt, wg, wu, wd)
-
-
-def back(gate_at, up_at, down_at, hid, gdel, udel, wg, wu, wd, feature_count, interpret=False):
+    )(turn, gate_at, up_at, down_at, xb, dyb, xt, dyt, wg, wu, wd)
+
+
+def back(turn, gate_at, up_at, down_at, hid, gdel, udel, wg, wu, wd, feature_count, count,
+         interpret=False):
     _, rows, size = hid.shape
     fshape = (feature_count, rows, size)
+    pshape = (count, feature_count // count, rows, size)
     return pl.pallas_call(
         _back_kernel,
         out_shape=(
-            jax.ShapeDtypeStruct(fshape, jnp.bfloat16),
-            jax.ShapeDtypeStruct(fshape, jnp.bfloat16),
-        ),
-        in_specs=_specs(3, 6),
+            jax.ShapeDtypeStruct(pshape, jnp.bfloat16),
+            jax.ShapeDtypeStruct(pshape, jnp.bfloat16),
+        ),
+        in_specs=_specs(4, 6),
         out_specs=tuple(_specs(0, 2)),
         scratch_shapes=[pltpu.VMEM(fshape, jnp.float32)] * 2,
         cost_estimate=pl.CostEstimate(
@@ -177,7 +183,7 @@
             * size * 2,
         ),
         interpret=interpret,
-    )(gate_at, up_at, down_at, hid, gdel, udel, wg, wu, wd)
+    )(turn, gate_at, up_at, down_at, hid, gdel, udel, wg, wu, wd)
 
 
 def gather_blocks(parts, axis, block_size):
@@ -191,26 +197,21 @@
     return blocks, flipped
 
 
-def scatter_blocks(full, axis):
-    count = lax.axis_size(axis)
-    own = lax.axis_index(axis)
-    pieces = full.reshape((count, -1) + full.shape[1:])
-    total = lax.dynamic_index_in_dim(pieces, own, 0, keepdims=False).astype(jnp.float32)
+def scatter_blocks(pieces, axis):
+    count = pieces.shape[0]
+    total = pieces[0].astype(jnp.float32)
     for shift in range(1, count):
-        outgoing = lax.dynamic_index_in_dim(pieces, (own + shift) % count, 0, keepdims=False)
         pairs = [(source, (source + shift) % count) for source in range(count)]
-        total = total + lax.ppermute(outgoing, axis, pairs).astype(jnp.float32)
-    return total.astype(jnp.bfloat16).transpose(1, 0, 2).reshape(full.shape[1], -1)
+        total = total + lax.ppermute(pieces[shift], axis, pairs).astype(jnp.float32)
+    return total.astype(jnp.bfloat16).transpose(1, 0, 2).reshape(pieces.shape[2], -1)
 
 
 def reduce_inner(grid, inner):
-    count = lax.axis_size(inner)
-    own = lax.axis_index(inner)
-    total = lax.dynamic_index_in_dim(grid, own, 0, keepdims=False).astype(jnp.float32)
+    count = grid.shape[0]
+    total = grid[0].astype(jnp.float32)
     for shift in range(1, count):
-        outgoing = lax.dynamic_index_in_dim(grid, (own + shift) % count, 0, keepdims=False)
         pairs = [(source, (source + shift) % count) for source in range(count)]
-        total = total + lax.ppermute(outgoing, inner, pairs).astype(jnp.float32)
+        total = total + lax.ppermute(grid[shift], inner, pairs).astype(jnp.float32)
     return total.astype(jnp.bfloat16)
 
 
@@ -231,13 +232,16 @@
     )
     gate_at, up_at, down_at = gate_blocks[0], up_blocks[0], down_blocks[0]
     weights = (gate_values[0], up_values[0], down_values[0])
+    y_turn = lax.axis_index("y").astype(jnp.int32).reshape(1)
+    tensor_turn = lax.axis_index("tensor").astype(jnp.int32).reshape(1)
     stacked, hidden, gate_delta, up_delta = front(
-        gate_at, up_at, down_at, inputs, upstream, inputs_t, upstream_t, *weights, hidden_count,
+        y_turn, gate_at, up_at, down_at, inputs, upstream, inputs_t, upstream_t, *weights, hidden_count,
         lax.axis_size("y"),
     )
     partial = reduce_inner(stacked, "y")
     mixed_part, input_part = back(
-        gate_at, up_at, down_at, hidden, gate_delta, up_delta, *weights, feature_count
+        tensor_turn, gate_at, up_at, down_at, hidden, gate_delta, up_delta, *weights,
+        feature_count, tensor_count,
     )
     mixed = scatter_blocks(mixed_part, "tensor")
     grad_tokens = scatter_blocks(input_part, "tensor")
@@ -272,6 +276,4 @@
         P("tensor", dp, None, None),
         P("tensor", dp, None, None),
     )
-    return jax.shard_map(
-        layer, mesh=split_mesh, in_specs=in_specs, out_specs=out_specs, check_vma=False
-    )
+    return jax.shard_map(layer, mesh=split_mesh, in_specs=in_specs, out_specs=out_specs, check_vma=False)

time: 177 us -> 175 us (0.989)
    reshape x2 -> x0, other arithmetic: 3.52 us -> none  [scatter_blocks(): total.astype(jnp.bfloat16).transpose(1, 0, 2).reshape(full.shape[1], -1)]
    squeeze x3, local copies, waits for them, and re-layouts: 5.88 us -> 3.24 us  [the longest x1 1.76 us: reduce_inner(): total = total + lax.ppermute(grid[shift], inner, pairs).astype(jnp.float32)]
    transpose x0 -> x2, other arithmetic: none -> 2.1 us  [scatter_blocks(): total.astype(jnp.bfloat16).transpose(1, 0, 2).reshape(pieces.shape[2], -1)]
  transfers between devices with their start and end apart: 19 -> 19, of which waited for: 8 -> 10; matrix products, arithmetic and copies ran while one was open for 4% -> 3% of each run, Pallas kernels for 8% -> 8%
where the time goes in v2:
time: 175 us; the launch traced here: 172 us
  waiting for transfers between devices  73.5 us (42%)
  Pallas kernels  40.7 us (23%)
  starting transfers between devices  34.6 us (20%)
  local copies, waits for them, and re-layouts  17.2 us (10%)
  other arithmetic  5.72 us (3%)
    ppermute x3, waiting for transfers between devices, reduce_inner(): total = total + lax.ppermute(grid[shift], inner, pairs).astype(jnp.float32)  34.5 us
    all_to_all x1, waiting for transfers between devices, gather_blocks(): pieces = lax.all_to_all(spread_out, axis, 0, 0, tiled=True)  27.2 us
    pallas_call x1, Pallas kernels, front(): pl.pallas_call(_front_kernel, out_shape=(jax.ShapeDtypeStruct((inner, slo...  26.2 us
    ppermute x14, starting transfers between devices, scatter_blocks(): total = total + lax.ppermute(pieces[shift], axis, pairs).astype(jnp.float32)  17.4 us
    pallas_call x1, Pallas kernels, back(): pl.pallas_call(_back_kernel, out_shape=(jax.ShapeDtypeStruct(pshape, jnp....  14.6 us
    ppermute x14, waiting for transfers between devices, scatter_blocks(): total = total + lax.ppermute(pieces[shift], axis, pairs).astype(jnp.float32)  11.8 us
    all_to_all x1, starting transfers between devices, reduce_outer(): grid = lax.all_to_all(grid, outer, 0, 0, tiled=True)  8.47 us
    another operation x2, local copies, waits for them, and re-layouts, layer(): (inputs, upstream), (inputs_t, upstream_t) = gather_blocks(jnp.stack([tok...  4.73 us
  transfers between devices with their start and end apart: 19, of which 10 were waited for; matrix products, arithmetic and copies ran while one was open for 3% of the time, Pallas kernels for 8%

profile of v2, /device:TPU:8, one launch (start us, length us, event | category | flops | bytes accessed | tf_op | source)
XLA Modules:
  0.0 172.5 jit_solution(9948545448162397245)
XLA Ops:
  0.6 1.0 pad_maximum_fusion
  1.6 0.2 copy.27
  1.8 1.8 %broadcast_in_dim.4 = bf16[8,2,128,512]{2,3,1,0:T(8,128)(2,1)} broadcast(bf16[2,128,512]{1,2,0:T(8,128)(2,1)S(1)} %copy.27), dimensions={1,2,3} | broadcast | bytes 2359296 | tf_op jit(solution)/shard_map/broadcast_in_dim | solution.py:191
  3.6 4.3 %all-to-all-start = ((bf16[8,2,128,512]{2,3,1,0:T(8,128)(2,1)}), bf16[8,2,128,512]{2,3,1,0:T(8,128)(2,1)S(1)}, u32[]{:S(2)}, u32[]{:S(2)}) async-start(bf16[8,2,128,512]{2,3,1,0:T(8,128)(2,1)} %broadcast_in_dim.4), calls=%async_computation | async-start | bytes 4194304 | tf_op jit(solution)/shard_map/all_to_all | solution.py:192
  7.9 27.2 %all-to-all-done = bf16[8,2,128,512]{2,3,1,0:T(8,128)(2,1)S(1)} async-done(((bf16[8,2,128,512]{2,3,1,0:T(8,128)(2,1)}), bf16[8,2,128,512]{2,3,1,0:T(8,128)(2,1)S(1)}, u32[]{:S(2)}, u32[]{:S(2)}) %all-to-all-start) | async-done | bytes 2097184 | tf_op jit(solution)/shard_map/all_to_all | solution.py:192
  35.0 1.4 copy.36
  36.5 2.6 %copy.28 = bf16[8,2,128,4,128]{4,2,3,0,1:T(8,128)(2,1)} copy(bf16[8,2,128,4,128]{2,4,3,1,0:T(8,128)(2,1)S(1)} %bitcast.72) | data formatting | bytes 4194304 | tf_op jit(solution)/shard_map/reshape | solution.py:194
  39.1 3.3 %fusion.19 = (bf16[1,8,4,128,128]{4,3,2,1,0:T(8,128)(2,1)}, bf16[1,8,4,128,128]{4,3,2,1,0:T(8,128)(2,1)}) fusion(bf16[2,8,4,128,128]{4,3,2,1,0:T(8,128)(2,1)} %bitcast.74), kind=kLoop, calls=%fused_computation.43 | loop fusion | bytes 4194304 | tf_op jit(solution)/shard_map/unstack | solution.py:230
  42.4 1.4 fusion.20
  43.8 26.2 %shard_map.119 = (bf16[4,8,3,128,128]{4,3,2,1,0:T(8,128)(2,1)}, bf16[14,128,128]{2,1,0:T(8,128)(2,1)}, bf16[14,128,128]{2,1,0:T(8,128)(2,1)}, bf16[14,128,128]{2,1,0:T(8,128)(2,1)}) custom-call(s32[1]{0:T(128)} %bitcast.4.turn, s32[32]{0:T(128)} %bitcast.90, s32[32]{0:T(128)} %bitcast.92, s32[32]{0:T(128)} %bitcast.94, bf16[32,128,128]{2,1,0:T(8,128)(2,1)} %bitcast.84, ...), custom_call_target="tpu_custom_call" | custom-call | flops 805306368 | bytes 11862016 | tf_op jit(solution)/shard_map/pallas_call | solution.py:144
  70.0 1.8 %slice_bitcast_fusion.2 = (bf16[8,3,128,128]{3,2,1,0:T(8,128)(2,1)S(1)}, bf16[8,3,128,128]{3,2,1,0:T(8,128)(2,1)S(1)}, bf16[8,3,128,128]{3,2,1,0:T(8,128)(2,1)S(1)}) fusion(bf16[4,8,3,128,128]{4,3,2,1,0:T(8,128)(2,1)} %get-tuple-element.16), kind=kLoop, calls=%fused_computation.8 | loop fusion | bytes 4718592 | tf_op jit(solution)/shard_map/squeeze | solution.py:214
  71.8 1.7 collective-permute-start.14
  73.4 0.4 collective-permute-start.16
  73.9 2.3 %collective-permute-start.15 = (bf16[8,3,128,128]{3,2,1,0:T(8,128)(2,1)S(1)}, bf16[8,3,128,128]{3,2,1,0:T(8,128)(2,1)S(1)}, u32[]{:S(2)}, u32[]{:S(2)}) collective-permute-start(bf16[8,3,128,128]{3,2,1,0:T(8,128)(2,1)S(1)} %get-tuple-element.34), channel_id=1, source_target_pairs={{0,16},{8,24},{16,0},{24,8},{1,17},{9,25},{17,1},{25,9},{2,18},{10... | collective-permute-start | bytes 2359304 | tf_op jit(solution)/shard_map/ppermute | solution.py:214
  76.2 15.1 %collective-permute-done.14 = bf16[8,3,128,128]{3,2,1,0:T(8,128)(2,1)S(1)} collective-permute-done((bf16[8,3,128,128]{3,2,1,0:T(8,128)(2,1)S(1)}, bf16[8,3,128,128]{3,2,1,0:T(8,128)(2,1)S(1)}, u32[]{:S(2)}, u32[]{:S(2)}) %collective-permute-start.14) | collective-permute-done | bytes 786464 | tf_op jit(solution)/shard_map/ppermute | solution.py:214
  91.3 1.9 %collective-permute-done.16 = bf16[8,3,128,128]{3,2,1,0:T(8,128)(2,1)S(1)} collective-permute-done((bf16[8,3,128,128]{3,2,1,0:T(8,128)(2,1)S(1)}, bf16[8,3,128,128]{3,2,1,0:T(8,128)(2,1)S(1)}, u32[]{:S(2)}, u32[]{:S(2)}) %collective-permute-start.16) | collective-permute-done | bytes 786464 | tf_op jit(solution)/shard_map/ppermute | solution.py:214
  93.1 17.6 %collective-permute-done.15 = bf16[8,3,128,128]{3,2,1,0:T(8,128)(2,1)S(1)} collective-permute-done((bf16[8,3,128,128]{3,2,1,0:T(8,128)(2,1)S(1)}, bf16[8,3,128,128]{3,2,1,0:T(8,128)(2,1)S(1)}, u32[]{:S(2)}, u32[]{:S(2)}) %collective-permute-start.15) | collective-permute-done | bytes 786464 | tf_op jit(solution)/shard_map/ppermute | solution.py:214
  110.7 2.5 %fusion.2 = bf16[8,3,128,128]{3,2,1,0:T(8,128)(2,1)} fusion(bf16[8,3,128,128]{3,2,1,0:T(8,128)(2,1)S(1)} %collective-permute-done.16, bf16[8,3,128,128]{3,2,1,0:T(8,128)(2,1)S(1)} %collective-permute-done.15, bf16[8,3,128,128]{3,2,1,0:T(8,128)(2,1)S(1)} %collective-permute-done.14, bf16[4,8,3,128,128]{4,3,2,1,0:T(8,128)(2,1)} %get-tuple-element.16), kind=kLoop, calls=%fused_computation.4 | loop fusion | flops 3145728 | bytes 3932160 | tf_op jit(solution)/shard_map/convert_element_type | solution.py:215
  113.2 8.5 %all-to-all-start.1 = ((bf16[8,3,128,128]{3,2,1,0:T(8,128)(2,1)}), bf16[8,3,128,128]{3,2,1,0:T(8,128)(2,1)S(1)}, u32[]{:S(2)}, u32[]{:S(2)}) async-start(bf16[8,3,128,128]{3,2,1,0:T(8,128)(2,1)} %fusion.2), calls=%async_computation.1 | async-start | bytes 1572864 | tf_op jit(solution)/shard_map/all_to_all | solution.py:219
  121.7 14.6 %shard_map.120 = (bf16[8,4,128,128]{3,2,1,0:T(8,128)(2,1)}, bf16[8,4,128,128]{3,2,1,0:T(8,128)(2,1)}) custom-call(s32[1]{0:T(128)} %bitcast.turn, s32[32]{0:T(128)} %bitcast.91, s32[32]{0:T(128)} %bitcast.93, s32[32]{0:T(128)} %bitcast.95, bf16[14,128,128]{2,1,0:T(8,128)(2,1)} %get-tuple-element.11.hid, bf16[14,128,128]{2,1,0:T(8,128)(2,1)} %get-tuple-element.12.gdel, ...), custom_call_target="tpu_custom_call" | custom-call | flops 402653184 | bytes 6619136 | tf_op jit(solution)/shard_map/pallas_call | solution.py:170
  136.2 1.4 slice_bitcast_fusion.16
  137.7 1.5 collective-permute-start
  139.1 1.5 collective-permute-start.6
  140.6 0.3 collective-permute-start.5
  140.9 3.0 %collective-permute-start.3 = (bf16[4,128,128]{2,1,0:T(8,128)(2,1)S(1)}, bf16[4,128,128]{2,1,0:T(8,128)(2,1)S(1)}, u32[]{:S(2)}, u32[]{:S(2)}) collective-permute-start(bf16[4,128,128]{2,1,0:T(8,128)(2,1)S(1)} %get-tuple-element.50), channel_id=1, source_target_pairs={{0,4},{1,5},{2,6},{3,7},{4,0},{5,1},{6,2},{7,3},{8,12},{9,13},{10,... | collective-permute-start | bytes 393224 | tf_op jit(solution)/shard_map/ppermute | solution.py:205
  143.9 0.1 slice_bitcast_fusion.9
  144.0 0.1 collective-permute-start.2
  144.1 0.5 collective-permute-done.6
  144.5 0.3 collective-permute-start.1
  144.8 3.1 %collective-permute-done.5 = bf16[4,128,128]{2,1,0:T(8,128)(2,1)S(1)} collective-permute-done((bf16[4,128,128]{2,1,0:T(8,128)(2,1)S(1)}, bf16[4,128,128]{2,1,0:T(8,128)(2,1)S(1)}, u32[]{:S(2)}, u32[]{:S(2)}) %collective-permute-start.5) | collective-permute-done | bytes 131104 | tf_op jit(solution)/shard_map/ppermute | solution.py:205
  148.0 5.2 %collective-permute-start.13 = (bf16[4,128,128]{2,1,0:T(8,128)(2,1)S(1)}, bf16[4,128,128]{2,1,0:T(8,128)(2,1)S(1)}, u32[]{:S(2)}, u32[]{:S(2)}) collective-permute-start(bf16[4,128,128]{2,1,0:T(8,128)(2,1)S(1)} %get-tuple-element.40), channel_id=1, source_target_pairs={{0,7},{1,0},{2,1},{3,2},{4,3},{5,4},{6,5},{7,6},{8,15},{9,8},{10,9... | collective-permute-start | bytes 393224 | tf_op jit(solution)/shard_map/ppermute | solution.py:205
  153.2 3.1 %collective-permute-start.12 = (bf16[4,128,128]{2,1,0:T(8,128)(2,1)S(1)}, bf16[4,128,128]{2,1,0:T(8,128)(2,1)S(1)}, u32[]{:S(2)}, u32[]{:S(2)}) collective-permute-start(bf16[4,128,128]{2,1,0:T(8,128)(2,1)S(1)} %get-tuple-element.41), channel_id=1, source_target_pairs={{0,6},{1,7},{2,0},{3,1},{4,2},{5,3},{6,4},{7,5},{8,14},{9,15},{10,... | collective-permute-start | bytes 393224 | tf_op jit(solution)/shard_map/ppermute | solution.py:205
  156.3 0.4 collective-permute-done.1
  156.6 0.8 collective-permute-start.10
  157.4 0.6 collective-permute-start.9
  158.1 1.1 collective-permute-start.8
  159.2 1.0 fusion.17
  160.2 0.1 copy.30
  160.4 0.8 copy.32
  161.2 4.1 %collective-permute-done.12 = bf16[4,128,128]{2,1,0:T(8,128)(2,1)S(1)} collective-permute-done((bf16[4,128,128]{2,1,0:T(8,128)(2,1)S(1)}, bf16[4,128,128]{2,1,0:T(8,128)(2,1)S(1)}, u32[]{:S(2)}, u32[]{:S(2)}) %collective-permute-start.12) | collective-permute-done | bytes 131104 | tf_op jit(solution)/shard_map/ppermute | solution.py:205
  165.2 0.1 collective-permute-done.9
  165.3 3.7 %collective-permute-done.8 = bf16[4,128,128]{2,1,0:T(8,128)(2,1)} collective-permute-done((bf16[4,128,128]{2,1,0:T(8,128)(2,1)S(1)}, bf16[4,128,128]{2,1,0:T(8,128)(2,1)}, u32[]{:S(2)}, u32[]{:S(2)}) %collective-permute-start.8) | collective-permute-done | bytes 131104 | tf_op jit(solution)/shard_map/ppermute | solution.py:205
  169.0 1.0 fusion.18
  170.1 0.1 copy.31
  170.2 0.8 copy.33
  171.0 0.1 convert_reduce_fusion
  171.1 0.7 slice_bitcast_fusion.17
  171.7 0.7 copy.34
  (16 shorter events, 0.0 us)
Async XLA Ops:
  3.6 31.5 %all-to-all-start = ((bf16[8,2,128,512]{2,3,1,0:T(8,128)(2,1)}), bf16[8,2,128,512]{2,3,1,0:T(8,128)(2,1)S(1)}, u32[]{:S(2)}, u32[]{:S(2)}) async-start(bf16[8,2,128,512]{2,3,1,0:T(8,128)(2,1)} %broadcast_in_dim.4), calls=%async_computation | async-start | bytes 4194304 | tf_op jit(solution)/shard_map/all_to_all | solution.py:192
  39.1 3.3 %copy-start = (bf16[8,2,128,4,128]{4,2,3,0,1:T(8,128)(2,1)S(1)}, bf16[8,2,128,4,128]{4,2,3,0,1:T(8,128)(2,1)}, u32[]{:S(2)}) copy-start(bf16[8,2,128,4,128]{4,2,3,0,1:T(8,128)(2,1)} %copy.28) | copy-start | bytes 6291460
  71.8 19.5 %collective-permute-start.14 = (bf16[8,3,128,128]{3,2,1,0:T(8,128)(2,1)S(1)}, bf16[8,3,128,128]{3,2,1,0:T(8,128)(2,1)S(1)}, u32[]{:S(2)}, u32[]{:S(2)}) collective-permute-start(bf16[8,3,128,128]{3,2,1,0:T(8,128)(2,1)S(1)} %get-tuple-element.32), channel_id=1, source_target_pairs={{0,8},{8,16},{16,24},{24,0},{1,9},{9,17},{17,25},{25,1},{2,10},{10... | collective-permute-start | bytes 2359304 | tf_op jit(solution)/shard_map/ppermute | solution.py:214
  73.4 19.7 %collective-permute-start.16 = (bf16[8,3,128,128]{3,2,1,0:T(8,128)(2,1)S(1)}, bf16[8,3,128,128]{3,2,1,0:T(8,128)(2,1)S(1)}, u32[]{:S(2)}, u32[]{:S(2)}) collective-permute-start(bf16[8,3,128,128]{3,2,1,0:T(8,128)(2,1)S(1)} %get-tuple-element.33), channel_id=1, source_target_pairs={{0,24},{8,0},{16,8},{24,16},{1,25},{9,1},{17,9},{25,17},{2,26},{10... | collective-permute-start | bytes 2359304 | tf_op jit(solution)/shard_map/ppermute | solution.py:214
  73.9 36.8 %collective-permute-start.15 = (bf16[8,3,128,128]{3,2,1,0:T(8,128)(2,1)S(1)}, bf16[8,3,128,128]{3,2,1,0:T(8,128)(2,1)S(1)}, u32[]{:S(2)}, u32[]{:S(2)}) collective-permute-start(bf16[8,3,128,128]{3,2,1,0:T(8,128)(2,1)S(1)} %get-tuple-element.34), channel_id=1, source_target_pairs={{0,16},{8,24},{16,0},{24,8},{1,17},{9,25},{17,1},{25,9},{2,18},{10... | collective-permute-start | bytes 2359304 | tf_op jit(solution)/shard_map/ppermute | solution.py:214
  113.2 57.8 %all-to-all-start.1 = ((bf16[8,3,128,128]{3,2,1,0:T(8,128)(2,1)}), bf16[8,3,128,128]{3,2,1,0:T(8,128)(2,1)S(1)}, u32[]{:S(2)}, u32[]{:S(2)}) async-start(bf16[8,3,128,128]{3,2,1,0:T(8,128)(2,1)} %fusion.2), calls=%async_computation.1 | async-start | bytes 1572864 | tf_op jit(solution)/shard_map/all_to_all | solution.py:219
  136.2 7.6 %copy-start.1 = (bf16[8,4,128,128]{3,2,1,0:T(8,128)(2,1)S(1)}, bf16[8,4,128,128]{3,2,1,0:T(8,128)(2,1)}, u32[]{:S(2)}) copy-start(bf16[8,4,128,128]{3,2,1,0:T(8,128)(2,1)} %get-tuple-element.15) | copy-start | bytes 3145732
  137.7 6.3 %collective-permute-start = (bf16[4,128,128]{2,1,0:T(8,128)(2,1)S(1)}, bf16[4,128,128]{2,1,0:T(8,128)(2,1)S(1)}, u32[]{:S(2)}, u32[]{:S(2)}) collective-permute-start(bf16[4,128,128]{2,1,0:T(8,128)(2,1)S(1)} %get-tuple-element.46), channel_id=1, source_target_pairs={{0,1},{1,2},{2,3},{3,4},{4,5},{5,6},{6,7},{7,0},{8,9},{9,10},{10,1... | collective-permute-start | bytes 393224 | tf_op jit(solution)/shard_map/ppermute | solution.py:205
  139.1 5.4 %collective-permute-start.6 = (bf16[4,128,128]{2,1,0:T(8,128)(2,1)S(1)}, bf16[4,128,128]{2,1,0:T(8,128)(2,1)S(1)}, u32[]{:S(2)}, u32[]{:S(2)}) collective-permute-start(bf16[4,128,128]{2,1,0:T(8,128)(2,1)S(1)} %get-tuple-element.47), channel_id=1, source_target_pairs={{0,7},{1,0},{2,1},{3,2},{4,3},{5,4},{6,5},{7,6},{8,15},{9,8},{10,9... | collective-permute-start | bytes 393224 | tf_op jit(solution)/shard_map/ppermute | solution.py:205
  140.6 7.3 %collective-permute-start.5 = (bf16[4,128,128]{2,1,0:T(8,128)(2,1)S(1)}, bf16[4,128,128]{2,1,0:T(8,128)(2,1)S(1)}, u32[]{:S(2)}, u32[]{:S(2)}) collective-permute-start(bf16[4,128,128]{2,1,0:T(8,128)(2,1)S(1)} %get-tuple-element.48), channel_id=1, source_target_pairs={{0,6},{1,7},{2,0},{3,1},{4,2},{5,3},{6,4},{7,5},{8,14},{9,15},{10,... | collective-permute-start | bytes 393224 | tf_op jit(solution)/shard_map/ppermute | solution.py:205
  140.9 7.0 %collective-permute-start.4 = (bf16[4,128,128]{2,1,0:T(8,128)(2,1)S(1)}, bf16[4,128,128]{2,1,0:T(8,128)(2,1)S(1)}, u32[]{:S(2)}, u32[]{:S(2)}) collective-permute-start(bf16[4,128,128]{2,1,0:T(8,128)(2,1)S(1)} %get-tuple-element.49), channel_id=1, source_target_pairs={{0,5},{1,6},{2,7},{3,0},{4,1},{5,2},{6,3},{7,4},{8,13},{9,14},{10,... | collective-permute-start | bytes 393224 | tf_op jit(solution)/shard_map/ppermute | solution.py:205
  140.9 12.2 %collective-permute-start.3 = (bf16[4,128,128]{2,1,0:T(8,128)(2,1)S(1)}, bf16[4,128,128]{2,1,0:T(8,128)(2,1)S(1)}, u32[]{:S(2)}, u32[]{:S(2)}) collective-permute-start(bf16[4,128,128]{2,1,0:T(8,128)(2,1)S(1)} %get-tuple-element.50), channel_id=1, source_target_pairs={{0,4},{1,5},{2,6},{3,7},{4,0},{5,1},{6,2},{7,3},{8,12},{9,13},{10,... | collective-permute-start | bytes 393224 | tf_op jit(solution)/shard_map/ppermute | solution.py:205
  144.0 12.3 %collective-permute-start.2 = (bf16[4,128,128]{2,1,0:T(8,128)(2,1)S(1)}, bf16[4,128,128]{2,1,0:T(8,128)(2,1)S(1)}, u32[]{:S(2)}, u32[]{:S(2)}) collective-permute-start(bf16[4,128,128]{2,1,0:T(8,128)(2,1)S(1)} %get-tuple-element.51), channel_id=1, source_target_pairs={{0,3},{1,4},{2,5},{3,6},{4,7},{5,0},{6,1},{7,2},{8,11},{9,12},{10,... | collective-permute-start | bytes 393224 | tf_op jit(solution)/shard_map/ppermute | solution.py:205
  144.5 12.1 %collective-permute-start.1 = (bf16[4,128,128]{2,1,0:T(8,128)(2,1)S(1)}, bf16[4,128,128]{2,1,0:T(8,128)(2,1)S(1)}, u32[]{:S(2)}, u32[]{:S(2)}) collective-permute-start(bf16[4,128,128]{2,1,0:T(8,128)(2,1)S(1)} %get-tuple-element.52), channel_id=1, source_target_pairs={{0,2},{1,3},{2,4},{3,5},{4,6},{5,7},{6,0},{7,1},{8,10},{9,11},{10,... | collective-permute-start | bytes 393224 | tf_op jit(solution)/shard_map/ppermute | solution.py:205
  148.0 9.5 %collective-permute-start.7 = (bf16[4,128,128]{2,1,0:T(8,128)(2,1)S(1)}, bf16[4,128,128]{2,1,0:T(8,128)(2,1)S(1)}, u32[]{:S(2)}, u32[]{:S(2)}) collective-permute-start(bf16[4,128,128]{2,1,0:T(8,128)(2,1)S(1)} %get-tuple-element.39), channel_id=1, source_target_pairs={{0,1},{1,2},{2,3},{3,4},{4,5},{5,6},{6,7},{7,0},{8,9},{9,10},{10,1... | collective-permute-start | bytes 393224 | tf_op jit(solution)/shard_map/ppermute | solution.py:205
  148.0 10.1 %collective-permute-start.13 = (bf16[4,128,128]{2,1,0:T(8,128)(2,1)S(1)}, bf16[4,128,128]{2,1,0:T(8,128)(2,1)S(1)}, u32[]{:S(2)}, u32[]{:S(2)}) collective-permute-start(bf16[4,128,128]{2,1,0:T(8,128)(2,1)S(1)} %get-tuple-element.40), channel_id=1, source_target_pairs={{0,7},{1,0},{2,1},{3,2},{4,3},{5,4},{6,5},{7,6},{8,15},{9,8},{10,9... | collective-permute-start | bytes 393224 | tf_op jit(solution)/shard_map/ppermute | solution.py:205
  153.2 12.1 %collective-permute-start.12 = (bf16[4,128,128]{2,1,0:T(8,128)(2,1)S(1)}, bf16[4,128,128]{2,1,0:T(8,128)(2,1)S(1)}, u32[]{:S(2)}, u32[]{:S(2)}) collective-permute-start(bf16[4,128,128]{2,1,0:T(8,128)(2,1)S(1)} %get-tuple-element.41), channel_id=1, source_target_pairs={{0,6},{1,7},{2,0},{3,1},{4,2},{5,3},{6,4},{7,5},{8,14},{9,15},{10,... | collective-permute-start | bytes 393224 | tf_op jit(solution)/shard_map/ppermute | solution.py:205
  156.3 9.0 %collective-permute-start.11 = (bf16[4,128,128]{2,1,0:T(8,128)(2,1)S(1)}, bf16[4,128,128]{2,1,0:T(8,128)(2,1)S(1)}, u32[]{:S(2)}, u32[]{:S(2)}) collective-permute-start(bf16[4,128,128]{2,1,0:T(8,128)(2,1)S(1)} %get-tuple-element.42), channel_id=1, source_target_pairs={{0,5},{1,6},{2,7},{3,0},{4,1},{5,2},{6,3},{7,4},{8,13},{9,14},{10,... | collective-permute-start | bytes 393224 | tf_op jit(solution)/shard_map/ppermute | solution.py:205
  156.6 8.6 %collective-permute-start.10 = (bf16[4,128,128]{2,1,0:T(8,128)(2,1)S(1)}, bf16[4,128,128]{2,1,0:T(8,128)(2,1)S(1)}, u32[]{:S(2)}, u32[]{:S(2)}) collective-permute-start(bf16[4,128,128]{2,1,0:T(8,128)(2,1)S(1)} %get-tuple-element.43), channel_id=1, source_target_pairs={{0,4},{1,5},{2,6},{3,7},{4,0},{5,1},{6,2},{7,3},{8,12},{9,13},{10,... | collective-permute-start | bytes 393224 | tf_op jit(solution)/shard_map/ppermute | solution.py:205
  157.4 7.9 %collective-permute-start.9 = (bf16[4,128,128]{2,1,0:T(8,128)(2,1)S(1)}, bf16[4,128,128]{2,1,0:T(8,128)(2,1)S(1)}, u32[]{:S(2)}, u32[]{:S(2)}) collective-permute-start(bf16[4,128,128]{2,1,0:T(8,128)(2,1)S(1)} %get-tuple-element.44), channel_id=1, source_target_pairs={{0,3},{1,4},{2,5},{3,6},{4,7},{5,0},{6,1},{7,2},{8,11},{9,12},{10,... | collective-permute-start | bytes 393224 | tf_op jit(solution)/shard_map/ppermute | solution.py:205
  158.1 10.9 %collective-permute-start.8 = (bf16[4,128,128]{2,1,0:T(8,128)(2,1)S(1)}, bf16[4,128,128]{2,1,0:T(8,128)(2,1)}, u32[]{:S(2)}, u32[]{:S(2)}) collective-permute-start(bf16[4,128,128]{2,1,0:T(8,128)(2,1)S(1)} %get-tuple-element.45), channel_id=1, source_target_pairs={{0,2},{1,3},{2,4},{3,5},{4,6},{5,7},{6,0},{7,1},{8,10},{9,11},{10,... | collective-permute-start | bytes 393224 | tf_op jit(solution)/shard_map/ppermute | solution.py:205

commit v3 on v0

--- a/solution.py
+++ b/solution.py
@@ -215,8 +215,14 @@
 
 
 def reduce_outer(grid, outer):
-    grid = lax.all_to_all(grid, outer, 0, 0, tiled=True)
-    return grid.astype(jnp.float32).sum(0)
+    count = lax.axis_size(outer)
+    own = lax.axis_index(outer)
+    total = lax.dynamic_index_in_dim(grid, own, 0, keepdims=False).astype(jnp.float32)
+    for shift in range(1, count):
+        outgoing = lax.dynamic_index_in_dim(grid, (own + shift) % count, 0, keepdims=False)
+        pairs = [(source, (source + shift) % count) for source in range(count)]
+        total = total + lax.ppermute(outgoing, outer, pairs).astype(jnp.float32)
+    return total
 
 
 def layer(

time: 177 us -> 164 us (0.927); the launches traced: 174 us -> 163 us
  waiting for transfers between devices: 74.1 us -> 53.7 us
  starting transfers between devices: 35.3 us -> 46.9 us
    ppermute x3, waiting for transfers between devices: 33.9 us -> 0.01 us  [reduce_inner(): total = total + lax.ppermute(outgoing, inner, pairs).astype(jnp.float32)]
    ppermute x0 -> x7, starting transfers between devices: none -> 17.2 us  [reduce_outer(): total = total + lax.ppermute(outgoing, outer, pairs).astype(jnp.float32)]
    ppermute x0 -> x7, waiting for transfers between devices: none -> 15.6 us  [reduce_outer(): total = total + lax.ppermute(outgoing, outer, pairs).astype(jnp.float32)]
    all_to_all x1 -> x0, starting transfers between devices: 8.47 us -> none  [reduce_outer(): grid = lax.all_to_all(grid, outer, 0, 0, tiled=True)]
    ppermute x14, starting transfers between devices: 17.6 us -> 20.5 us  [scatter_blocks(): total = total + lax.ppermute(outgoing, axis, pairs).astype(jnp.float32)]
    ppermute x14, waiting for transfers between devices: 13 us -> 10.9 us  [scatter_blocks(): total = total + lax.ppermute(outgoing, axis, pairs).astype(jnp.float32)]
  transfers between devices with their start and end apart: 19 -> 25, of which waited for: 8 -> 11; matrix products, arithmetic and copies ran while one was open for 4% -> 4% of each run, Pallas kernels for 8% -> 9%
where the time goes in v3:
time: 164 us; the launch traced here: 163 us
  waiting for transfers between devices  53.7 us (33%)
  starting transfers between devices  46.9 us (29%)
  Pallas kernels  40.6 us (25%)
  local copies, waits for them, and re-layouts  15.8 us (10%)
  other arithmetic  5.42 us (3%)
    all_to_all x1, waiting for transfers between devices, gather_blocks(): pieces = lax.all_to_all(spread_out, axis, 0, 0, tiled=True)  27.2 us
    pallas_call x1, Pallas kernels, front(): pl.pallas_call(_front_kernel, out_shape=(jax.ShapeDtypeStruct((inner, slo...  26.1 us
    ppermute x14, starting transfers between devices, scatter_blocks(): total = total + lax.ppermute(outgoing, axis, pairs).astype(jnp.float32)  20.5 us
    ppermute x7, starting transfers between devices, reduce_outer(): total = total + lax.ppermute(outgoing, outer, pairs).astype(jnp.float32)  17.2 us
    ppermute x7, waiting for transfers between devices, reduce_outer(): total = total + lax.ppermute(outgoing, outer, pairs).astype(jnp.float32)  15.6 us
    pallas_call x1, Pallas kernels, back(): pl.pallas_call(_back_kernel, out_shape=(jax.ShapeDtypeStruct(fshape, jnp....  14.5 us
    ppermute x14, waiting for transfers between devices, scatter_blocks(): total = total + lax.ppermute(outgoing, axis, pairs).astype(jnp.float32)  10.9 us
    ppermute x3, starting transfers between devices, reduce_inner(): total = total + lax.ppermute(outgoing, inner, pairs).astype(jnp.float32)  4.93 us
  transfers between devices with their start and end apart: 25, of which 11 were waited for; matrix products, arithmetic and copies ran while one was open for 4% of the time, Pallas kernels for 9%

profile of v3, /device:TPU:8, one launch (start us, length us, event | category | flops | bytes accessed | tf_op | source)
XLA Modules:
  0.0 163.2 jit_solution(7938360392797794712)
XLA Ops:
  0.6 1.0 pad_maximum_fusion
  1.6 0.2 copy.19
  1.8 1.8 %broadcast_in_dim.4 = bf16[8,2,128,512]{2,3,1,0:T(8,128)(2,1)} broadcast(bf16[2,128,512]{1,2,0:T(8,128)(2,1)S(1)} %copy.19), dimensions={1,2,3} | broadcast | bytes 2359296 | tf_op jit(solution)/shard_map/broadcast_in_dim | solution.py:185
  3.6 4.3 %all-to-all-start = ((bf16[8,2,128,512]{2,3,1,0:T(8,128)(2,1)}), bf16[8,2,128,512]{2,3,1,0:T(8,128)(2,1)S(1)}, u32[]{:S(2)}, u32[]{:S(2)}) async-start(bf16[8,2,128,512]{2,3,1,0:T(8,128)(2,1)} %broadcast_in_dim.4), calls=%async_computation | async-start | bytes 4194304 | tf_op jit(solution)/shard_map/all_to_all | solution.py:186
  7.9 27.2 %all-to-all-done = bf16[8,2,128,512]{2,3,1,0:T(8,128)(2,1)S(1)} async-done(((bf16[8,2,128,512]{2,3,1,0:T(8,128)(2,1)}), bf16[8,2,128,512]{2,3,1,0:T(8,128)(2,1)S(1)}, u32[]{:S(2)}, u32[]{:S(2)}) %all-to-all-start) | async-done | bytes 2097184 | tf_op jit(solution)/shard_map/all_to_all | solution.py:186
  35.0 2.6 %copy.20 = bf16[8,2,128,4,128]{4,2,3,0,1:T(8,128)(2,1)} copy(bf16[8,2,128,4,128]{2,4,3,1,0:T(8,128)(2,1)S(1)} %bitcast.97) | data formatting | bytes 4194304 | tf_op jit(solution)/shard_map/reshape | solution.py:188
  37.6 0.1 copy.30
  37.8 1.4 copy-done
  39.2 1.5 fusion.27
  40.7 1.4 fusion.26
  42.1 26.1 %shard_map.119 = (bf16[4,8,3,128,128]{4,3,2,1,0:T(8,128)(2,1)}, bf16[14,128,128]{2,1,0:T(8,128)(2,1)}, bf16[14,128,128]{2,1,0:T(8,128)(2,1)}, bf16[14,128,128]{2,1,0:T(8,128)(2,1)}) custom-call(s32[32]{0:T(128)} %bitcast.117, s32[32]{0:T(128)} %bitcast.119, s32[32]{0:T(128)} %bitcast.121, bf16[32,128,128]{2,1,0:T(8,128)(2,1)} %bitcast.108, ...), custom_call_target="tpu_custom_call" | custom-call | flops 805306368 | bytes 11862016 | tf_op jit(solution)/shard_map/pallas_call | solution.py:140
  68.3 3.1 %dynamic-slice_bitcast_fusion.2 = (bf16[8,3,128,128]{3,2,1,0:T(8,128)(2,1)}, bf16[8,3,128,128]{3,2,1,0:T(8,128)(2,1)}, bf16[8,3,128,128]{3,2,1,0:T(8,128)(2,1)}) fusion(bf16[4,8,3,128,128]{4,3,2,1,0:T(8,128)(2,1)} %get-tuple-element.16, s32[]{:T(128)S(6)} %select_n.173, s32[]{:T(128)S(6)} %select_n.177, s32[]{:T(128)S(6)} %select_n.175), kind=kLoop, calls=%fused_computation.7 | loop fusion | bytes 4718604 | tf_op jit(solution)/shard_map/jit(dynamic_index_in_dim)/squeeze | solution.py:211
  71.3 1.4 collective-permute-start.16
  72.7 1.6 %collective-permute-start.15 = (bf16[8,3,128,128]{3,2,1,0:T(8,128)(2,1)}, bf16[8,3,128,128]{3,2,1,0:T(8,128)(2,1)S(1)}, u32[]{:S(2)}, u32[]{:S(2)}) collective-permute-start(bf16[8,3,128,128]{3,2,1,0:T(8,128)(2,1)} %get-tuple-element.29), channel_id=1, source_target_pairs={{0,16},{8,24},{16,0},{24,8},{1,17},{9,25},{17,1},{25,9},{2,18},{10... | collective-permute-start | bytes 2359304 | tf_op jit(solution)/shard_map/ppermute | solution.py:213
  74.4 1.9 %collective-permute-start.14 = (bf16[8,3,128,128]{3,2,1,0:T(8,128)(2,1)}, bf16[8,3,128,128]{3,2,1,0:T(8,128)(2,1)S(1)}, u32[]{:S(2)}, u32[]{:S(2)}) collective-permute-start(bf16[8,3,128,128]{3,2,1,0:T(8,128)(2,1)} %get-tuple-element.27), channel_id=1, source_target_pairs={{0,8},{8,16},{16,24},{24,0},{1,9},{9,17},{17,25},{25,1},{2,10},{10... | collective-permute-start | bytes 2359304 | tf_op jit(solution)/shard_map/ppermute | solution.py:213
  76.3 14.5 %shard_map.120 = (bf16[32,128,128]{2,1,0:T(8,128)(2,1)}, bf16[32,128,128]{2,1,0:T(8,128)(2,1)}) custom-call(s32[32]{0:T(128)} %bitcast.118, s32[32]{0:T(128)} %bitcast.120, s32[32]{0:T(128)} %bitcast.122, bf16[14,128,128]{2,1,0:T(8,128)(2,1)} %get-tuple-element.11.hid, bf16[14,128,128]{2,1,0:T(8,128)(2,1)} %get-tuple-element.12.gdel, ...), custom_call_target="tpu_custom_call" | custom-call | flops 402653184 | bytes 6619136 | tf_op jit(solution)/shard_map/pallas_call | solution.py:164
  90.8 2.2 %dynamic-slice_bitcast_fusion.16 = (bf16[4,128,128]{2,1,0:T(8,128)(2,1)}, bf16[4,128,128]{2,1,0:T(8,128)(2,1)S(1)}, bf16[4,128,128]{2,1,0:T(8,128)(2,1)S(1)}, bf...) fusion(bf16[8,4,128,128]{3,2,1,0:T(8,128)(2,1)} %bitcast.113, ...), kind=kLoop, calls=%fused_computation.50 | loop fusion | bytes 1835036 | tf_op jit(solution)/shard_map/jit(dynamic_index_in_dim)/squeeze | solution.py:200
  92.9 4.5 %collective-permute-start.5 = (bf16[4,128,128]{2,1,0:T(8,128)(2,1)S(1)}, bf16[4,128,128]{2,1,0:T(8,128)(2,1)}, u32[]{:S(2)}, u32[]{:S(2)}) collective-permute-start(bf16[4,128,128]{2,1,0:T(8,128)(2,1)S(1)} %get-tuple-element.43), channel_id=1, source_target_pairs={{0,6},{1,7},{2,0},{3,1},{4,2},{5,3},{6,4},{7,5},{8,14},{9,15},{10,... | collective-permute-start | bytes 393224 | tf_op jit(solution)/shard_map/ppermute | solution.py:202
  97.4 5.6 %collective-permute-start.4 = (bf16[4,128,128]{2,1,0:T(8,128)(2,1)}, bf16[4,128,128]{2,1,0:T(8,128)(2,1)}, u32[]{:S(2)}, u32[]{:S(2)}) collective-permute-start(bf16[4,128,128]{2,1,0:T(8,128)(2,1)} %get-tuple-element.44), channel_id=1, source_target_pairs={{0,5},{1,6},{2,7},{3,0},{4,1},{5,2},{6,3},{7,4},{8,13},{9,14},{10,... | collective-permute-start | bytes 393224 | tf_op jit(solution)/shard_map/ppermute | solution.py:202
  103.0 0.7 collective-permute-done.5
  103.6 2.3 %collective-permute-start.3 = (bf16[4,128,128]{2,1,0:T(8,128)(2,1)}, bf16[4,128,128]{2,1,0:T(8,128)(2,1)}, u32[]{:S(2)}, u32[]{:S(2)}) collective-permute-start(bf16[4,128,128]{2,1,0:T(8,128)(2,1)} %get-tuple-element.45), channel_id=1, source_target_pairs={{0,4},{1,5},{2,6},{3,7},{4,0},{5,1},{6,2},{7,3},{8,12},{9,13},{10,... | collective-permute-start | bytes 393224 | tf_op jit(solution)/shard_map/ppermute | solution.py:202
  105.9 0.7 collective-permute-done.4
  106.6 0.2 collective-permute-start.2
  106.8 3.6 %collective-permute-done.3 = bf16[4,128,128]{2,1,0:T(8,128)(2,1)} collective-permute-done((bf16[4,128,128]{2,1,0:T(8,128)(2,1)}, bf16[4,128,128]{2,1,0:T(8,128)(2,1)}, u32[]{:S(2)}, u32[]{:S(2)}) %collective-permute-start.3) | collective-permute-done | bytes 131104 | tf_op jit(solution)/shard_map/ppermute | solution.py:202
  110.5 2.8 %collective-permute-done.2 = bf16[4,128,128]{2,1,0:T(8,128)(2,1)S(1)} collective-permute-done((bf16[4,128,128]{2,1,0:T(8,128)(2,1)}, bf16[4,128,128]{2,1,0:T(8,128)(2,1)S(1)}, u32[]{:S(2)}, u32[]{:S(2)}) %collective-permute-start.2) | collective-permute-done | bytes 131104 | tf_op jit(solution)/shard_map/ppermute | solution.py:202
  113.3 1.9 %collective-permute-start = (bf16[4,128,128]{2,1,0:T(8,128)(2,1)}, bf16[4,128,128]{2,1,0:T(8,128)(2,1)S(1)}, u32[]{:S(2)}, u32[]{:S(2)}) collective-permute-start(bf16[4,128,128]{2,1,0:T(8,128)(2,1)} %get-tuple-element.41), channel_id=1, source_target_pairs={{0,1},{1,2},{2,3},{3,4},{4,5},{5,6},{6,7},{7,0},{8,9},{9,10},{10,1... | collective-permute-start | bytes 393224 | tf_op jit(solution)/shard_map/ppermute | solution.py:202
  115.2 2.3 %collective-permute-done.1 = bf16[4,128,128]{2,1,0:T(8,128)(2,1)S(1)} collective-permute-done((bf16[4,128,128]{2,1,0:T(8,128)(2,1)}, bf16[4,128,128]{2,1,0:T(8,128)(2,1)S(1)}, u32[]{:S(2)}, u32[]{:S(2)}) %collective-permute-start.1) | collective-permute-done | bytes 131104 | tf_op jit(solution)/shard_map/ppermute | solution.py:202
  117.5 1.5 collective-permute-start.11
  119.0 2.2 %collective-permute-start.10 = (bf16[4,128,128]{2,1,0:T(8,128)(2,1)S(1)}, bf16[4,128,128]{2,1,0:T(8,128)(2,1)S(1)}, u32[]{:S(2)}, u32[]{:S(2)}) collective-permute-start(bf16[4,128,128]{2,1,0:T(8,128)(2,1)S(1)} %get-tuple-element.38), channel_id=1, source_target_pairs={{0,4},{1,5},{2,6},{3,7},{4,0},{5,1},{6,2},{7,3},{8,12},{9,13},{10,... | collective-permute-start | bytes 393224 | tf_op jit(solution)/shard_map/ppermute | solution.py:202
  121.2 1.6 fusion.2
  122.9 0.4 collective-permute-start.9
  123.4 1.6 collective-permute-start.8
  125.0 0.3 collective-permute-start.7
  125.4 0.8 collective-permute-done.11
  126.2 5.9 %collective-permute-start.23 = (bf16[3,128,128]{2,1,0:T(8,128)(2,1)S(1)}, bf16[3,128,128]{2,1,0:T(8,128)(2,1)S(1)}, u32[]{:S(2)}, u32[]{:S(2)}) collective-permute-start(bf16[3,128,128]{2,1,0:T(8,128)(2,1)S(1)} %get-tuple-element.49), channel_id=1, source_target_pairs={{0,224},{32,0},{64,32},{96,64},{128,96},{160,128},{192,160},{224,1... | collective-permute-start | bytes 294920 | tf_op jit(solution)/shard_map/ppermute | solution.py:224
  132.1 1.5 collective-permute-start.22
  133.5 1.9 %copy_bitcast_fusion.2 = bf16[128,512]{1,0:T(8,128)(2,1)} fusion(bf16[4,128,128]{2,1,0:T(8,128)(2,1)S(1)} %collective-permute-done.6, bf16[4,128,128]{2,1,0:T(8,128)(2,1)} %collective-permute-done.5, bf16[4,128,128]{2,1,0:T(8,128)(2,1)} %collective-permute-done.4, bf16[4,128,128]{2,1,0:T(8,128)(2,1)} %collective-permute-done.3, ...), kind=kLoop, calls=%fused_computation.36 | loop fusion | flops 1048576 | bytes 1179652 | tf_op jit(solution)/shard_map/reshape | solution.py:203
  135.4 1.6 %collective-permute-start.21 = (bf16[3,128,128]{2,1,0:T(8,128)(2,1)S(1)}, bf16[3,128,128]{2,1,0:T(8,128)(2,1)S(1)}, u32[]{:S(2)}, u32[]{:S(2)}) collective-permute-start(bf16[3,128,128]{2,1,0:T(8,128)(2,1)S(1)} %get-tuple-element.51), channel_id=1, source_target_pairs={{0,160},{32,192},{64,224},{96,0},{128,32},{160,64},{192,96},{224,1... | collective-permute-start | bytes 294920 | tf_op jit(solution)/shard_map/ppermute | solution.py:224
  137.0 4.5 %collective-permute-start.20 = (bf16[3,128,128]{2,1,0:T(8,128)(2,1)S(1)}, bf16[3,128,128]{2,1,0:T(8,128)(2,1)S(1)}, u32[]{:S(2)}, u32[]{:S(2)}) collective-permute-start(bf16[3,128,128]{2,1,0:T(8,128)(2,1)S(1)} %get-tuple-element.52), channel_id=1, source_target_pairs={{0,128},{32,160},{64,192},{96,224},{128,0},{160,32},{192,64},{224,... | collective-permute-start | bytes 294920 | tf_op jit(solution)/shard_map/ppermute | solution.py:224
  141.6 1.9 %collective-permute-start.19 = (bf16[3,128,128]{2,1,0:T(8,128)(2,1)S(1)}, bf16[3,128,128]{2,1,0:T(8,128)(2,1)S(1)}, u32[]{:S(2)}, u32[]{:S(2)}) collective-permute-start(bf16[3,128,128]{2,1,0:T(8,128)(2,1)S(1)} %get-tuple-element.53), channel_id=1, source_target_pairs={{0,96},{32,128},{64,160},{96,192},{128,224},{160,0},{192,32},{224,... | collective-permute-start | bytes 294920 | tf_op jit(solution)/shard_map/ppermute | solution.py:224
  143.5 0.5 collective-permute-start.18
  144.0 1.3 collective-permute-start.17
  145.3 0.8 copy_bitcast_fusion.1
  146.1 9.0 %collective-permute-done.19 = bf16[3,128,128]{2,1,0:T(8,128)(2,1)S(1)} collective-permute-done((bf16[3,128,128]{2,1,0:T(8,128)(2,1)S(1)}, bf16[3,128,128]{2,1,0:T(8,128)(2,1)S(1)}, u32[]{:S(2)}, u32[]{:S(2)}) %collective-permute-start.19) | collective-permute-done | bytes 98336 | tf_op jit(solution)/shard_map/ppermute | solution.py:224
  155.1 2.0 %collective-permute-done.18 = bf16[3,128,128]{2,1,0:T(8,128)(2,1)S(1)} collective-permute-done((bf16[3,128,128]{2,1,0:T(8,128)(2,1)S(1)}, bf16[3,128,128]{2,1,0:T(8,128)(2,1)S(1)}, u32[]{:S(2)}, u32[]{:S(2)}) %collective-permute-start.18) | collective-permute-done | bytes 98336 | tf_op jit(solution)/shard_map/ppermute | solution.py:224
  157.1 4.5 %collective-permute-done.17 = bf16[3,128,128]{2,1,0:T(8,128)(2,1)S(1)} collective-permute-done((bf16[3,128,128]{2,1,0:T(8,128)(2,1)S(1)}, bf16[3,128,128]{2,1,0:T(8,128)(2,1)S(1)}, u32[]{:S(2)}, u32[]{:S(2)}) %collective-permute-start.17) | collective-permute-done | bytes 98336 | tf_op jit(solution)/shard_map/ppermute | solution.py:224
  161.8 0.7 slice_bitcast_fusion
  162.4 0.7 copy.24
  (25 shorter events, 0.4 us)
Async XLA Ops:
  3.6 31.5 %all-to-all-start = ((bf16[8,2,128,512]{2,3,1,0:T(8,128)(2,1)}), bf16[8,2,128,512]{2,3,1,0:T(8,128)(2,1)S(1)}, u32[]{:S(2)}, u32[]{:S(2)}) async-start(bf16[8,2,128,512]{2,3,1,0:T(8,128)(2,1)} %broadcast_in_dim.4), calls=%async_computation | async-start | bytes 4194304 | tf_op jit(solution)/shard_map/all_to_all | solution.py:186
  37.6 1.6 copy-start
  71.3 46.1 %collective-permute-start.16 = (bf16[8,3,128,128]{3,2,1,0:T(8,128)(2,1)}, bf16[8,3,128,128]{3,2,1,0:T(8,128)(2,1)S(1)}, u32[]{:S(2)}, u32[]{:S(2)}) collective-permute-start(bf16[8,3,128,128]{3,2,1,0:T(8,128)(2,1)} %get-tuple-element.28), channel_id=1, source_target_pairs={{0,24},{8,0},{16,8},{24,16},{1,25},{9,1},{17,9},{25,17},{2,26},{10... | collective-permute-start | bytes 2359304 | tf_op jit(solution)/shard_map/ppermute | solution.py:213
  72.7 44.8 %collective-permute-start.15 = (bf16[8,3,128,128]{3,2,1,0:T(8,128)(2,1)}, bf16[8,3,128,128]{3,2,1,0:T(8,128)(2,1)S(1)}, u32[]{:S(2)}, u32[]{:S(2)}) collective-permute-start(bf16[8,3,128,128]{3,2,1,0:T(8,128)(2,1)} %get-tuple-element.29), channel_id=1, source_target_pairs={{0,16},{8,24},{16,0},{24,8},{1,17},{9,25},{17,1},{25,9},{2,18},{10... | collective-permute-start | bytes 2359304 | tf_op jit(solution)/shard_map/ppermute | solution.py:213
  74.4 44.6 %collective-permute-start.14 = (bf16[8,3,128,128]{3,2,1,0:T(8,128)(2,1)}, bf16[8,3,128,128]{3,2,1,0:T(8,128)(2,1)S(1)}, u32[]{:S(2)}, u32[]{:S(2)}) collective-permute-start(bf16[8,3,128,128]{3,2,1,0:T(8,128)(2,1)} %get-tuple-element.27), channel_id=1, source_target_pairs={{0,8},{8,16},{16,24},{24,0},{1,9},{9,17},{17,25},{25,1},{2,10},{10... | collective-permute-start | bytes 2359304 | tf_op jit(solution)/shard_map/ppermute | solution.py:213
  90.7 19.7 %copy-start.1 = (bf16[32,128,128]{2,1,0:T(8,128)(2,1)S(1)}, bf16[32,128,128]{2,1,0:T(8,128)(2,1)}, u32[]{:S(2)}) copy-start(bf16[32,128,128]{2,1,0:T(8,128)(2,1)} %get-tuple-element.15) | copy-start | bytes 3145732
  92.9 4.5 %collective-permute-start.6 = (bf16[4,128,128]{2,1,0:T(8,128)(2,1)S(1)}, bf16[4,128,128]{2,1,0:T(8,128)(2,1)S(1)}, u32[]{:S(2)}, u32[]{:S(2)}) collective-permute-start(bf16[4,128,128]{2,1,0:T(8,128)(2,1)S(1)} %get-tuple-element.42), channel_id=1, source_target_pairs={{0,7},{1,0},{2,1},{3,2},{4,3},{5,4},{6,5},{7,6},{8,15},{9,8},{10,9... | collective-permute-start | bytes 393224 | tf_op jit(solution)/shard_map/ppermute | solution.py:202
  92.9 10.7 %collective-permute-start.5 = (bf16[4,128,128]{2,1,0:T(8,128)(2,1)S(1)}, bf16[4,128,128]{2,1,0:T(8,128)(2,1)}, u32[]{:S(2)}, u32[]{:S(2)}) collective-permute-start(bf16[4,128,128]{2,1,0:T(8,128)(2,1)S(1)} %get-tuple-element.43), channel_id=1, source_target_pairs={{0,6},{1,7},{2,0},{3,1},{4,2},{5,3},{6,4},{7,5},{8,14},{9,15},{10,... | collective-permute-start | bytes 393224 | tf_op jit(solution)/shard_map/ppermute | solution.py:202
  97.4 9.2 %collective-permute-start.4 = (bf16[4,128,128]{2,1,0:T(8,128)(2,1)}, bf16[4,128,128]{2,1,0:T(8,128)(2,1)}, u32[]{:S(2)}, u32[]{:S(2)}) collective-permute-start(bf16[4,128,128]{2,1,0:T(8,128)(2,1)} %get-tuple-element.44), channel_id=1, source_target_pairs={{0,5},{1,6},{2,7},{3,0},{4,1},{5,2},{6,3},{7,4},{8,13},{9,14},{10,... | collective-permute-start | bytes 393224 | tf_op jit(solution)/shard_map/ppermute | solution.py:202
  103.6 6.8 %collective-permute-start.3 = (bf16[4,128,128]{2,1,0:T(8,128)(2,1)}, bf16[4,128,128]{2,1,0:T(8,128)(2,1)}, u32[]{:S(2)}, u32[]{:S(2)}) collective-permute-start(bf16[4,128,128]{2,1,0:T(8,128)(2,1)} %get-tuple-element.45), channel_id=1, source_target_pairs={{0,4},{1,5},{2,6},{3,7},{4,0},{5,1},{6,2},{7,3},{8,12},{9,13},{10,... | collective-permute-start | bytes 393224 | tf_op jit(solution)/shard_map/ppermute | solution.py:202
  106.6 6.7 %collective-permute-start.2 = (bf16[4,128,128]{2,1,0:T(8,128)(2,1)}, bf16[4,128,128]{2,1,0:T(8,128)(2,1)S(1)}, u32[]{:S(2)}, u32[]{:S(2)}) collective-permute-start(bf16[4,128,128]{2,1,0:T(8,128)(2,1)} %get-tuple-element.46), channel_id=1, source_target_pairs={{0,3},{1,4},{2,5},{3,6},{4,7},{5,0},{6,1},{7,2},{8,11},{9,12},{10,... | collective-permute-start | bytes 393224 | tf_op jit(solution)/shard_map/ppermute | solution.py:202
  110.4 7.0 %collective-permute-start.1 = (bf16[4,128,128]{2,1,0:T(8,128)(2,1)}, bf16[4,128,128]{2,1,0:T(8,128)(2,1)S(1)}, u32[]{:S(2)}, u32[]{:S(2)}) collective-permute-start(bf16[4,128,128]{2,1,0:T(8,128)(2,1)} %get-tuple-element.47), channel_id=1, source_target_pairs={{0,2},{1,3},{2,4},{3,5},{4,6},{5,7},{6,0},{7,1},{8,10},{9,11},{10,... | collective-permute-start | bytes 393224 | tf_op jit(solution)/shard_map/ppermute | solution.py:202
  113.3 9.6 %collective-permute-start = (bf16[4,128,128]{2,1,0:T(8,128)(2,1)}, bf16[4,128,128]{2,1,0:T(8,128)(2,1)S(1)}, u32[]{:S(2)}, u32[]{:S(2)}) collective-permute-start(bf16[4,128,128]{2,1,0:T(8,128)(2,1)} %get-tuple-element.41), channel_id=1, source_target_pairs={{0,1},{1,2},{2,3},{3,4},{4,5},{5,6},{6,7},{7,0},{8,9},{9,10},{10,1... | collective-permute-start | bytes 393224 | tf_op jit(solution)/shard_map/ppermute | solution.py:202
  117.5 5.9 %collective-permute-start.13 = (bf16[4,128,128]{2,1,0:T(8,128)(2,1)S(1)}, bf16[4,128,128]{2,1,0:T(8,128)(2,1)S(1)}, u32[]{:S(2)}, u32[]{:S(2)}) collective-permute-start(bf16[4,128,128]{2,1,0:T(8,128)(2,1)S(1)} %get-tuple-element.35), channel_id=1, source_target_pairs={{0,7},{1,0},{2,1},{3,2},{4,3},{5,4},{6,5},{7,6},{8,15},{9,8},{10,9... | collective-permute-start | bytes 393224 | tf_op jit(solution)/shard_map/ppermute | solution.py:202
  117.5 7.6 %collective-permute-start.12 = (bf16[4,128,128]{2,1,0:T(8,128)(2,1)S(1)}, bf16[4,128,128]{2,1,0:T(8,128)(2,1)S(1)}, u32[]{:S(2)}, u32[]{:S(2)}) collective-permute-start(bf16[4,128,128]{2,1,0:T(8,128)(2,1)S(1)} %get-tuple-element.36), channel_id=1, source_target_pairs={{0,6},{1,7},{2,0},{3,1},{4,2},{5,3},{6,4},{7,5},{8,14},{9,15},{10,... | collective-permute-start | bytes 393224 | tf_op jit(solution)/shard_map/ppermute | solution.py:202
  117.5 8.7 %collective-permute-start.11 = (bf16[4,128,128]{2,1,0:T(8,128)(2,1)S(1)}, bf16[4,128,128]{2,1,0:T(8,128)(2,1)S(1)}, u32[]{:S(2)}, u32[]{:S(2)}) collective-permute-start(bf16[4,128,128]{2,1,0:T(8,128)(2,1)S(1)} %get-tuple-element.37), channel_id=1, source_target_pairs={{0,5},{1,6},{2,7},{3,0},{4,1},{5,2},{6,3},{7,4},{8,13},{9,14},{10,... | collective-permute-start | bytes 393224 | tf_op jit(solution)/shard_map/ppermute | solution.py:202
  119.0 13.1 %collective-permute-start.10 = (bf16[4,128,128]{2,1,0:T(8,128)(2,1)S(1)}, bf16[4,128,128]{2,1,0:T(8,128)(2,1)S(1)}, u32[]{:S(2)}, u32[]{:S(2)}) collective-permute-start(bf16[4,128,128]{2,1,0:T(8,128)(2,1)S(1)} %get-tuple-element.38), channel_id=1, source_target_pairs={{0,4},{1,5},{2,6},{3,7},{4,0},{5,1},{6,2},{7,3},{8,12},{9,13},{10,... | collective-permute-start | bytes 393224 | tf_op jit(solution)/shard_map/ppermute | solution.py:202
  122.9 12.5 %collective-permute-start.9 = (bf16[4,128,128]{2,1,0:T(8,128)(2,1)S(1)}, bf16[4,128,128]{2,1,0:T(8,128)(2,1)S(1)}, u32[]{:S(2)}, u32[]{:S(2)}) collective-permute-start(bf16[4,128,128]{2,1,0:T(8,128)(2,1)S(1)} %get-tuple-element.39), channel_id=1, source_target_pairs={{0,3},{1,4},{2,5},{3,6},{4,7},{5,0},{6,1},{7,2},{8,11},{9,12},{10,... | collective-permute-start | bytes 393224 | tf_op jit(solution)/shard_map/ppermute | solution.py:202
  123.4 13.7 %collective-permute-start.8 = (bf16[4,128,128]{2,1,0:T(8,128)(2,1)S(1)}, bf16[4,128,128]{2,1,0:T(8,128)(2,1)S(1)}, u32[]{:S(2)}, u32[]{:S(2)}) collective-permute-start(bf16[4,128,128]{2,1,0:T(8,128)(2,1)S(1)} %get-tuple-element.40), channel_id=1, source_target_pairs={{0,2},{1,3},{2,4},{3,5},{4,6},{5,7},{6,0},{7,1},{8,10},{9,11},{10,... | collective-permute-start | bytes 393224 | tf_op jit(solution)/shard_map/ppermute | solution.py:202
  125.0 16.5 %collective-permute-start.7 = (bf16[4,128,128]{2,1,0:T(8,128)(2,1)S(1)}, bf16[4,128,128]{2,1,0:T(8,128)(2,1)S(1)}, u32[]{:S(2)}, u32[]{:S(2)}) collective-permute-start(bf16[4,128,128]{2,1,0:T(8,128)(2,1)S(1)} %get-tuple-element.34), channel_id=1, source_target_pairs={{0,1},{1,2},{2,3},{3,4},{4,5},{5,6},{6,7},{7,0},{8,9},{9,10},{10,1... | collective-permute-start | bytes 393224 | tf_op jit(solution)/shard_map/ppermute | solution.py:202
  126.2 17.3 %collective-permute-start.23 = (bf16[3,128,128]{2,1,0:T(8,128)(2,1)S(1)}, bf16[3,128,128]{2,1,0:T(8,128)(2,1)S(1)}, u32[]{:S(2)}, u32[]{:S(2)}) collective-permute-start(bf16[3,128,128]{2,1,0:T(8,128)(2,1)S(1)} %get-tuple-element.49), channel_id=1, source_target_pairs={{0,224},{32,0},{64,32},{96,64},{128,96},{160,128},{192,160},{224,1... | collective-permute-start | bytes 294920 | tf_op jit(solution)/shard_map/ppermute | solution.py:224
  132.1 12.0 %collective-permute-start.22 = (bf16[3,128,128]{2,1,0:T(8,128)(2,1)S(1)}, bf16[3,128,128]{2,1,0:T(8,128)(2,1)S(1)}, u32[]{:S(2)}, u32[]{:S(2)}) collective-permute-start(bf16[3,128,128]{2,1,0:T(8,128)(2,1)S(1)} %get-tuple-element.50), channel_id=1, source_target_pairs={{0,192},{32,224},{64,0},{96,32},{128,64},{160,96},{192,128},{224,1... | collective-permute-start | bytes 294920 | tf_op jit(solution)/shard_map/ppermute | solution.py:224
  135.4 10.7 %collective-permute-start.21 = (bf16[3,128,128]{2,1,0:T(8,128)(2,1)S(1)}, bf16[3,128,128]{2,1,0:T(8,128)(2,1)S(1)}, u32[]{:S(2)}, u32[]{:S(2)}) collective-permute-start(bf16[3,128,128]{2,1,0:T(8,128)(2,1)S(1)} %get-tuple-element.51), channel_id=1, source_target_pairs={{0,160},{32,192},{64,224},{96,0},{128,32},{160,64},{192,96},{224,1... | collective-permute-start | bytes 294920 | tf_op jit(solution)/shard_map/ppermute | solution.py:224
  137.0 9.0 %collective-permute-start.20 = (bf16[3,128,128]{2,1,0:T(8,128)(2,1)S(1)}, bf16[3,128,128]{2,1,0:T(8,128)(2,1)S(1)}, u32[]{:S(2)}, u32[]{:S(2)}) collective-permute-start(bf16[3,128,128]{2,1,0:T(8,128)(2,1)S(1)} %get-tuple-element.52), channel_id=1, source_target_pairs={{0,128},{32,160},{64,192},{96,224},{128,0},{160,32},{192,64},{224,... | collective-permute-start | bytes 294920 | tf_op jit(solution)/shard_map/ppermute | solution.py:224
  141.6 13.5 %collective-permute-start.19 = (bf16[3,128,128]{2,1,0:T(8,128)(2,1)S(1)}, bf16[3,128,128]{2,1,0:T(8,128)(2,1)S(1)}, u32[]{:S(2)}, u32[]{:S(2)}) collective-permute-start(bf16[3,128,128]{2,1,0:T(8,128)(2,1)S(1)} %get-tuple-element.53), channel_id=1, source_target_pairs={{0,96},{32,128},{64,160},{96,192},{128,224},{160,0},{192,32},{224,... | collective-permute-start | bytes 294920 | tf_op jit(solution)/shard_map/ppermute | solution.py:224
  143.5 13.6 %collective-permute-start.18 = (bf16[3,128,128]{2,1,0:T(8,128)(2,1)S(1)}, bf16[3,128,128]{2,1,0:T(8,128)(2,1)S(1)}, u32[]{:S(2)}, u32[]{:S(2)}) collective-permute-start(bf16[3,128,128]{2,1,0:T(8,128)(2,1)S(1)} %get-tuple-element.54), channel_id=1, source_target_pairs={{0,64},{32,96},{64,128},{96,160},{128,192},{160,224},{192,0},{224,... | collective-permute-start | bytes 294920 | tf_op jit(solution)/shard_map/ppermute | solution.py:224
  144.0 17.6 %collective-permute-start.17 = (bf16[3,128,128]{2,1,0:T(8,128)(2,1)S(1)}, bf16[3,128,128]{2,1,0:T(8,128)(2,1)S(1)}, u32[]{:S(2)}, u32[]{:S(2)}) collective-permute-start(bf16[3,128,128]{2,1,0:T(8,128)(2,1)S(1)} %get-tuple-element.48), channel_id=1, source_target_pairs={{0,32},{32,64},{64,96},{96,128},{128,160},{160,192},{192,224},{224... | collective-permute-start | bytes 294920 | tf_op jit(solution)/shard_map/ppermute | solution.py:224

commit v4 on v3

--- a/solution.py
+++ b/solution.py
@@ -191,16 +191,18 @@
     return blocks, flipped
 
 
-def scatter_blocks(full, axis):
+def scatter_blocks(fulls, axis):
     count = lax.axis_size(axis)
     own = lax.axis_index(axis)
-    pieces = full.reshape((count, -1) + full.shape[1:])
+    rows = fulls[0].shape[1]
+    pieces = jnp.stack([full.reshape((count, -1) + full.shape[1:]) for full in fulls], 1)
     total = lax.dynamic_index_in_dim(pieces, own, 0, keepdims=False).astype(jnp.float32)
     for shift in range(1, count):
         outgoing = lax.dynamic_index_in_dim(pieces, (own + shift) % count, 0, keepdims=False)
         pairs = [(source, (source + shift) % count) for source in range(count)]
         total = total + lax.ppermute(outgoing, axis, pairs).astype(jnp.float32)
-    return total.astype(jnp.bfloat16).transpose(1, 0, 2).reshape(full.shape[1], -1)
+    total = total.astype(jnp.bfloat16)
+    return [part.transpose(1, 0, 2).reshape(rows, -1) for part in total]
 
 
 def reduce_inner(grid, inner):
@@ -245,8 +247,7 @@
     mixed_part, input_part = back(
         gate_at, up_at, down_at, hidden, gate_delta, up_delta, *weights, feature_count
     )
-    mixed = scatter_blocks(mixed_part, "tensor")
-    grad_tokens = scatter_blocks(input_part, "tensor")
+    mixed, grad_tokens = scatter_blocks((mixed_part, input_part), "tensor")
     combined = reduce_outer(partial, "z")[None]
     grad_gate = combined[None, :, 0]
     grad_up = combined[None, :, 1]

time: 164 us -> 173 us (1.055)
  the two profiles are of different devices: /device:TPU:8 before, /device:TPU:1 now
where the time goes in v4:
time: 173 us
  waiting for transfers between devices  63.2 us (37%)
  Pallas kernels  44.3 us (26%)
  starting transfers between devices  42.5 us (25%)
  local copies, waits for them, and re-layouts  14.9 us (9%)
  other arithmetic  7.17 us (4%)
    pallas_call x1, Pallas kernels, front(): pl.pallas_call(_front_kernel, out_shape=(jax.ShapeDtypeStruct((inner, slo...  28.6 us
    all_to_all x1, waiting for transfers between devices, gather_blocks(): pieces = lax.all_to_all(spread_out, axis, 0, 0, tiled=True)  26.2 us
    ppermute x7, starting transfers between devices, scatter_blocks(): total = total + lax.ppermute(outgoing, axis, pairs).astype(jnp.float32)  17.4 us
    ppermute x3, waiting for transfers between devices, reduce_inner(): total = total + lax.ppermute(outgoing, inner, pairs).astype(jnp.float32)  16 us
    pallas_call x1, Pallas kernels, back(): pl.pallas_call(_back_kernel, out_shape=(jax.ShapeDtypeStruct(fshape, jnp....  15.7 us
    ppermute x7, starting transfers between devices, reduce_outer(): total = total + lax.ppermute(outgoing, outer, pairs).astype(jnp.float32)  15.6 us
    ppermute x7, waiting for transfers between devices, reduce_outer(): total = total + lax.ppermute(outgoing, outer, pairs).astype(jnp.float32)  14 us
    ppermute x7, waiting for transfers between devices, scatter_blocks(): total = total + lax.ppermute(outgoing, axis, pairs).astype(jnp.float32)  6.97 us
  transfers between devices with their start and end apart: 18, of which 9 were waited for; matrix products, arithmetic and copies ran while one was open for 4% of the time, Pallas kernels for 0%

profile of v4, /device:TPU:1, one launch (start us, length us, event | category | flops | bytes accessed | tf_op | source)
XLA Modules:
  0.0 172.8 jit_solution(1061716863473112129)
XLA Ops:
  0.6 1.0 pad_maximum_fusion
  1.6 0.2 copy.19
  1.8 1.8 %broadcast_in_dim.4 = bf16[8,2,128,512]{2,3,1,0:T(8,128)(2,1)} broadcast(bf16[2,128,512]{1,2,0:T(8,128)(2,1)S(1)} %copy.19), dimensions={1,2,3} | broadcast | bytes 2359296 | tf_op jit(solution)/shard_map/broadcast_in_dim | solution.py:185
  3.6 6.7 %all-to-all-start = ((bf16[8,2,128,512]{2,3,1,0:T(8,128)(2,1)}), bf16[8,2,128,512]{2,3,1,0:T(8,128)(2,1)S(1)}, u32[]{:S(2)}, u32[]{:S(2)}) async-start(bf16[8,2,128,512]{2,3,1,0:T(8,128)(2,1)} %broadcast_in_dim.4), calls=%async_computation | async-start | bytes 4194304 | tf_op jit(solution)/shard_map/all_to_all | solution.py:186
  10.3 26.2 %all-to-all-done = bf16[8,2,128,512]{2,3,1,0:T(8,128)(2,1)S(1)} async-done(((bf16[8,2,128,512]{2,3,1,0:T(8,128)(2,1)}), bf16[8,2,128,512]{2,3,1,0:T(8,128)(2,1)S(1)}, u32[]{:S(2)}, u32[]{:S(2)}) %all-to-all-start) | async-done | bytes 2097184 | tf_op jit(solution)/shard_map/all_to_all | solution.py:186
  36.5 2.6 %copy.20 = bf16[8,2,128,4,128]{4,2,3,0,1:T(8,128)(2,1)} copy(bf16[8,2,128,4,128]{2,4,3,1,0:T(8,128)(2,1)S(1)} %bitcast.80) | data formatting | bytes 4194304 | tf_op jit(solution)/shard_map/reshape | solution.py:188
  39.1 0.1 copy.30
  39.2 1.4 copy-done.2
  40.7 1.5 fusion.33
  42.2 1.5 fusion.32
  43.6 28.6 %shard_map.119 = (bf16[4,8,3,128,128]{4,3,2,1,0:T(8,128)(2,1)}, bf16[14,128,128]{2,1,0:T(8,128)(2,1)}, bf16[14,128,128]{2,1,0:T(8,128)(2,1)}, bf16[14,128,128]{2,1,0:T(8,128)(2,1)}) custom-call(s32[32]{0:T(128)} %bitcast.102, s32[32]{0:T(128)} %bitcast.104, s32[32]{0:T(128)} %bitcast.106, bf16[32,128,128]{2,1,0:T(8,128)(2,1)} %bitcast.97, ...), custom_call_target="tpu_custom_call" | custom-call | flops 805306368 | bytes 11862016 | tf_op jit(solution)/shard_map/pallas_call | solution.py:140
  72.2 15.7 %shard_map.120 = (bf16[32,128,128]{2,1,0:T(8,128)(2,1)}, bf16[32,128,128]{2,1,0:T(8,128)(2,1)}) custom-call(s32[32]{0:T(128)} %bitcast.103, s32[32]{0:T(128)} %bitcast.105, s32[32]{0:T(128)} %bitcast.107, bf16[14,128,128]{2,1,0:T(8,128)(2,1)} %get-tuple-element.11.hid, bf16[14,128,128]{2,1,0:T(8,128)(2,1)} %get-tuple-element.12.gdel, ...), custom_call_target="tpu_custom_call" | custom-call | flops 402653184 | bytes 6619136 | tf_op jit(solution)/shard_map/pallas_call | solution.py:164
  87.9 1.1 fusion.24
  89.0 0.0 collective-permute-start.6
  89.1 0.2 copy-done
  89.2 0.3 copy-done.1
  89.6 1.2 fusion.23
  90.8 0.9 collective-permute-start.5
  91.7 0.4 collective-permute-start.4
  92.1 1.7 collective-permute-start.3
  93.8 1.8 %collective-permute-start.2 = (bf16[2,4,128,128]{3,2,1,0:T(8,128)(2,1)}, bf16[2,4,128,128]{3,2,1,0:T(8,128)(2,1)}, u32[]{:S(2)}, u32[]{:S(2)}) collective-permute-start(bf16[2,4,128,128]{3,2,1,0:T(8,128)(2,1)} %get-tuple-element.32), channel_id=1, source_target_pairs={{0,3},{1,4},{2,5},{3,6},{4,7},{5,0},{6,1},{7,2},{8,11},{9,12},{10,... | collective-permute-start | bytes 786440 | tf_op jit(solution)/shard_map/ppermute | solution.py:203
  95.6 3.1 %dynamic-slice_bitcast_fusion.2 = (bf16[8,3,128,128]{3,2,1,0:T(8,128)(2,1)}, bf16[8,3,128,128]{3,2,1,0:T(8,128)(2,1)}, bf16[8,3,128,128]{3,2,1,0:T(8,128)(2,1)}) fusion(bf16[4,8,3,128,128]{4,3,2,1,0:T(8,128)(2,1)} %get-tuple-element.16, s32[]{:T(128)S(6)} %select_n.151, s32[]{:T(128)S(6)} %select_n.155, s32[]{:T(128)S(6)} %select_n.153), kind=kLoop, calls=%fused_computation.23 | loop fusion | bytes 4718604 | tf_op jit(solution)/shard_map/jit(dynamic_index_in_dim)/squeeze | solution.py:213
  98.8 1.8 %collective-permute-start.9 = (bf16[8,3,128,128]{3,2,1,0:T(8,128)(2,1)}, bf16[8,3,128,128]{3,2,1,0:T(8,128)(2,1)S(1)}, u32[]{:S(2)}, u32[]{:S(2)}) collective-permute-start(bf16[8,3,128,128]{3,2,1,0:T(8,128)(2,1)} %get-tuple-element.28), channel_id=1, source_target_pairs={{0,24},{8,0},{16,8},{24,16},{1,25},{9,1},{17,9},{25,17},{2,26},{10... | collective-permute-start | bytes 2359304 | tf_op jit(solution)/shard_map/ppermute | solution.py:215
  100.6 0.7 collective-permute-start.8
  101.3 1.2 collective-permute-done.4
  102.5 0.4 collective-permute-start.7
  102.9 7.9 %collective-permute-start.1 = (bf16[2,4,128,128]{3,2,1,0:T(8,128)(2,1)}, bf16[2,4,128,128]{3,2,1,0:T(8,128)(2,1)}, u32[]{:S(2)}, u32[]{:S(2)}) collective-permute-start(bf16[2,4,128,128]{3,2,1,0:T(8,128)(2,1)} %get-tuple-element.31), channel_id=1, source_target_pairs={{0,2},{1,3},{2,4},{3,5},{4,6},{5,7},{6,0},{7,1},{8,10},{9,11},{10,... | collective-permute-start | bytes 786440 | tf_op jit(solution)/shard_map/ppermute | solution.py:203
  110.7 4.6 %collective-permute-start = (bf16[2,4,128,128]{3,2,1,0:T(8,128)(2,1)}, bf16[2,4,128,128]{3,2,1,0:T(8,128)(2,1)}, u32[]{:S(2)}, u32[]{:S(2)}) collective-permute-start(bf16[2,4,128,128]{3,2,1,0:T(8,128)(2,1)} %get-tuple-element.30), channel_id=1, source_target_pairs={{0,1},{1,2},{2,3},{3,4},{4,5},{5,6},{6,7},{7,0},{8,9},{9,10},{10,1... | collective-permute-start | bytes 786440 | tf_op jit(solution)/shard_map/ppermute | solution.py:203
  115.4 2.1 %collective-permute-done.1 = bf16[2,4,128,128]{3,2,1,0:T(8,128)(2,1)} collective-permute-done((bf16[2,4,128,128]{3,2,1,0:T(8,128)(2,1)}, bf16[2,4,128,128]{3,2,1,0:T(8,128)(2,1)}, u32[]{:S(2)}, u32[]{:S(2)}) %collective-permute-start.1) | collective-permute-done | bytes 262176 | tf_op jit(solution)/shard_map/ppermute | solution.py:203
  117.4 3.7 %collective-permute-done = bf16[2,4,128,128]{3,2,1,0:T(8,128)(2,1)} collective-permute-done((bf16[2,4,128,128]{3,2,1,0:T(8,128)(2,1)}, bf16[2,4,128,128]{3,2,1,0:T(8,128)(2,1)}, u32[]{:S(2)}, u32[]{:S(2)}) %collective-permute-start) | collective-permute-done | bytes 262176 | tf_op jit(solution)/shard_map/ppermute | solution.py:203
  121.1 1.6 fusion.9
  122.7 16.0 %collective-permute-done.7 = bf16[8,3,128,128]{3,2,1,0:T(8,128)(2,1)} collective-permute-done((bf16[8,3,128,128]{3,2,1,0:T(8,128)(2,1)}, bf16[8,3,128,128]{3,2,1,0:T(8,128)(2,1)}, u32[]{:S(2)}, u32[]{:S(2)}) %collective-permute-start.7) | collective-permute-done | bytes 786464 | tf_op jit(solution)/shard_map/ppermute | solution.py:215
  138.7 2.1 %fusion.2 = bf16[8,3,128,128]{3,2,1,0:T(8,128)(2,1)S(1)} fusion(bf16[8,3,128,128]{3,2,1,0:T(8,128)(2,1)S(1)} %collective-permute-done.9, bf16[8,3,128,128]{3,2,1,0:T(8,128)(2,1)} %collective-permute-done.8, bf16[8,3,128,128]{3,2,1,0:T(8,128)(2,1)} %collective-permute-done.7, bf16[4,8,3,128,128]{4,3,2,1,0:T(8,128)(2,1)} %get-tuple-element.16, s32[]{:T(128)S(6)} %select_n.149), kind=kLoop, calls=%fused_computation.20 | loop fusion | flops 3145728 | bytes 3932164 | tf_op jit(solution)/shard_map/convert_element_type | solution.py:216
  140.8 0.1 dynamic-slice_bitcast_fusion.9
  140.9 5.7 %collective-permute-start.16 = (bf16[3,128,128]{2,1,0:T(8,128)(2,1)S(1)}, bf16[3,128,128]{2,1,0:T(8,128)(2,1)S(1)}, u32[]{:S(2)}, u32[]{:S(2)}) collective-permute-start(bf16[3,128,128]{2,1,0:T(8,128)(2,1)S(1)} %get-tuple-element.41), channel_id=1, source_target_pairs={{0,224},{32,0},{64,32},{96,64},{128,96},{160,128},{192,160},{224,1... | collective-permute-start | bytes 294920 | tf_op jit(solution)/shard_map/ppermute | solution.py:226
  146.6 1.2 collective-permute-start.15
  147.8 0.7 collective-permute-start.14
  148.5 4.5 %collective-permute-start.13 = (bf16[3,128,128]{2,1,0:T(8,128)(2,1)S(1)}, bf16[3,128,128]{2,1,0:T(8,128)(2,1)S(1)}, u32[]{:S(2)}, u32[]{:S(2)}) collective-permute-start(bf16[3,128,128]{2,1,0:T(8,128)(2,1)S(1)} %get-tuple-element.44), channel_id=1, source_target_pairs={{0,128},{32,160},{64,192},{96,224},{128,0},{160,32},{192,64},{224,... | collective-permute-start | bytes 294920 | tf_op jit(solution)/shard_map/ppermute | solution.py:226
  153.0 2.2 %collective-permute-start.11 = (bf16[3,128,128]{2,1,0:T(8,128)(2,1)S(1)}, bf16[3,128,128]{2,1,0:T(8,128)(2,1)S(1)}, u32[]{:S(2)}, u32[]{:S(2)}) collective-permute-start(bf16[3,128,128]{2,1,0:T(8,128)(2,1)S(1)} %get-tuple-element.46), channel_id=1, source_target_pairs={{0,64},{32,96},{64,128},{96,160},{128,192},{160,224},{192,0},{224,... | collective-permute-start | bytes 294920 | tf_op jit(solution)/shard_map/ppermute | solution.py:226
  155.1 1.4 collective-permute-start.10
  156.5 0.7 copy_bitcast_fusion.1
  157.2 1.6 collective-permute-done.13
  158.8 3.5 %collective-permute-done.12 = bf16[3,128,128]{2,1,0:T(8,128)(2,1)S(1)} collective-permute-done((bf16[3,128,128]{2,1,0:T(8,128)(2,1)S(1)}, bf16[3,128,128]{2,1,0:T(8,128)(2,1)S(1)}, u32[]{:S(2)}, u32[]{:S(2)}) %collective-permute-start.12) | collective-permute-done | bytes 98336 | tf_op jit(solution)/shard_map/ppermute | solution.py:226
  162.4 7.0 %collective-permute-done.11 = bf16[3,128,128]{2,1,0:T(8,128)(2,1)S(1)} collective-permute-done((bf16[3,128,128]{2,1,0:T(8,128)(2,1)S(1)}, bf16[3,128,128]{2,1,0:T(8,128)(2,1)S(1)}, u32[]{:S(2)}, u32[]{:S(2)}) %collective-permute-start.11) | collective-permute-done | bytes 98336 | tf_op jit(solution)/shard_map/ppermute | solution.py:226
  169.3 1.9 %collective-permute-done.10 = bf16[3,128,128]{2,1,0:T(8,128)(2,1)S(1)} collective-permute-done((bf16[3,128,128]{2,1,0:T(8,128)(2,1)S(1)}, bf16[3,128,128]{2,1,0:T(8,128)(2,1)S(1)}, u32[]{:S(2)}, u32[]{:S(2)}) %collective-permute-start.10) | collective-permute-done | bytes 98336 | tf_op jit(solution)/shard_map/ppermute | solution.py:226
  171.3 0.1 fusion.31
  171.4 0.7 slice_bitcast_fusion.2
  172.0 0.7 copy.24
  (14 shorter events, 0.0 us)
Async XLA Ops:
  3.6 32.9 %all-to-all-start = ((bf16[8,2,128,512]{2,3,1,0:T(8,128)(2,1)}), bf16[8,2,128,512]{2,3,1,0:T(8,128)(2,1)S(1)}, u32[]{:S(2)}, u32[]{:S(2)}) async-start(bf16[8,2,128,512]{2,3,1,0:T(8,128)(2,1)} %broadcast_in_dim.4), calls=%async_computation | async-start | bytes 4194304 | tf_op jit(solution)/shard_map/all_to_all | solution.py:186
  39.1 1.6 copy-start.2
  87.9 1.4 copy-start
  87.9 1.7 copy-start.1
  89.0 9.7 %collective-permute-start.6 = (bf16[2,4,128,128]{3,2,1,0:T(8,128)(2,1)S(1)}, bf16[2,4,128,128]{3,2,1,0:T(8,128)(2,1)S(1)}, u32[]{:S(2)}, u32[]{:S(2)}) collective-permute-start(bf16[2,4,128,128]{3,2,1,0:T(8,128)(2,1)S(1)} %fusion.24), channel_id=1, source_target_pairs={{0,7},{1,0},{2,1},{3,2},{4,3},{5,4},{6,5},{7,6},{8,15},{9,8},{10,9... | collective-permute-start | bytes 786440 | tf_op jit(solution)/shard_map/ppermute | solution.py:203
  90.8 9.8 %collective-permute-start.5 = (bf16[2,4,128,128]{3,2,1,0:T(8,128)(2,1)}, bf16[2,4,128,128]{3,2,1,0:T(8,128)(2,1)S(1)}, u32[]{:S(2)}, u32[]{:S(2)}) collective-permute-start(bf16[2,4,128,128]{3,2,1,0:T(8,128)(2,1)} %get-tuple-element.35), channel_id=1, source_target_pairs={{0,6},{1,7},{2,0},{3,1},{4,2},{5,3},{6,4},{7,5},{8,14},{9,15},{10,... | collective-permute-start | bytes 786440 | tf_op jit(solution)/shard_map/ppermute | solution.py:203
  91.7 10.8 %collective-permute-start.4 = (bf16[2,4,128,128]{3,2,1,0:T(8,128)(2,1)}, bf16[2,4,128,128]{3,2,1,0:T(8,128)(2,1)}, u32[]{:S(2)}, u32[]{:S(2)}) collective-permute-start(bf16[2,4,128,128]{3,2,1,0:T(8,128)(2,1)} %get-tuple-element.34), channel_id=1, source_target_pairs={{0,5},{1,6},{2,7},{3,0},{4,1},{5,2},{6,3},{7,4},{8,13},{9,14},{10,... | collective-permute-start | bytes 786440 | tf_op jit(solution)/shard_map/ppermute | solution.py:203
  92.1 10.7 %collective-permute-start.3 = (bf16[2,4,128,128]{3,2,1,0:T(8,128)(2,1)}, bf16[2,4,128,128]{3,2,1,0:T(8,128)(2,1)}, u32[]{:S(2)}, u32[]{:S(2)}) collective-permute-start(bf16[2,4,128,128]{3,2,1,0:T(8,128)(2,1)} %get-tuple-element.33), channel_id=1, source_target_pairs={{0,4},{1,5},{2,6},{3,7},{4,0},{5,1},{6,2},{7,3},{8,12},{9,13},{10,... | collective-permute-start | bytes 786440 | tf_op jit(solution)/shard_map/ppermute | solution.py:203
  93.8 16.9 %collective-permute-start.2 = (bf16[2,4,128,128]{3,2,1,0:T(8,128)(2,1)}, bf16[2,4,128,128]{3,2,1,0:T(8,128)(2,1)}, u32[]{:S(2)}, u32[]{:S(2)}) collective-permute-start(bf16[2,4,128,128]{3,2,1,0:T(8,128)(2,1)} %get-tuple-element.32), channel_id=1, source_target_pairs={{0,3},{1,4},{2,5},{3,6},{4,7},{5,0},{6,1},{7,2},{8,11},{9,12},{10,... | collective-permute-start | bytes 786440 | tf_op jit(solution)/shard_map/ppermute | solution.py:203
  98.8 23.9 %collective-permute-start.9 = (bf16[8,3,128,128]{3,2,1,0:T(8,128)(2,1)}, bf16[8,3,128,128]{3,2,1,0:T(8,128)(2,1)S(1)}, u32[]{:S(2)}, u32[]{:S(2)}) collective-permute-start(bf16[8,3,128,128]{3,2,1,0:T(8,128)(2,1)} %get-tuple-element.28), channel_id=1, source_target_pairs={{0,24},{8,0},{16,8},{24,16},{1,25},{9,1},{17,9},{25,17},{2,26},{10... | collective-permute-start | bytes 2359304 | tf_op jit(solution)/shard_map/ppermute | solution.py:215
  100.6 22.1 %collective-permute-start.8 = (bf16[8,3,128,128]{3,2,1,0:T(8,128)(2,1)}, bf16[8,3,128,128]{3,2,1,0:T(8,128)(2,1)}, u32[]{:S(2)}, u32[]{:S(2)}) collective-permute-start(bf16[8,3,128,128]{3,2,1,0:T(8,128)(2,1)} %get-tuple-element.29), channel_id=1, source_target_pairs={{0,16},{8,24},{16,0},{24,8},{1,17},{9,25},{17,1},{25,9},{2,18},{10... | collective-permute-start | bytes 2359304 | tf_op jit(solution)/shard_map/ppermute | solution.py:215
  102.5 36.2 %collective-permute-start.7 = (bf16[8,3,128,128]{3,2,1,0:T(8,128)(2,1)}, bf16[8,3,128,128]{3,2,1,0:T(8,128)(2,1)}, u32[]{:S(2)}, u32[]{:S(2)}) collective-permute-start(bf16[8,3,128,128]{3,2,1,0:T(8,128)(2,1)} %get-tuple-element.27), channel_id=1, source_target_pairs={{0,8},{8,16},{16,24},{24,0},{1,9},{9,17},{17,25},{25,1},{2,10},{10... | collective-permute-start | bytes 2359304 | tf_op jit(solution)/shard_map/ppermute | solution.py:215
  102.9 14.6 %collective-permute-start.1 = (bf16[2,4,128,128]{3,2,1,0:T(8,128)(2,1)}, bf16[2,4,128,128]{3,2,1,0:T(8,128)(2,1)}, u32[]{:S(2)}, u32[]{:S(2)}) collective-permute-start(bf16[2,4,128,128]{3,2,1,0:T(8,128)(2,1)} %get-tuple-element.31), channel_id=1, source_target_pairs={{0,2},{1,3},{2,4},{3,5},{4,6},{5,7},{6,0},{7,1},{8,10},{9,11},{10,... | collective-permute-start | bytes 786440 | tf_op jit(solution)/shard_map/ppermute | solution.py:203
  110.7 10.4 %collective-permute-start = (bf16[2,4,128,128]{3,2,1,0:T(8,128)(2,1)}, bf16[2,4,128,128]{3,2,1,0:T(8,128)(2,1)}, u32[]{:S(2)}, u32[]{:S(2)}) collective-permute-start(bf16[2,4,128,128]{3,2,1,0:T(8,128)(2,1)} %get-tuple-element.30), channel_id=1, source_target_pairs={{0,1},{1,2},{2,3},{3,4},{4,5},{5,6},{6,7},{7,0},{8,9},{9,10},{10,1... | collective-permute-start | bytes 786440 | tf_op jit(solution)/shard_map/ppermute | solution.py:203
  140.9 12.0 %collective-permute-start.16 = (bf16[3,128,128]{2,1,0:T(8,128)(2,1)S(1)}, bf16[3,128,128]{2,1,0:T(8,128)(2,1)S(1)}, u32[]{:S(2)}, u32[]{:S(2)}) collective-permute-start(bf16[3,128,128]{2,1,0:T(8,128)(2,1)S(1)} %get-tuple-element.41), channel_id=1, source_target_pairs={{0,224},{32,0},{64,32},{96,64},{128,96},{160,128},{192,160},{224,1... | collective-permute-start | bytes 294920 | tf_op jit(solution)/shard_map/ppermute | solution.py:226
  146.6 8.6 %collective-permute-start.15 = (bf16[3,128,128]{2,1,0:T(8,128)(2,1)S(1)}, bf16[3,128,128]{2,1,0:T(8,128)(2,1)S(1)}, u32[]{:S(2)}, u32[]{:S(2)}) collective-permute-start(bf16[3,128,128]{2,1,0:T(8,128)(2,1)S(1)} %get-tuple-element.42), channel_id=1, source_target_pairs={{0,192},{32,224},{64,0},{96,32},{128,64},{160,96},{192,128},{224,1... | collective-permute-start | bytes 294920 | tf_op jit(solution)/shard_map/ppermute | solution.py:226
  147.8 9.5 %collective-permute-start.14 = (bf16[3,128,128]{2,1,0:T(8,128)(2,1)S(1)}, bf16[3,128,128]{2,1,0:T(8,128)(2,1)S(1)}, u32[]{:S(2)}, u32[]{:S(2)}) collective-permute-start(bf16[3,128,128]{2,1,0:T(8,128)(2,1)S(1)} %get-tuple-element.43), channel_id=1, source_target_pairs={{0,160},{32,192},{64,224},{96,0},{128,32},{160,64},{192,96},{224,1... | collective-permute-start | bytes 294920 | tf_op jit(solution)/shard_map/ppermute | solution.py:226
  148.5 10.4 %collective-permute-start.13 = (bf16[3,128,128]{2,1,0:T(8,128)(2,1)S(1)}, bf16[3,128,128]{2,1,0:T(8,128)(2,1)S(1)}, u32[]{:S(2)}, u32[]{:S(2)}) collective-permute-start(bf16[3,128,128]{2,1,0:T(8,128)(2,1)S(1)} %get-tuple-element.44), channel_id=1, source_target_pairs={{0,128},{32,160},{64,192},{96,224},{128,0},{160,32},{192,64},{224,... | collective-permute-start | bytes 294920 | tf_op jit(solution)/shard_map/ppermute | solution.py:226
  153.0 9.4 %collective-permute-start.12 = (bf16[3,128,128]{2,1,0:T(8,128)(2,1)S(1)}, bf16[3,128,128]{2,1,0:T(8,128)(2,1)S(1)}, u32[]{:S(2)}, u32[]{:S(2)}) collective-permute-start(bf16[3,128,128]{2,1,0:T(8,128)(2,1)S(1)} %get-tuple-element.45), channel_id=1, source_target_pairs={{0,96},{32,128},{64,160},{96,192},{128,224},{160,0},{192,32},{224,... | collective-permute-start | bytes 294920 | tf_op jit(solution)/shard_map/ppermute | solution.py:226
  153.0 16.4 %collective-permute-start.11 = (bf16[3,128,128]{2,1,0:T(8,128)(2,1)S(1)}, bf16[3,128,128]{2,1,0:T(8,128)(2,1)S(1)}, u32[]{:S(2)}, u32[]{:S(2)}) collective-permute-start(bf16[3,128,128]{2,1,0:T(8,128)(2,1)S(1)} %get-tuple-element.46), channel_id=1, source_target_pairs={{0,64},{32,96},{64,128},{96,160},{128,192},{160,224},{192,0},{224,... | collective-permute-start | bytes 294920 | tf_op jit(solution)/shard_map/ppermute | solution.py:226
  155.1 16.1 %collective-permute-start.10 = (bf16[3,128,128]{2,1,0:T(8,128)(2,1)S(1)}, bf16[3,128,128]{2,1,0:T(8,128)(2,1)S(1)}, u32[]{:S(2)}, u32[]{:S(2)}) collective-permute-start(bf16[3,128,128]{2,1,0:T(8,128)(2,1)S(1)} %get-tuple-element.40), channel_id=1, source_target_pairs={{0,32},{32,64},{64,96},{96,128},{128,160},{160,192},{192,224},{224... | collective-permute-start | bytes 294920 | tf_op jit(solution)/shard_map/ppermute | solution.py:226

commit v5 on v4

--- a/solution.py
+++ b/solution.py
@@ -182,8 +182,12 @@
 
 def gather_blocks(parts, axis, block_size):
     count = lax.axis_size(axis)
-    spread_out = jnp.broadcast_to(parts[None], (count,) + parts.shape)
-    pieces = lax.all_to_all(spread_out, axis, 0, 0, tiled=True)
+    own = lax.axis_index(axis)
+    received = [parts] + [
+        lax.ppermute(parts, axis, [(source, (source + shift) % count) for source in range(count)])
+        for shift in range(1, count)
+    ]
+    pieces = jnp.take(jnp.stack(received), (own - jnp.arange(count)) % count, axis=0)
     kinds, rows, width = parts.shape
     pieces = pieces.reshape(count, kinds, rows, width // block_size, block_size)
     blocks = pieces.transpose(1, 0, 3, 2, 4).reshape(kinds, -1, rows, block_size)

time: 173 us -> 174 us (level)
  the two profiles are of different devices: /device:TPU:1 before, /device:TPU:8 now
where the time goes in v5:
time: 174 us; the launch traced here: 171 us
  starting transfers between devices  54.6 us (31%)
  waiting for transfers between devices  43.4 us (25%)
  Pallas kernels  40.6 us (23%)
  local copies, waits for them, and re-layouts  21.2 us (12%)
  other arithmetic  10.8 us (6%)
    pallas_call x1, Pallas kernels, front(): pl.pallas_call(_front_kernel, out_shape=(jax.ShapeDtypeStruct((inner, slo...  26.1 us
    ppermute x7, starting transfers between devices, reduce_outer(): total = total + lax.ppermute(outgoing, outer, pairs).astype(jnp.float32)  17.5 us
    ppermute x7, starting transfers between devices, scatter_blocks(): total = total + lax.ppermute(outgoing, axis, pairs).astype(jnp.float32)  17.2 us
    pallas_call x1, Pallas kernels, back(): pl.pallas_call(_back_kernel, out_shape=(jax.ShapeDtypeStruct(fshape, jnp....  14.5 us
    ppermute x7, starting transfers between devices, gather_blocks(): lax.ppermute(parts, axis, [(source, (source + shift) % count) for source...  13.4 us
    ppermute x3, waiting for transfers between devices, reduce_inner(): total = total + lax.ppermute(outgoing, inner, pairs).astype(jnp.float32)  12.5 us
    ppermute x7, waiting for transfers between devices, scatter_blocks(): total = total + lax.ppermute(outgoing, axis, pairs).astype(jnp.float32)  12.5 us
    ppermute x7, waiting for transfers between devices, reduce_outer(): total = total + lax.ppermute(outgoing, outer, pairs).astype(jnp.float32)  11.4 us
  transfers between devices with their start and end apart: 24, of which 13 were waited for; matrix products, arithmetic and copies ran while one was open for 7% of the time, Pallas kernels for 0%

profile of v5, /device:TPU:8, one launch (start us, length us, event | category | flops | bytes accessed | tf_op | source)
XLA Modules:
  0.0 171.4 jit_solution(3376484204536013792)
XLA Ops:
  0.6 1.0 pad_maximum_fusion
  1.7 1.6 collective-permute-start.1
  3.2 2.0 %collective-permute-start.2 = (bf16[2,128,512]{2,1,0:T(8,128)(2,1)S(1)}, bf16[2,128,512]{2,1,0:T(8,128)(2,1)S(1)}, u32[]{:S(2)}, u32[]{:S(2)}) collective-permute-start(bf16[2,128,512]{2,1,0:T(8,128)(2,1)S(1)} %pad_maximum_fusion), channel_id=1, source_target_pairs={{0,3},{1,4},{2,5},{3,6},{4,7},{5,0},{6,1},{7,2},{8,11},{9,12},{10,... | collective-permute-start | bytes 786440 | tf_op jit(solution)/shard_map/ppermute | solution.py:187
  5.3 2.0 %collective-permute-start.3 = (bf16[2,128,512]{2,1,0:T(8,128)(2,1)S(1)}, bf16[2,128,512]{2,1,0:T(8,128)(2,1)S(1)}, u32[]{:S(2)}, u32[]{:S(2)}) collective-permute-start(bf16[2,128,512]{2,1,0:T(8,128)(2,1)S(1)} %pad_maximum_fusion), channel_id=1, source_target_pairs={{0,4},{1,5},{2,6},{3,7},{4,0},{5,1},{6,2},{7,3},{8,12},{9,13},{10,... | collective-permute-start | bytes 786440 | tf_op jit(solution)/shard_map/ppermute | solution.py:187
  7.3 1.7 collective-permute-start.4
  8.9 1.7 bitcast_dynamic-update-slice_fusion.7
  10.8 1.5 collective-permute-start.5
  13.1 4.6 %collective-permute-start.6 = (bf16[2,128,512]{2,1,0:T(8,128)(2,1)S(1)}, bf16[2,128,512]{2,1,0:T(8,128)(2,1)S(1)}, u32[]{:S(2)}, u32[]{:S(2)}) collective-permute-start(bf16[2,128,512]{2,1,0:T(8,128)(2,1)S(1)} %pad_maximum_fusion), channel_id=1, source_target_pairs={{0,7},{1,0},{2,1},{3,2},{4,3},{5,4},{6,5},{7,6},{8,15},{9,8},{10,9... | collective-permute-start | bytes 786440 | tf_op jit(solution)/shard_map/ppermute | solution.py:187
  18.4 4.6 %collective-permute-done.2 = bf16[2,128,512]{2,1,0:T(8,128)(2,1)S(1)} collective-permute-done((bf16[2,128,512]{2,1,0:T(8,128)(2,1)S(1)}, bf16[2,128,512]{2,1,0:T(8,128)(2,1)S(1)}, u32[]{:S(2)}, u32[]{:S(2)}) %collective-permute-start.2) | collective-permute-done | bytes 262176 | tf_op jit(solution)/shard_map/ppermute | solution.py:187
  23.0 0.7 bitcast_dynamic-update-slice_fusion.4
  25.1 1.0 collective-permute-done.4
  26.8 0.7 bitcast_dynamic-update-slice_fusion.1
  29.0 2.3 %gather_fusion = bf16[8,2,128,512]{3,2,1,0:T(8,128)(2,1)S(1)} fusion(bf16[8,2,128,512]{3,2,1,0:T(8,128)(2,1)} %bitcast_dynamic-update-slice_fusion, s32[1024]{0:T(1024)S(1)} %pad_clamp_fusion), kind=kCustom, calls=%fused_computation | custom fusion | bytes 4194336 | tf_op jit(solution)/shard_map/jit(_take)/gather | solution.py:190
  31.2 2.4 %copy.19 = bf16[8,2,128,512]{2,3,0,1:T(8,128)(2,1)} copy(bf16[8,2,128,512]{3,2,1,0:T(8,128)(2,1)S(1)} %gather_fusion) | data formatting | bytes 4194304 | tf_op jit(solution)/shard_map/jit(_take)/gather | solution.py:190
  33.6 1.9 %fusion.3 = (bf16[2,8,4,128,128]{4,3,2,1,0:T(8,128)(2,1)S(1)}, bf16[2,8,4,128,128]{3,4,2,1,0:T(8,128)(2,1)S(1)}) fusion(bf16[8,2,128,4,128]{2,4,3,0,1:T(8,128)(2,1)} %bitcast.104, pred[8]{0:T(512)(128)(4,1)S(1)} %compare_and_fusion), kind=kLoop, calls=%fused_computation.22 | loop fusion | flops 1048576 | bytes 6291464 | tf_op jit(solution)/shard_map/transpose | solution.py:194
  35.5 1.2 fusion.38
  36.7 2.3 %copy.14 = bf16[1,8,4,128,128]{4,3,2,1,0:T(8,128)(2,1)} copy(bf16[1,8,4,128,128]{3,4,2,1,0:T(8,128)(2,1)} %get-tuple-element.36) | data formatting | bytes 2097152 | tf_op jit(solution)/shard_map/unstack | solution.py:241
  39.0 1.3 copy.15
  40.3 1.4 fusion.37
  41.8 26.1 %shard_map.119 = (bf16[4,8,3,128,128]{4,3,2,1,0:T(8,128)(2,1)}, bf16[14,128,128]{2,1,0:T(8,128)(2,1)}, bf16[14,128,128]{2,1,0:T(8,128)(2,1)}, bf16[14,128,128]{2,1,0:T(8,128)(2,1)}) custom-call(s32[32]{0:T(128)} %bitcast.119, s32[32]{0:T(128)} %bitcast.121, s32[32]{0:T(128)} %bitcast.123, bf16[32,128,128]{2,1,0:T(8,128)(2,1)} %bitcast.105, ...), custom_call_target="tpu_custom_call" | custom-call | flops 805306368 | bytes 11862016 | tf_op jit(solution)/shard_map/pallas_call | solution.py:140
  67.9 14.5 %shard_map.120 = (bf16[32,128,128]{2,1,0:T(8,128)(2,1)}, bf16[32,128,128]{2,1,0:T(8,128)(2,1)}) custom-call(s32[32]{0:T(128)} %bitcast.120, s32[32]{0:T(128)} %bitcast.122, s32[32]{0:T(128)} %bitcast.124, bf16[14,128,128]{2,1,0:T(8,128)(2,1)} %get-tuple-element.11.hid, bf16[14,128,128]{2,1,0:T(8,128)(2,1)} %get-tuple-element.12.gdel, ...), custom_call_target="tpu_custom_call" | custom-call | flops 402653184 | bytes 6619136 | tf_op jit(solution)/shard_map/pallas_call | solution.py:164
  82.4 1.1 fusion.26
  83.6 4.0 %collective-permute-start.13 = (bf16[2,4,128,128]{3,2,1,0:T(8,128)(2,1)S(1)}, bf16[2,4,128,128]{3,2,1,0:T(8,128)(2,1)S(1)}, u32[]{:S(2)}, u32[]{:S(2)}) collective-permute-start(bf16[2,4,128,128]{3,2,1,0:T(8,128)(2,1)S(1)} %fusion.26), channel_id=1, source_target_pairs={{0,7},{1,0},{2,1},{3,2},{4,3},{5,4},{6,5},{7,6},{8,15},{9,8},{10,9... | collective-permute-start | bytes 786440 | tf_op jit(solution)/shard_map/ppermute | solution.py:207
  87.5 1.2 fusion.25
  88.7 2.7 %collective-permute-start.12 = (bf16[2,4,128,128]{3,2,1,0:T(8,128)(2,1)}, bf16[2,4,128,128]{3,2,1,0:T(8,128)(2,1)S(1)}, u32[]{:S(2)}, u32[]{:S(2)}) collective-permute-start(bf16[2,4,128,128]{3,2,1,0:T(8,128)(2,1)} %get-tuple-element.32), channel_id=1, source_target_pairs={{0,6},{1,7},{2,0},{3,1},{4,2},{5,3},{6,4},{7,5},{8,14},{9,15},{10,... | collective-permute-start | bytes 786440 | tf_op jit(solution)/shard_map/ppermute | solution.py:207
  91.4 3.1 %collective-permute-start.10 = (bf16[2,4,128,128]{3,2,1,0:T(8,128)(2,1)}, bf16[2,4,128,128]{3,2,1,0:T(8,128)(2,1)}, u32[]{:S(2)}, u32[]{:S(2)}) collective-permute-start(bf16[2,4,128,128]{3,2,1,0:T(8,128)(2,1)} %get-tuple-element.30), channel_id=1, source_target_pairs={{0,4},{1,5},{2,6},{3,7},{4,0},{5,1},{6,2},{7,3},{8,12},{9,13},{10,... | collective-permute-start | bytes 786440 | tf_op jit(solution)/shard_map/ppermute | solution.py:207
  94.5 0.9 collective-permute-start.9
  95.4 3.1 %dynamic-slice_bitcast_fusion.2 = (bf16[8,3,128,128]{3,2,1,0:T(8,128)(2,1)}, bf16[8,3,128,128]{3,2,1,0:T(8,128)(2,1)}, bf16[8,3,128,128]{3,2,1,0:T(8,128)(2,1)}) fusion(bf16[4,8,3,128,128]{4,3,2,1,0:T(8,128)(2,1)} %get-tuple-element.16, s32[]{:T(128)S(6)} %select_n.194, s32[]{:T(128)S(6)} %select_n.198, s32[]{:T(128)S(6)} %select_n.196), kind=kLoop, calls=%fused_computation.26 | loop fusion | bytes 4718604 | tf_op jit(solution)/shard_map/jit(dynamic_index_in_dim)/squeeze | solution.py:217
  98.5 2.6 %collective-permute-start.16 = (bf16[8,3,128,128]{3,2,1,0:T(8,128)(2,1)}, bf16[8,3,128,128]{3,2,1,0:T(8,128)(2,1)S(1)}, u32[]{:S(2)}, u32[]{:S(2)}) collective-permute-start(bf16[8,3,128,128]{3,2,1,0:T(8,128)(2,1)} %get-tuple-element.23), channel_id=1, source_target_pairs={{0,24},{8,0},{16,8},{24,16},{1,25},{9,1},{17,9},{25,17},{2,26},{10... | collective-permute-start | bytes 2359304 | tf_op jit(solution)/shard_map/ppermute | solution.py:219
  101.1 1.6 collective-permute-done.12
  102.7 2.3 %collective-permute-start.15 = (bf16[8,3,128,128]{3,2,1,0:T(8,128)(2,1)}, bf16[8,3,128,128]{3,2,1,0:T(8,128)(2,1)}, u32[]{:S(2)}, u32[]{:S(2)}) collective-permute-start(bf16[8,3,128,128]{3,2,1,0:T(8,128)(2,1)} %get-tuple-element.24), channel_id=1, source_target_pairs={{0,16},{8,24},{16,0},{24,8},{1,17},{9,25},{17,1},{25,9},{2,18},{10... | collective-permute-start | bytes 2359304 | tf_op jit(solution)/shard_map/ppermute | solution.py:219
  105.5 1.6 collective-permute-start.14
  107.3 6.6 %collective-permute-start.8 = (bf16[2,4,128,128]{3,2,1,0:T(8,128)(2,1)}, bf16[2,4,128,128]{3,2,1,0:T(8,128)(2,1)}, u32[]{:S(2)}, u32[]{:S(2)}) collective-permute-start(bf16[2,4,128,128]{3,2,1,0:T(8,128)(2,1)} %get-tuple-element.28), channel_id=1, source_target_pairs={{0,2},{1,3},{2,4},{3,5},{4,6},{5,7},{6,0},{7,1},{8,10},{9,11},{10,... | collective-permute-start | bytes 786440 | tf_op jit(solution)/shard_map/ppermute | solution.py:207
  113.9 10.1 %collective-permute-done.8 = bf16[2,4,128,128]{3,2,1,0:T(8,128)(2,1)} collective-permute-done((bf16[2,4,128,128]{3,2,1,0:T(8,128)(2,1)}, bf16[2,4,128,128]{3,2,1,0:T(8,128)(2,1)}, u32[]{:S(2)}, u32[]{:S(2)}) %collective-permute-start.8) | collective-permute-done | bytes 262176 | tf_op jit(solution)/shard_map/ppermute | solution.py:207
  124.0 1.6 fusion.11
  125.6 10.2 %collective-permute-done.15 = bf16[8,3,128,128]{3,2,1,0:T(8,128)(2,1)} collective-permute-done((bf16[8,3,128,128]{3,2,1,0:T(8,128)(2,1)}, bf16[8,3,128,128]{3,2,1,0:T(8,128)(2,1)}, u32[]{:S(2)}, u32[]{:S(2)}) %collective-permute-start.15) | collective-permute-done | bytes 786464 | tf_op jit(solution)/shard_map/ppermute | solution.py:219
  135.8 2.3 %collective-permute-done.14 = bf16[8,3,128,128]{3,2,1,0:T(8,128)(2,1)} collective-permute-done((bf16[8,3,128,128]{3,2,1,0:T(8,128)(2,1)}, bf16[8,3,128,128]{3,2,1,0:T(8,128)(2,1)}, u32[]{:S(2)}, u32[]{:S(2)}) %collective-permute-start.14) | collective-permute-done | bytes 786464 | tf_op jit(solution)/shard_map/ppermute | solution.py:219
  138.1 2.1 %fusion.2 = bf16[8,3,128,128]{3,2,1,0:T(8,128)(2,1)S(1)} fusion(bf16[8,3,128,128]{3,2,1,0:T(8,128)(2,1)S(1)} %collective-permute-done.16, bf16[8,3,128,128]{3,2,1,0:T(8,128)(2,1)} %collective-permute-done.15, bf16[8,3,128,128]{3,2,1,0:T(8,128)(2,1)} %collective-permute-done.14, bf16[4,8,3,128,128]{4,3,2,1,0:T(8,128)(2,1)} %get-tuple-element.16, s32[]{:T(128)S(6)} %select_n.192), kind=kLoop, calls=%fused_computation.21 | loop fusion | flops 3145728 | bytes 3932164 | tf_op jit(solution)/shard_map/convert_element_type | solution.py:220
  140.3 5.9 %collective-permute-start.23 = (bf16[3,128,128]{2,1,0:T(8,128)(2,1)S(1)}, bf16[3,128,128]{2,1,0:T(8,128)(2,1)S(1)}, u32[]{:S(2)}, u32[]{:S(2)}) collective-permute-start(bf16[3,128,128]{2,1,0:T(8,128)(2,1)S(1)} %get-tuple-element.38), channel_id=1, source_target_pairs={{0,224},{32,0},{64,32},{96,64},{128,96},{160,128},{192,160},{224,1... | collective-permute-start | bytes 294920 | tf_op jit(solution)/shard_map/ppermute | solution.py:230
  146.2 1.5 collective-permute-start.22
  148.2 5.0 %collective-permute-start.20 = (bf16[3,128,128]{2,1,0:T(8,128)(2,1)S(1)}, bf16[3,128,128]{2,1,0:T(8,128)(2,1)S(1)}, u32[]{:S(2)}, u32[]{:S(2)}) collective-permute-start(bf16[3,128,128]{2,1,0:T(8,128)(2,1)S(1)} %get-tuple-element.41), channel_id=1, source_target_pairs={{0,128},{32,160},{64,192},{96,224},{128,0},{160,32},{192,64},{224,... | collective-permute-start | bytes 294920 | tf_op jit(solution)/shard_map/ppermute | solution.py:230
  153.3 2.5 %collective-permute-start.18 = (bf16[3,128,128]{2,1,0:T(8,128)(2,1)S(1)}, bf16[3,128,128]{2,1,0:T(8,128)(2,1)S(1)}, u32[]{:S(2)}, u32[]{:S(2)}) collective-permute-start(bf16[3,128,128]{2,1,0:T(8,128)(2,1)S(1)} %get-tuple-element.43), channel_id=1, source_target_pairs={{0,64},{32,96},{64,128},{96,160},{128,192},{160,224},{192,0},{224,... | collective-permute-start | bytes 294920 | tf_op jit(solution)/shard_map/ppermute | solution.py:230
  155.7 2.1 %collective-permute-start.17 = (bf16[3,128,128]{2,1,0:T(8,128)(2,1)S(1)}, bf16[3,128,128]{2,1,0:T(8,128)(2,1)S(1)}, u32[]{:S(2)}, u32[]{:S(2)}) collective-permute-start(bf16[3,128,128]{2,1,0:T(8,128)(2,1)S(1)} %get-tuple-element.37), channel_id=1, source_target_pairs={{0,32},{32,64},{64,96},{96,128},{128,160},{160,192},{192,224},{224... | collective-permute-start | bytes 294920 | tf_op jit(solution)/shard_map/ppermute | solution.py:230
  157.8 0.7 copy_bitcast_fusion
  158.6 3.8 %collective-permute-done.21 = bf16[3,128,128]{2,1,0:T(8,128)(2,1)S(1)} collective-permute-done((bf16[3,128,128]{2,1,0:T(8,128)(2,1)S(1)}, bf16[3,128,128]{2,1,0:T(8,128)(2,1)S(1)}, u32[]{:S(2)}, u32[]{:S(2)}) %collective-permute-start.21) | collective-permute-done | bytes 98336 | tf_op jit(solution)/shard_map/ppermute | solution.py:230
  162.3 4.6 %collective-permute-done.19 = bf16[3,128,128]{2,1,0:T(8,128)(2,1)S(1)} collective-permute-done((bf16[3,128,128]{2,1,0:T(8,128)(2,1)S(1)}, bf16[3,128,128]{2,1,0:T(8,128)(2,1)S(1)}, u32[]{:S(2)}, u32[]{:S(2)}) %collective-permute-start.19) | collective-permute-done | bytes 98336 | tf_op jit(solution)/shard_map/ppermute | solution.py:230
  166.9 3.0 %collective-permute-done.18 = bf16[3,128,128]{2,1,0:T(8,128)(2,1)S(1)} collective-permute-done((bf16[3,128,128]{2,1,0:T(8,128)(2,1)S(1)}, bf16[3,128,128]{2,1,0:T(8,128)(2,1)S(1)}, u32[]{:S(2)}, u32[]{:S(2)}) %collective-permute-start.18) | collective-permute-done | bytes 98336 | tf_op jit(solution)/shard_map/ppermute | solution.py:230
  170.7 0.7 copy.18
  (36 shorter events, 7.1 us)
Async XLA Ops:
  1.6 9.2 %collective-permute-start = (bf16[2,128,512]{2,1,0:T(8,128)(2,1)S(1)}, bf16[2,128,512]{2,1,0:T(8,128)(2,1)S(1)}, u32[]{:S(2)}, u32[]{:S(2)}) collective-permute-start(bf16[2,128,512]{2,1,0:T(8,128)(2,1)S(1)} %pad_maximum_fusion), channel_id=1, source_target_pairs={{0,1},{1,2},{2,3},{3,4},{4,5},{5,6},{6,7},{7,0},{8,9},{9,10},{10,1... | collective-permute-start | bytes 786440 | tf_op jit(solution)/shard_map/ppermute | solution.py:187
  1.7 11.4 %collective-permute-start.1 = (bf16[2,128,512]{2,1,0:T(8,128)(2,1)S(1)}, bf16[2,128,512]{2,1,0:T(8,128)(2,1)S(1)}, u32[]{:S(2)}, u32[]{:S(2)}) collective-permute-start(bf16[2,128,512]{2,1,0:T(8,128)(2,1)S(1)} %pad_maximum_fusion), channel_id=1, source_target_pairs={{0,2},{1,3},{2,4},{3,5},{4,6},{5,7},{6,0},{7,1},{8,10},{9,11},{10,... | collective-permute-start | bytes 786440 | tf_op jit(solution)/shard_map/ppermute | solution.py:187
  3.2 19.8 %collective-permute-start.2 = (bf16[2,128,512]{2,1,0:T(8,128)(2,1)S(1)}, bf16[2,128,512]{2,1,0:T(8,128)(2,1)S(1)}, u32[]{:S(2)}, u32[]{:S(2)}) collective-permute-start(bf16[2,128,512]{2,1,0:T(8,128)(2,1)S(1)} %pad_maximum_fusion), channel_id=1, source_target_pairs={{0,3},{1,4},{2,5},{3,6},{4,7},{5,0},{6,1},{7,2},{8,11},{9,12},{10,... | collective-permute-start | bytes 786440 | tf_op jit(solution)/shard_map/ppermute | solution.py:187
  5.3 19.1 %collective-permute-start.3 = (bf16[2,128,512]{2,1,0:T(8,128)(2,1)S(1)}, bf16[2,128,512]{2,1,0:T(8,128)(2,1)S(1)}, u32[]{:S(2)}, u32[]{:S(2)}) collective-permute-start(bf16[2,128,512]{2,1,0:T(8,128)(2,1)S(1)} %pad_maximum_fusion), channel_id=1, source_target_pairs={{0,4},{1,5},{2,6},{3,7},{4,0},{5,1},{6,2},{7,3},{8,12},{9,13},{10,... | collective-permute-start | bytes 786440 | tf_op jit(solution)/shard_map/ppermute | solution.py:187
  7.3 18.8 %collective-permute-start.4 = (bf16[2,128,512]{2,1,0:T(8,128)(2,1)S(1)}, bf16[2,128,512]{2,1,0:T(8,128)(2,1)S(1)}, u32[]{:S(2)}, u32[]{:S(2)}) collective-permute-start(bf16[2,128,512]{2,1,0:T(8,128)(2,1)S(1)} %pad_maximum_fusion), channel_id=1, source_target_pairs={{0,5},{1,6},{2,7},{3,0},{4,1},{5,2},{6,3},{7,4},{8,13},{9,14},{10,... | collective-permute-start | bytes 786440 | tf_op jit(solution)/shard_map/ppermute | solution.py:187
  10.8 16.0 %collective-permute-start.5 = (bf16[2,128,512]{2,1,0:T(8,128)(2,1)S(1)}, bf16[2,128,512]{2,1,0:T(8,128)(2,1)S(1)}, u32[]{:S(2)}, u32[]{:S(2)}) collective-permute-start(bf16[2,128,512]{2,1,0:T(8,128)(2,1)S(1)} %pad_maximum_fusion), channel_id=1, source_target_pairs={{0,6},{1,7},{2,0},{3,1},{4,2},{5,3},{6,4},{7,5},{8,14},{9,15},{10,... | collective-permute-start | bytes 786440 | tf_op jit(solution)/shard_map/ppermute | solution.py:187
  13.1 15.2 %collective-permute-start.6 = (bf16[2,128,512]{2,1,0:T(8,128)(2,1)S(1)}, bf16[2,128,512]{2,1,0:T(8,128)(2,1)S(1)}, u32[]{:S(2)}, u32[]{:S(2)}) collective-permute-start(bf16[2,128,512]{2,1,0:T(8,128)(2,1)S(1)} %pad_maximum_fusion), channel_id=1, source_target_pairs={{0,7},{1,0},{2,1},{3,2},{4,3},{5,4},{6,5},{7,6},{8,15},{9,8},{10,9... | collective-permute-start | bytes 786440 | tf_op jit(solution)/shard_map/ppermute | solution.py:187
  82.4 5.1 %copy-start = (bf16[32,128,128]{2,1,0:T(8,128)(2,1)S(1)}, bf16[32,128,128]{2,1,0:T(8,128)(2,1)}, u32[]{:S(2)}) copy-start(bf16[32,128,128]{2,1,0:T(8,128)(2,1)} %get-tuple-element.14) | copy-start | bytes 3145732
  82.4 5.1 %copy-start.1 = (bf16[32,128,128]{2,1,0:T(8,128)(2,1)S(1)}, bf16[32,128,128]{2,1,0:T(8,128)(2,1)}, u32[]{:S(2)}) copy-start(bf16[32,128,128]{2,1,0:T(8,128)(2,1)} %get-tuple-element.15) | copy-start | bytes 3145732
  83.6 14.9 %collective-permute-start.13 = (bf16[2,4,128,128]{3,2,1,0:T(8,128)(2,1)S(1)}, bf16[2,4,128,128]{3,2,1,0:T(8,128)(2,1)S(1)}, u32[]{:S(2)}, u32[]{:S(2)}) collective-permute-start(bf16[2,4,128,128]{3,2,1,0:T(8,128)(2,1)S(1)} %fusion.26), channel_id=1, source_target_pairs={{0,7},{1,0},{2,1},{3,2},{4,3},{5,4},{6,5},{7,6},{8,15},{9,8},{10,9... | collective-permute-start | bytes 786440 | tf_op jit(solution)/shard_map/ppermute | solution.py:207
  88.7 14.0 %collective-permute-start.12 = (bf16[2,4,128,128]{3,2,1,0:T(8,128)(2,1)}, bf16[2,4,128,128]{3,2,1,0:T(8,128)(2,1)S(1)}, u32[]{:S(2)}, u32[]{:S(2)}) collective-permute-start(bf16[2,4,128,128]{3,2,1,0:T(8,128)(2,1)} %get-tuple-element.32), channel_id=1, source_target_pairs={{0,6},{1,7},{2,0},{3,1},{4,2},{5,3},{6,4},{7,5},{8,14},{9,15},{10,... | collective-permute-start | bytes 786440 | tf_op jit(solution)/shard_map/ppermute | solution.py:207
  91.4 14.0 %collective-permute-start.11 = (bf16[2,4,128,128]{3,2,1,0:T(8,128)(2,1)}, bf16[2,4,128,128]{3,2,1,0:T(8,128)(2,1)}, u32[]{:S(2)}, u32[]{:S(2)}) collective-permute-start(bf16[2,4,128,128]{3,2,1,0:T(8,128)(2,1)} %get-tuple-element.31), channel_id=1, source_target_pairs={{0,5},{1,6},{2,7},{3,0},{4,1},{5,2},{6,3},{7,4},{8,13},{9,14},{10,... | collective-permute-start | bytes 786440 | tf_op jit(solution)/shard_map/ppermute | solution.py:207
  91.4 15.9 %collective-permute-start.10 = (bf16[2,4,128,128]{3,2,1,0:T(8,128)(2,1)}, bf16[2,4,128,128]{3,2,1,0:T(8,128)(2,1)}, u32[]{:S(2)}, u32[]{:S(2)}) collective-permute-start(bf16[2,4,128,128]{3,2,1,0:T(8,128)(2,1)} %get-tuple-element.30), channel_id=1, source_target_pairs={{0,4},{1,5},{2,6},{3,7},{4,0},{5,1},{6,2},{7,3},{8,12},{9,13},{10,... | collective-permute-start | bytes 786440 | tf_op jit(solution)/shard_map/ppermute | solution.py:207
  94.5 19.4 %collective-permute-start.9 = (bf16[2,4,128,128]{3,2,1,0:T(8,128)(2,1)}, bf16[2,4,128,128]{3,2,1,0:T(8,128)(2,1)}, u32[]{:S(2)}, u32[]{:S(2)}) collective-permute-start(bf16[2,4,128,128]{3,2,1,0:T(8,128)(2,1)} %get-tuple-element.29), channel_id=1, source_target_pairs={{0,3},{1,4},{2,5},{3,6},{4,7},{5,0},{6,1},{7,2},{8,11},{9,12},{10,... | collective-permute-start | bytes 786440 | tf_op jit(solution)/shard_map/ppermute | solution.py:207
  98.5 27.1 %collective-permute-start.16 = (bf16[8,3,128,128]{3,2,1,0:T(8,128)(2,1)}, bf16[8,3,128,128]{3,2,1,0:T(8,128)(2,1)S(1)}, u32[]{:S(2)}, u32[]{:S(2)}) collective-permute-start(bf16[8,3,128,128]{3,2,1,0:T(8,128)(2,1)} %get-tuple-element.23), channel_id=1, source_target_pairs={{0,24},{8,0},{16,8},{24,16},{1,25},{9,1},{17,9},{25,17},{2,26},{10... | collective-permute-start | bytes 2359304 | tf_op jit(solution)/shard_map/ppermute | solution.py:219
  102.7 33.1 %collective-permute-start.15 = (bf16[8,3,128,128]{3,2,1,0:T(8,128)(2,1)}, bf16[8,3,128,128]{3,2,1,0:T(8,128)(2,1)}, u32[]{:S(2)}, u32[]{:S(2)}) collective-permute-start(bf16[8,3,128,128]{3,2,1,0:T(8,128)(2,1)} %get-tuple-element.24), channel_id=1, source_target_pairs={{0,16},{8,24},{16,0},{24,8},{1,17},{9,25},{17,1},{25,9},{2,18},{10... | collective-permute-start | bytes 2359304 | tf_op jit(solution)/shard_map/ppermute | solution.py:219
  105.5 32.7 %collective-permute-start.14 = (bf16[8,3,128,128]{3,2,1,0:T(8,128)(2,1)}, bf16[8,3,128,128]{3,2,1,0:T(8,128)(2,1)}, u32[]{:S(2)}, u32[]{:S(2)}) collective-permute-start(bf16[8,3,128,128]{3,2,1,0:T(8,128)(2,1)} %get-tuple-element.22), channel_id=1, source_target_pairs={{0,8},{8,16},{16,24},{24,0},{1,9},{9,17},{17,25},{25,1},{2,10},{10... | collective-permute-start | bytes 2359304 | tf_op jit(solution)/shard_map/ppermute | solution.py:219
  107.3 16.7 %collective-permute-start.8 = (bf16[2,4,128,128]{3,2,1,0:T(8,128)(2,1)}, bf16[2,4,128,128]{3,2,1,0:T(8,128)(2,1)}, u32[]{:S(2)}, u32[]{:S(2)}) collective-permute-start(bf16[2,4,128,128]{3,2,1,0:T(8,128)(2,1)} %get-tuple-element.28), channel_id=1, source_target_pairs={{0,2},{1,3},{2,4},{3,5},{4,6},{5,7},{6,0},{7,1},{8,10},{9,11},{10,... | collective-permute-start | bytes 786440 | tf_op jit(solution)/shard_map/ppermute | solution.py:207
  113.9 10.1 %collective-permute-start.7 = (bf16[2,4,128,128]{3,2,1,0:T(8,128)(2,1)}, bf16[2,4,128,128]{3,2,1,0:T(8,128)(2,1)}, u32[]{:S(2)}, u32[]{:S(2)}) collective-permute-start(bf16[2,4,128,128]{3,2,1,0:T(8,128)(2,1)} %get-tuple-element.27), channel_id=1, source_target_pairs={{0,1},{1,2},{2,3},{3,4},{4,5},{5,6},{6,7},{7,0},{8,9},{9,10},{10,1... | collective-permute-start | bytes 786440 | tf_op jit(solution)/shard_map/ppermute | solution.py:207
  140.3 13.0 %collective-permute-start.23 = (bf16[3,128,128]{2,1,0:T(8,128)(2,1)S(1)}, bf16[3,128,128]{2,1,0:T(8,128)(2,1)S(1)}, u32[]{:S(2)}, u32[]{:S(2)}) collective-permute-start(bf16[3,128,128]{2,1,0:T(8,128)(2,1)S(1)} %get-tuple-element.38), channel_id=1, source_target_pairs={{0,224},{32,0},{64,32},{96,64},{128,96},{160,128},{192,160},{224,1... | collective-permute-start | bytes 294920 | tf_op jit(solution)/shard_map/ppermute | solution.py:230
  146.2 9.5 %collective-permute-start.22 = (bf16[3,128,128]{2,1,0:T(8,128)(2,1)S(1)}, bf16[3,128,128]{2,1,0:T(8,128)(2,1)S(1)}, u32[]{:S(2)}, u32[]{:S(2)}) collective-permute-start(bf16[3,128,128]{2,1,0:T(8,128)(2,1)S(1)} %get-tuple-element.39), channel_id=1, source_target_pairs={{0,192},{32,224},{64,0},{96,32},{128,64},{160,96},{192,128},{224,1... | collective-permute-start | bytes 294920 | tf_op jit(solution)/shard_map/ppermute | solution.py:230
  147.7 14.6 %collective-permute-start.21 = (bf16[3,128,128]{2,1,0:T(8,128)(2,1)S(1)}, bf16[3,128,128]{2,1,0:T(8,128)(2,1)S(1)}, u32[]{:S(2)}, u32[]{:S(2)}) collective-permute-start(bf16[3,128,128]{2,1,0:T(8,128)(2,1)S(1)} %get-tuple-element.40), channel_id=1, source_target_pairs={{0,160},{32,192},{64,224},{96,0},{128,32},{160,64},{192,96},{224,1... | collective-permute-start | bytes 294920 | tf_op jit(solution)/shard_map/ppermute | solution.py:230
  148.2 14.1 %collective-permute-start.20 = (bf16[3,128,128]{2,1,0:T(8,128)(2,1)S(1)}, bf16[3,128,128]{2,1,0:T(8,128)(2,1)S(1)}, u32[]{:S(2)}, u32[]{:S(2)}) collective-permute-start(bf16[3,128,128]{2,1,0:T(8,128)(2,1)S(1)} %get-tuple-element.41), channel_id=1, source_target_pairs={{0,128},{32,160},{64,192},{96,224},{128,0},{160,32},{192,64},{224,... | collective-permute-start | bytes 294920 | tf_op jit(solution)/shard_map/ppermute | solution.py:230
  153.3 13.6 %collective-permute-start.19 = (bf16[3,128,128]{2,1,0:T(8,128)(2,1)S(1)}, bf16[3,128,128]{2,1,0:T(8,128)(2,1)S(1)}, u32[]{:S(2)}, u32[]{:S(2)}) collective-permute-start(bf16[3,128,128]{2,1,0:T(8,128)(2,1)S(1)} %get-tuple-element.42), channel_id=1, source_target_pairs={{0,96},{32,128},{64,160},{96,192},{128,224},{160,0},{192,32},{224,... | collective-permute-start | bytes 294920 | tf_op jit(solution)/shard_map/ppermute | solution.py:230
  153.3 16.6 %collective-permute-start.18 = (bf16[3,128,128]{2,1,0:T(8,128)(2,1)S(1)}, bf16[3,128,128]{2,1,0:T(8,128)(2,1)S(1)}, u32[]{:S(2)}, u32[]{:S(2)}) collective-permute-start(bf16[3,128,128]{2,1,0:T(8,128)(2,1)S(1)} %get-tuple-element.43), channel_id=1, source_target_pairs={{0,64},{32,96},{64,128},{96,160},{128,192},{160,224},{192,0},{224,... | collective-permute-start | bytes 294920 | tf_op jit(solution)/shard_map/ppermute | solution.py:230
  155.7 14.2 %collective-permute-start.17 = (bf16[3,128,128]{2,1,0:T(8,128)(2,1)S(1)}, bf16[3,128,128]{2,1,0:T(8,128)(2,1)S(1)}, u32[]{:S(2)}, u32[]{:S(2)}) collective-permute-start(bf16[3,128,128]{2,1,0:T(8,128)(2,1)S(1)} %get-tuple-element.37), channel_id=1, source_target_pairs={{0,32},{32,64},{64,96},{96,128},{128,160},{160,192},{192,224},{224... | collective-permute-start | bytes 294920 | tf_op jit(solution)/shard_map/ppermute | solution.py:230

commit v6 on v4

--- a/solution.py
+++ b/solution.py
@@ -24,7 +24,7 @@
     upre[...] = jnp.zeros(upre.shape, jnp.float32)
     hgrad[...] = jnp.zeros(hgrad.shape, jnp.float32)
 
-    @pl.loop(0, slots)
+    @pl.loop(0, slots, unroll=8)
     def _(s):
         bg = gate_at[s]
 
@@ -56,7 +56,7 @@
     gdel[...] = (hg * u * sig * (1.0 + g * (1.0 - sig))).astype(gdel.dtype)
     udel[...] = (hg * act).astype(udel.dtype)
 
-    @pl.loop(0, slots)
+    @pl.loop(0, slots, unroll=8)
     def _(s):
         bg = gate_at[s]
 
@@ -99,7 +99,7 @@
     macc[...] = jnp.zeros(macc.shape, jnp.float32)
     iacc[...] = jnp.zeros(iacc.shape, jnp.float32)
 
-    @pl.loop(0, slots)
+    @pl.loop(0, slots, unroll=8)
     def _(s):
         bd = down_at[s]
 

time: 173 us -> 173 us (level)
  no operation moved by 1% of the time
where the time goes in v6:
time: 173 us
  waiting for transfers between devices  63.2 us (37%)
  Pallas kernels  44.3 us (26%)
  starting transfers between devices  42.3 us (24%)
  local copies, waits for them, and re-layouts  14.9 us (9%)
  other arithmetic  7.17 us (4%)
    pallas_call x1, Pallas kernels, front(): pl.pallas_call(_front_kernel, out_shape=(jax.ShapeDtypeStruct((inner, slo...  28.6 us
    all_to_all x1, waiting for transfers between devices, gather_blocks(): pieces = lax.all_to_all(spread_out, axis, 0, 0, tiled=True)  26.2 us
    ppermute x7, starting transfers between devices, scatter_blocks(): total = total + lax.ppermute(outgoing, axis, pairs).astype(jnp.float32)  17.3 us
    ppermute x3, waiting for transfers between devices, reduce_inner(): total = total + lax.ppermute(outgoing, inner, pairs).astype(jnp.float32)  16 us
    pallas_call x1, Pallas kernels, back(): pl.pallas_call(_back_kernel, out_shape=(jax.ShapeDtypeStruct(fshape, jnp....  15.7 us
    ppermute x7, starting transfers between devices, reduce_outer(): total = total + lax.ppermute(outgoing, outer, pairs).astype(jnp.float32)  15.4 us
    ppermute x7, waiting for transfers between devices, reduce_outer(): total = total + lax.ppermute(outgoing, outer, pairs).astype(jnp.float32)  14 us
    ppermute x7, waiting for transfers between devices, scatter_blocks(): total = total + lax.ppermute(outgoing, axis, pairs).astype(jnp.float32)  6.94 us
  transfers between devices with their start and end apart: 18, of which 9 were waited for; matrix products, arithmetic and copies ran while one was open for 4% of the time, Pallas kernels for 0%

profile of v6, /device:TPU:1, one launch (start us, length us, event | category | flops | bytes accessed | tf_op | source)
XLA Modules:
  0.0 172.6 jit_solution(7636888207958006598)
XLA Ops:
  0.6 1.0 pad_maximum_fusion
  1.6 0.2 copy.19
  1.8 1.8 %broadcast_in_dim.4 = bf16[8,2,128,512]{2,3,1,0:T(8,128)(2,1)} broadcast(bf16[2,128,512]{1,2,0:T(8,128)(2,1)S(1)} %copy.19), dimensions={1,2,3} | broadcast | bytes 2359296 | tf_op jit(solution)/shard_map/broadcast_in_dim | solution.py:185
  3.6 6.7 %all-to-all-start = ((bf16[8,2,128,512]{2,3,1,0:T(8,128)(2,1)}), bf16[8,2,128,512]{2,3,1,0:T(8,128)(2,1)S(1)}, u32[]{:S(2)}, u32[]{:S(2)}) async-start(bf16[8,2,128,512]{2,3,1,0:T(8,128)(2,1)} %broadcast_in_dim.4), calls=%async_computation | async-start | bytes 4194304 | tf_op jit(solution)/shard_map/all_to_all | solution.py:186
  10.3 26.2 %all-to-all-done = bf16[8,2,128,512]{2,3,1,0:T(8,128)(2,1)S(1)} async-done(((bf16[8,2,128,512]{2,3,1,0:T(8,128)(2,1)}), bf16[8,2,128,512]{2,3,1,0:T(8,128)(2,1)S(1)}, u32[]{:S(2)}, u32[]{:S(2)}) %all-to-all-start) | async-done | bytes 2097184 | tf_op jit(solution)/shard_map/all_to_all | solution.py:186
  36.5 2.6 %copy.20 = bf16[8,2,128,4,128]{4,2,3,0,1:T(8,128)(2,1)} copy(bf16[8,2,128,4,128]{2,4,3,1,0:T(8,128)(2,1)S(1)} %bitcast.80) | data formatting | bytes 4194304 | tf_op jit(solution)/shard_map/reshape | solution.py:188
  39.1 0.1 copy.30
  39.2 1.4 copy-done.2
  40.7 1.5 fusion.33
  42.2 1.5 fusion.32
  43.6 28.6 %shard_map.119 = (bf16[4,8,3,128,128]{4,3,2,1,0:T(8,128)(2,1)}, bf16[14,128,128]{2,1,0:T(8,128)(2,1)}, bf16[14,128,128]{2,1,0:T(8,128)(2,1)}, bf16[14,128,128]{2,1,0:T(8,128)(2,1)}) custom-call(s32[32]{0:T(128)} %bitcast.102, s32[32]{0:T(128)} %bitcast.104, s32[32]{0:T(128)} %bitcast.106, bf16[32,128,128]{2,1,0:T(8,128)(2,1)} %bitcast.97, ...), custom_call_target="tpu_custom_call" | custom-call | flops 805306368 | bytes 11862016 | tf_op jit(solution)/shard_map/pallas_call | solution.py:140
  72.2 15.7 %shard_map.120 = (bf16[32,128,128]{2,1,0:T(8,128)(2,1)}, bf16[32,128,128]{2,1,0:T(8,128)(2,1)}) custom-call(s32[32]{0:T(128)} %bitcast.103, s32[32]{0:T(128)} %bitcast.105, s32[32]{0:T(128)} %bitcast.107, bf16[14,128,128]{2,1,0:T(8,128)(2,1)} %get-tuple-element.11.hid, bf16[14,128,128]{2,1,0:T(8,128)(2,1)} %get-tuple-element.12.gdel, ...), custom_call_target="tpu_custom_call" | custom-call | flops 402653184 | bytes 6619136 | tf_op jit(solution)/shard_map/pallas_call | solution.py:164
  87.9 1.1 fusion.24
  89.0 0.0 collective-permute-start.6
  89.1 0.2 copy-done
  89.2 0.3 copy-done.1
  89.6 1.2 fusion.23
  90.8 0.9 collective-permute-start.5
  91.7 0.4 collective-permute-start.4
  92.1 1.7 %collective-permute-start.3 = (bf16[2,4,128,128]{3,2,1,0:T(8,128)(2,1)}, bf16[2,4,128,128]{3,2,1,0:T(8,128)(2,1)}, u32[]{:S(2)}, u32[]{:S(2)}) collective-permute-start(bf16[2,4,128,128]{3,2,1,0:T(8,128)(2,1)} %get-tuple-element.33), channel_id=1, source_target_pairs={{0,4},{1,5},{2,6},{3,7},{4,0},{5,1},{6,2},{7,3},{8,12},{9,13},{10,... | collective-permute-start | bytes 786440 | tf_op jit(solution)/shard_map/ppermute | solution.py:203
  93.8 1.8 %collective-permute-start.2 = (bf16[2,4,128,128]{3,2,1,0:T(8,128)(2,1)}, bf16[2,4,128,128]{3,2,1,0:T(8,128)(2,1)}, u32[]{:S(2)}, u32[]{:S(2)}) collective-permute-start(bf16[2,4,128,128]{3,2,1,0:T(8,128)(2,1)} %get-tuple-element.32), channel_id=1, source_target_pairs={{0,3},{1,4},{2,5},{3,6},{4,7},{5,0},{6,1},{7,2},{8,11},{9,12},{10,... | collective-permute-start | bytes 786440 | tf_op jit(solution)/shard_map/ppermute | solution.py:203
  95.6 3.1 %dynamic-slice_bitcast_fusion.2 = (bf16[8,3,128,128]{3,2,1,0:T(8,128)(2,1)}, bf16[8,3,128,128]{3,2,1,0:T(8,128)(2,1)}, bf16[8,3,128,128]{3,2,1,0:T(8,128)(2,1)}) fusion(bf16[4,8,3,128,128]{4,3,2,1,0:T(8,128)(2,1)} %get-tuple-element.16, s32[]{:T(128)S(6)} %select_n.151, s32[]{:T(128)S(6)} %select_n.155, s32[]{:T(128)S(6)} %select_n.153), kind=kLoop, calls=%fused_computation.23 | loop fusion | bytes 4718604 | tf_op jit(solution)/shard_map/jit(dynamic_index_in_dim)/squeeze | solution.py:213
  98.7 1.8 %collective-permute-start.9 = (bf16[8,3,128,128]{3,2,1,0:T(8,128)(2,1)}, bf16[8,3,128,128]{3,2,1,0:T(8,128)(2,1)S(1)}, u32[]{:S(2)}, u32[]{:S(2)}) collective-permute-start(bf16[8,3,128,128]{3,2,1,0:T(8,128)(2,1)} %get-tuple-element.28), channel_id=1, source_target_pairs={{0,24},{8,0},{16,8},{24,16},{1,25},{9,1},{17,9},{25,17},{2,26},{10... | collective-permute-start | bytes 2359304 | tf_op jit(solution)/shard_map/ppermute | solution.py:215
  100.6 0.7 collective-permute-start.8
  101.3 1.2 collective-permute-done.4
  102.5 0.4 collective-permute-start.7
  102.8 7.9 %collective-permute-start.1 = (bf16[2,4,128,128]{3,2,1,0:T(8,128)(2,1)}, bf16[2,4,128,128]{3,2,1,0:T(8,128)(2,1)}, u32[]{:S(2)}, u32[]{:S(2)}) collective-permute-start(bf16[2,4,128,128]{3,2,1,0:T(8,128)(2,1)} %get-tuple-element.31), channel_id=1, source_target_pairs={{0,2},{1,3},{2,4},{3,5},{4,6},{5,7},{6,0},{7,1},{8,10},{9,11},{10,... | collective-permute-start | bytes 786440 | tf_op jit(solution)/shard_map/ppermute | solution.py:203
  110.7 4.6 %collective-permute-start = (bf16[2,4,128,128]{3,2,1,0:T(8,128)(2,1)}, bf16[2,4,128,128]{3,2,1,0:T(8,128)(2,1)}, u32[]{:S(2)}, u32[]{:S(2)}) collective-permute-start(bf16[2,4,128,128]{3,2,1,0:T(8,128)(2,1)} %get-tuple-element.30), channel_id=1, source_target_pairs={{0,1},{1,2},{2,3},{3,4},{4,5},{5,6},{6,7},{7,0},{8,9},{9,10},{10,1... | collective-permute-start | bytes 786440 | tf_op jit(solution)/shard_map/ppermute | solution.py:203
  115.3 2.1 %collective-permute-done.1 = bf16[2,4,128,128]{3,2,1,0:T(8,128)(2,1)} collective-permute-done((bf16[2,4,128,128]{3,2,1,0:T(8,128)(2,1)}, bf16[2,4,128,128]{3,2,1,0:T(8,128)(2,1)}, u32[]{:S(2)}, u32[]{:S(2)}) %collective-permute-start.1) | collective-permute-done | bytes 262176 | tf_op jit(solution)/shard_map/ppermute | solution.py:203
  117.4 3.7 %collective-permute-done = bf16[2,4,128,128]{3,2,1,0:T(8,128)(2,1)} collective-permute-done((bf16[2,4,128,128]{3,2,1,0:T(8,128)(2,1)}, bf16[2,4,128,128]{3,2,1,0:T(8,128)(2,1)}, u32[]{:S(2)}, u32[]{:S(2)}) %collective-permute-start) | collective-permute-done | bytes 262176 | tf_op jit(solution)/shard_map/ppermute | solution.py:203
  121.1 1.6 fusion.9
  122.7 16.0 %collective-permute-done.7 = bf16[8,3,128,128]{3,2,1,0:T(8,128)(2,1)} collective-permute-done((bf16[8,3,128,128]{3,2,1,0:T(8,128)(2,1)}, bf16[8,3,128,128]{3,2,1,0:T(8,128)(2,1)}, u32[]{:S(2)}, u32[]{:S(2)}) %collective-permute-start.7) | collective-permute-done | bytes 786464 | tf_op jit(solution)/shard_map/ppermute | solution.py:215
  138.7 2.1 %fusion.2 = bf16[8,3,128,128]{3,2,1,0:T(8,128)(2,1)S(1)} fusion(bf16[8,3,128,128]{3,2,1,0:T(8,128)(2,1)S(1)} %collective-permute-done.9, bf16[8,3,128,128]{3,2,1,0:T(8,128)(2,1)} %collective-permute-done.8, bf16[8,3,128,128]{3,2,1,0:T(8,128)(2,1)} %collective-permute-done.7, bf16[4,8,3,128,128]{4,3,2,1,0:T(8,128)(2,1)} %get-tuple-element.16, s32[]{:T(128)S(6)} %select_n.149), kind=kLoop, calls=%fused_computation.20 | loop fusion | flops 3145728 | bytes 3932164 | tf_op jit(solution)/shard_map/convert_element_type | solution.py:216
  140.8 0.1 dynamic-slice_bitcast_fusion.9
  140.9 5.7 %collective-permute-start.16 = (bf16[3,128,128]{2,1,0:T(8,128)(2,1)S(1)}, bf16[3,128,128]{2,1,0:T(8,128)(2,1)S(1)}, u32[]{:S(2)}, u32[]{:S(2)}) collective-permute-start(bf16[3,128,128]{2,1,0:T(8,128)(2,1)S(1)} %get-tuple-element.41), channel_id=1, source_target_pairs={{0,224},{32,0},{64,32},{96,64},{128,96},{160,128},{192,160},{224,1... | collective-permute-start | bytes 294920 | tf_op jit(solution)/shard_map/ppermute | solution.py:226
  146.6 1.2 collective-permute-start.15
  147.7 0.5 collective-permute-start.14
  148.3 4.5 %collective-permute-start.13 = (bf16[3,128,128]{2,1,0:T(8,128)(2,1)S(1)}, bf16[3,128,128]{2,1,0:T(8,128)(2,1)S(1)}, u32[]{:S(2)}, u32[]{:S(2)}) collective-permute-start(bf16[3,128,128]{2,1,0:T(8,128)(2,1)S(1)} %get-tuple-element.44), channel_id=1, source_target_pairs={{0,128},{32,160},{64,192},{96,224},{128,0},{160,32},{192,64},{224,... | collective-permute-start | bytes 294920 | tf_op jit(solution)/shard_map/ppermute | solution.py:226
  152.8 2.2 %collective-permute-start.11 = (bf16[3,128,128]{2,1,0:T(8,128)(2,1)S(1)}, bf16[3,128,128]{2,1,0:T(8,128)(2,1)S(1)}, u32[]{:S(2)}, u32[]{:S(2)}) collective-permute-start(bf16[3,128,128]{2,1,0:T(8,128)(2,1)S(1)} %get-tuple-element.46), channel_id=1, source_target_pairs={{0,64},{32,96},{64,128},{96,160},{128,192},{160,224},{192,0},{224,... | collective-permute-start | bytes 294920 | tf_op jit(solution)/shard_map/ppermute | solution.py:226
  154.9 1.4 collective-permute-start.10
  156.3 0.7 copy_bitcast_fusion.1
  157.0 1.6 collective-permute-done.13
  158.6 3.5 %collective-permute-done.12 = bf16[3,128,128]{2,1,0:T(8,128)(2,1)S(1)} collective-permute-done((bf16[3,128,128]{2,1,0:T(8,128)(2,1)S(1)}, bf16[3,128,128]{2,1,0:T(8,128)(2,1)S(1)}, u32[]{:S(2)}, u32[]{:S(2)}) %collective-permute-start.12) | collective-permute-done | bytes 98336 | tf_op jit(solution)/shard_map/ppermute | solution.py:226
  162.2 7.0 %collective-permute-done.11 = bf16[3,128,128]{2,1,0:T(8,128)(2,1)S(1)} collective-permute-done((bf16[3,128,128]{2,1,0:T(8,128)(2,1)S(1)}, bf16[3,128,128]{2,1,0:T(8,128)(2,1)S(1)}, u32[]{:S(2)}, u32[]{:S(2)}) %collective-permute-start.11) | collective-permute-done | bytes 98336 | tf_op jit(solution)/shard_map/ppermute | solution.py:226
  169.1 1.9 %collective-permute-done.10 = bf16[3,128,128]{2,1,0:T(8,128)(2,1)S(1)} collective-permute-done((bf16[3,128,128]{2,1,0:T(8,128)(2,1)S(1)}, bf16[3,128,128]{2,1,0:T(8,128)(2,1)S(1)}, u32[]{:S(2)}, u32[]{:S(2)}) %collective-permute-start.10) | collective-permute-done | bytes 98336 | tf_op jit(solution)/shard_map/ppermute | solution.py:226
  171.1 0.1 fusion.31
  171.2 0.7 slice_bitcast_fusion.2
  171.8 0.7 copy.24
  (14 shorter events, 0.0 us)
Async XLA Ops:
  3.6 32.9 %all-to-all-start = ((bf16[8,2,128,512]{2,3,1,0:T(8,128)(2,1)}), bf16[8,2,128,512]{2,3,1,0:T(8,128)(2,1)S(1)}, u32[]{:S(2)}, u32[]{:S(2)}) async-start(bf16[8,2,128,512]{2,3,1,0:T(8,128)(2,1)} %broadcast_in_dim.4), calls=%async_computation | async-start | bytes 4194304 | tf_op jit(solution)/shard_map/all_to_all | solution.py:186
  39.1 1.6 copy-start.2
  87.9 1.4 copy-start
  87.9 1.7 copy-start.1
  89.0 9.7 %collective-permute-start.6 = (bf16[2,4,128,128]{3,2,1,0:T(8,128)(2,1)S(1)}, bf16[2,4,128,128]{3,2,1,0:T(8,128)(2,1)S(1)}, u32[]{:S(2)}, u32[]{:S(2)}) collective-permute-start(bf16[2,4,128,128]{3,2,1,0:T(8,128)(2,1)S(1)} %fusion.24), channel_id=1, source_target_pairs={{0,7},{1,0},{2,1},{3,2},{4,3},{5,4},{6,5},{7,6},{8,15},{9,8},{10,9... | collective-permute-start | bytes 786440 | tf_op jit(solution)/shard_map/ppermute | solution.py:203
  90.8 9.8 %collective-permute-start.5 = (bf16[2,4,128,128]{3,2,1,0:T(8,128)(2,1)}, bf16[2,4,128,128]{3,2,1,0:T(8,128)(2,1)S(1)}, u32[]{:S(2)}, u32[]{:S(2)}) collective-permute-start(bf16[2,4,128,128]{3,2,1,0:T(8,128)(2,1)} %get-tuple-element.35), channel_id=1, source_target_pairs={{0,6},{1,7},{2,0},{3,1},{4,2},{5,3},{6,4},{7,5},{8,14},{9,15},{10,... | collective-permute-start | bytes 786440 | tf_op jit(solution)/shard_map/ppermute | solution.py:203
  91.7 10.8 %collective-permute-start.4 = (bf16[2,4,128,128]{3,2,1,0:T(8,128)(2,1)}, bf16[2,4,128,128]{3,2,1,0:T(8,128)(2,1)}, u32[]{:S(2)}, u32[]{:S(2)}) collective-permute-start(bf16[2,4,128,128]{3,2,1,0:T(8,128)(2,1)} %get-tuple-element.34), channel_id=1, source_target_pairs={{0,5},{1,6},{2,7},{3,0},{4,1},{5,2},{6,3},{7,4},{8,13},{9,14},{10,... | collective-permute-start | bytes 786440 | tf_op jit(solution)/shard_map/ppermute | solution.py:203
  92.1 10.7 %collective-permute-start.3 = (bf16[2,4,128,128]{3,2,1,0:T(8,128)(2,1)}, bf16[2,4,128,128]{3,2,1,0:T(8,128)(2,1)}, u32[]{:S(2)}, u32[]{:S(2)}) collective-permute-start(bf16[2,4,128,128]{3,2,1,0:T(8,128)(2,1)} %get-tuple-element.33), channel_id=1, source_target_pairs={{0,4},{1,5},{2,6},{3,7},{4,0},{5,1},{6,2},{7,3},{8,12},{9,13},{10,... | collective-permute-start | bytes 786440 | tf_op jit(solution)/shard_map/ppermute | solution.py:203
  93.8 16.9 %collective-permute-start.2 = (bf16[2,4,128,128]{3,2,1,0:T(8,128)(2,1)}, bf16[2,4,128,128]{3,2,1,0:T(8,128)(2,1)}, u32[]{:S(2)}, u32[]{:S(2)}) collective-permute-start(bf16[2,4,128,128]{3,2,1,0:T(8,128)(2,1)} %get-tuple-element.32), channel_id=1, source_target_pairs={{0,3},{1,4},{2,5},{3,6},{4,7},{5,0},{6,1},{7,2},{8,11},{9,12},{10,... | collective-permute-start | bytes 786440 | tf_op jit(solution)/shard_map/ppermute | solution.py:203
  98.7 23.9 %collective-permute-start.9 = (bf16[8,3,128,128]{3,2,1,0:T(8,128)(2,1)}, bf16[8,3,128,128]{3,2,1,0:T(8,128)(2,1)S(1)}, u32[]{:S(2)}, u32[]{:S(2)}) collective-permute-start(bf16[8,3,128,128]{3,2,1,0:T(8,128)(2,1)} %get-tuple-element.28), channel_id=1, source_target_pairs={{0,24},{8,0},{16,8},{24,16},{1,25},{9,1},{17,9},{25,17},{2,26},{10... | collective-permute-start | bytes 2359304 | tf_op jit(solution)/shard_map/ppermute | solution.py:215
  100.6 22.1 %collective-permute-start.8 = (bf16[8,3,128,128]{3,2,1,0:T(8,128)(2,1)}, bf16[8,3,128,128]{3,2,1,0:T(8,128)(2,1)}, u32[]{:S(2)}, u32[]{:S(2)}) collective-permute-start(bf16[8,3,128,128]{3,2,1,0:T(8,128)(2,1)} %get-tuple-element.29), channel_id=1, source_target_pairs={{0,16},{8,24},{16,0},{24,8},{1,17},{9,25},{17,1},{25,9},{2,18},{10... | collective-permute-start | bytes 2359304 | tf_op jit(solution)/shard_map/ppermute | solution.py:215
  102.5 36.2 %collective-permute-start.7 = (bf16[8,3,128,128]{3,2,1,0:T(8,128)(2,1)}, bf16[8,3,128,128]{3,2,1,0:T(8,128)(2,1)}, u32[]{:S(2)}, u32[]{:S(2)}) collective-permute-start(bf16[8,3,128,128]{3,2,1,0:T(8,128)(2,1)} %get-tuple-element.27), channel_id=1, source_target_pairs={{0,8},{8,16},{16,24},{24,0},{1,9},{9,17},{17,25},{25,1},{2,10},{10... | collective-permute-start | bytes 2359304 | tf_op jit(solution)/shard_map/ppermute | solution.py:215
  102.8 14.6 %collective-permute-start.1 = (bf16[2,4,128,128]{3,2,1,0:T(8,128)(2,1)}, bf16[2,4,128,128]{3,2,1,0:T(8,128)(2,1)}, u32[]{:S(2)}, u32[]{:S(2)}) collective-permute-start(bf16[2,4,128,128]{3,2,1,0:T(8,128)(2,1)} %get-tuple-element.31), channel_id=1, source_target_pairs={{0,2},{1,3},{2,4},{3,5},{4,6},{5,7},{6,0},{7,1},{8,10},{9,11},{10,... | collective-permute-start | bytes 786440 | tf_op jit(solution)/shard_map/ppermute | solution.py:203
  110.7 10.4 %collective-permute-start = (bf16[2,4,128,128]{3,2,1,0:T(8,128)(2,1)}, bf16[2,4,128,128]{3,2,1,0:T(8,128)(2,1)}, u32[]{:S(2)}, u32[]{:S(2)}) collective-permute-start(bf16[2,4,128,128]{3,2,1,0:T(8,128)(2,1)} %get-tuple-element.30), channel_id=1, source_target_pairs={{0,1},{1,2},{2,3},{3,4},{4,5},{5,6},{6,7},{7,0},{8,9},{9,10},{10,1... | collective-permute-start | bytes 786440 | tf_op jit(solution)/shard_map/ppermute | solution.py:203
  140.9 11.9 %collective-permute-start.16 = (bf16[3,128,128]{2,1,0:T(8,128)(2,1)S(1)}, bf16[3,128,128]{2,1,0:T(8,128)(2,1)S(1)}, u32[]{:S(2)}, u32[]{:S(2)}) collective-permute-start(bf16[3,128,128]{2,1,0:T(8,128)(2,1)S(1)} %get-tuple-element.41), channel_id=1, source_target_pairs={{0,224},{32,0},{64,32},{96,64},{128,96},{160,128},{192,160},{224,1... | collective-permute-start | bytes 294920 | tf_op jit(solution)/shard_map/ppermute | solution.py:226
  146.6 8.4 %collective-permute-start.15 = (bf16[3,128,128]{2,1,0:T(8,128)(2,1)S(1)}, bf16[3,128,128]{2,1,0:T(8,128)(2,1)S(1)}, u32[]{:S(2)}, u32[]{:S(2)}) collective-permute-start(bf16[3,128,128]{2,1,0:T(8,128)(2,1)S(1)} %get-tuple-element.42), channel_id=1, source_target_pairs={{0,192},{32,224},{64,0},{96,32},{128,64},{160,96},{192,128},{224,1... | collective-permute-start | bytes 294920 | tf_op jit(solution)/shard_map/ppermute | solution.py:226
  147.7 9.3 %collective-permute-start.14 = (bf16[3,128,128]{2,1,0:T(8,128)(2,1)S(1)}, bf16[3,128,128]{2,1,0:T(8,128)(2,1)S(1)}, u32[]{:S(2)}, u32[]{:S(2)}) collective-permute-start(bf16[3,128,128]{2,1,0:T(8,128)(2,1)S(1)} %get-tuple-element.43), channel_id=1, source_target_pairs={{0,160},{32,192},{64,224},{96,0},{128,32},{160,64},{192,96},{224,1... | collective-permute-start | bytes 294920 | tf_op jit(solution)/shard_map/ppermute | solution.py:226
  148.3 10.4 %collective-permute-start.13 = (bf16[3,128,128]{2,1,0:T(8,128)(2,1)S(1)}, bf16[3,128,128]{2,1,0:T(8,128)(2,1)S(1)}, u32[]{:S(2)}, u32[]{:S(2)}) collective-permute-start(bf16[3,128,128]{2,1,0:T(8,128)(2,1)S(1)} %get-tuple-element.44), channel_id=1, source_target_pairs={{0,128},{32,160},{64,192},{96,224},{128,0},{160,32},{192,64},{224,... | collective-permute-start | bytes 294920 | tf_op jit(solution)/shard_map/ppermute | solution.py:226
  152.8 9.4 %collective-permute-start.12 = (bf16[3,128,128]{2,1,0:T(8,128)(2,1)S(1)}, bf16[3,128,128]{2,1,0:T(8,128)(2,1)S(1)}, u32[]{:S(2)}, u32[]{:S(2)}) collective-permute-start(bf16[3,128,128]{2,1,0:T(8,128)(2,1)S(1)} %get-tuple-element.45), channel_id=1, source_target_pairs={{0,96},{32,128},{64,160},{96,192},{128,224},{160,0},{192,32},{224,... | collective-permute-start | bytes 294920 | tf_op jit(solution)/shard_map/ppermute | solution.py:226
  152.8 16.4 %collective-permute-start.11 = (bf16[3,128,128]{2,1,0:T(8,128)(2,1)S(1)}, bf16[3,128,128]{2,1,0:T(8,128)(2,1)S(1)}, u32[]{:S(2)}, u32[]{:S(2)}) collective-permute-start(bf16[3,128,128]{2,1,0:T(8,128)(2,1)S(1)} %get-tuple-element.46), channel_id=1, source_target_pairs={{0,64},{32,96},{64,128},{96,160},{128,192},{160,224},{192,0},{224,... | collective-permute-start | bytes 294920 | tf_op jit(solution)/shard_map/ppermute | solution.py:226
  154.9 16.1 %collective-permute-start.10 = (bf16[3,128,128]{2,1,0:T(8,128)(2,1)S(1)}, bf16[3,128,128]{2,1,0:T(8,128)(2,1)S(1)}, u32[]{:S(2)}, u32[]{:S(2)}) collective-permute-start(bf16[3,128,128]{2,1,0:T(8,128)(2,1)S(1)} %get-tuple-element.40), channel_id=1, source_target_pairs={{0,32},{32,64},{64,96},{96,128},{128,160},{160,192},{192,224},{224... | collective-permute-start | bytes 294920 | tf_op jit(solution)/shard_map/ppermute | solution.py:226

commit v7 on v6

--- a/solution.py
+++ b/solution.py
@@ -24,7 +24,7 @@
     upre[...] = jnp.zeros(upre.shape, jnp.float32)
     hgrad[...] = jnp.zeros(hgrad.shape, jnp.float32)
 
-    @pl.loop(0, slots, unroll=8)
+    @pl.loop(0, slots, unroll=4)
     def _(s):
         bg = gate_at[s]
 
@@ -56,7 +56,7 @@
     gdel[...] = (hg * u * sig * (1.0 + g * (1.0 - sig))).astype(gdel.dtype)
     udel[...] = (hg * act).astype(udel.dtype)
 
-    @pl.loop(0, slots, unroll=8)
+    @pl.loop(0, slots, unroll=4)
     def _(s):
         bg = gate_at[s]
 
@@ -99,7 +99,7 @@
     macc[...] = jnp.zeros(macc.shape, jnp.float32)
     iacc[...] = jnp.zeros(iacc.shape, jnp.float32)
 
-    @pl.loop(0, slots, unroll=8)
+    @pl.loop(0, slots, unroll=4)
     def _(s):
         bd = down_at[s]
 
@@ -182,13 +182,12 @@
 
 def gather_blocks(parts, axis, block_size):
     count = lax.axis_size(axis)
-    spread_out = jnp.broadcast_to(parts[None], (count,) + parts.shape)
+    kinds, rows, width = parts.shape
+    local = parts.reshape(kinds, rows, width // block_size, block_size).transpose(0, 2, 1, 3)
+    spread_out = jnp.broadcast_to(local[None], (count,) + local.shape)
     pieces = lax.all_to_all(spread_out, axis, 0, 0, tiled=True)
-    kinds, rows, width = parts.shape
-    pieces = pieces.reshape(count, kinds, rows, width // block_size, block_size)
-    blocks = pieces.transpose(1, 0, 3, 2, 4).reshape(kinds, -1, rows, block_size)
-    flipped = pieces.transpose(1, 0, 3, 4, 2).reshape(kinds, -1, block_size, rows)
-    return blocks, flipped
+    blocks = pieces.transpose(1, 0, 2, 3, 4).reshape(kinds, -1, rows, block_size)
+    return blocks, blocks.swapaxes(-1, -2)
 
 
 def scatter_blocks(fulls, axis):

time: 173 us -> 175 us (1.012)
  local copies, waits for them, and re-layouts: 14.9 us -> 17.8 us
    another operation x2 -> x4, local copies, waits for them, and re-layouts: 2.93 us -> 6.48 us  [layer(): (inputs, upstream), (inputs_t, upstream_t) = gather_blocks(jnp.stack([tok...]
    reshape x2 -> x0, local copies, waits for them, and re-layouts: 2.72 us -> none  [gather_blocks(): pieces = pieces.reshape(count, kinds, rows, width // block_size, block_size)]
    another operation x1 -> x2, local copies, waits for them, and re-layouts: 0.17 us -> 2.05 us  [layer(): jnp.stack([tokens, grad_out])]
where the time goes in v7:
time: 175 us
  waiting for transfers between devices  63.2 us (36%)
  Pallas kernels  44.3 us (25%)
  starting transfers between devices  42.5 us (24%)
  local copies, waits for them, and re-layouts  17.8 us (10%)
  other arithmetic  6.21 us (4%)
    pallas_call x1, Pallas kernels, front(): pl.pallas_call(_front_kernel, out_shape=(jax.ShapeDtypeStruct((inner, slo...  28.6 us
    all_to_all x1, waiting for transfers between devices, gather_blocks(): pieces = lax.all_to_all(spread_out, axis, 0, 0, tiled=True)  26.2 us
    ppermute x7, starting transfers between devices, scatter_blocks(): total = total + lax.ppermute(outgoing, axis, pairs).astype(jnp.float32)  17.3 us
    ppermute x3, waiting for transfers between devices, reduce_inner(): total = total + lax.ppermute(outgoing, inner, pairs).astype(jnp.float32)  16 us
    pallas_call x1, Pallas kernels, back(): pl.pallas_call(_back_kernel, out_shape=(jax.ShapeDtypeStruct(fshape, jnp....  15.7 us
    ppermute x7, starting transfers between devices, reduce_outer(): total = total + lax.ppermute(outgoing, outer, pairs).astype(jnp.float32)  15.6 us
    ppermute x7, waiting for transfers between devices, reduce_outer(): total = total + lax.ppermute(outgoing, outer, pairs).astype(jnp.float32)  14 us
    ppermute x7, waiting for transfers between devices, scatter_blocks(): total = total + lax.ppermute(outgoing, axis, pairs).astype(jnp.float32)  6.95 us
  transfers between devices with their start and end apart: 18, of which 9 were waited for; matrix products, arithmetic and copies ran while one was open for 4% of the time, Pallas kernels for 0%

profile of v7, /device:TPU:1, one launch (start us, length us, event | category | flops | bytes accessed | tf_op | source)
XLA Modules:
  0.0 174.7 jit_solution(7317677664805004441)
XLA Ops:
  0.6 1.0 copy.28
  1.7 1.0 copy.27
  2.7 1.9 %broadcast_in_dim.4 = bf16[8,2,4,128,128]{3,4,2,1,0:T(8,128)(2,1)} broadcast(bf16[2,4,128,128]{2,3,1,0:T(8,128)(2,1)S(1)} %maximum_bitcast_fusion), dimensions={1,2,3,4} | broadcast | bytes 2359296 | tf_op jit(solution)/shard_map/broadcast_in_dim | solution.py:187
  4.6 6.7 %all-to-all-start = ((bf16[8,2,4,128,128]{3,4,2,1,0:T(8,128)(2,1)}), bf16[8,2,4,128,128]{3,4,2,1,0:T(8,128)(2,1)S(1)}, u32[]{:S(2)}, u32[]{:S(2)}) async-start(bf16[8,2,4,128,128]{3,4,2,1,0:T(8,128)(2,1)} %broadcast_in_dim.4), calls=%async_computation | async-start | bytes 4194304 | tf_op jit(solution)/shard_map/all_to_all | solution.py:188
  11.3 26.2 %all-to-all-done = bf16[8,2,4,128,128]{3,4,2,1,0:T(8,128)(2,1)S(1)} async-done(((bf16[8,2,4,128,128]{3,4,2,1,0:T(8,128)(2,1)}), bf16[8,2,4,128,128]{3,4,2,1,0:T(8,128)(2,1)S(1)}, u32[]{:S(2)}, u32[]{:S(2)}) %all-to-all-start) | async-done | bytes 2097184 | tf_op jit(solution)/shard_map/all_to_all | solution.py:188
  37.5 1.2 fusion.32
  38.7 1.6 copy.23
  40.3 2.4 %copy.21 = bf16[1,8,4,128,128]{4,3,2,1,0:T(8,128)(2,1)} copy(bf16[1,8,4,128,128]{3,4,2,0,1:T(8,128)(2,1)} %get-tuple-element.39) | data formatting | bytes 2097152 | tf_op jit(solution)/shard_map/unstack | solution.py:236
  42.7 1.3 copy.22
  44.0 1.6 slice_bitcast_fusion
  45.6 28.6 %shard_map.119 = (bf16[4,8,3,128,128]{4,3,2,1,0:T(8,128)(2,1)}, bf16[14,128,128]{2,1,0:T(8,128)(2,1)}, bf16[14,128,128]{2,1,0:T(8,128)(2,1)}, bf16[14,128,128]{2,1,0:T(8,128)(2,1)}) custom-call(s32[32]{0:T(128)} %bitcast.102, s32[32]{0:T(128)} %bitcast.104, s32[32]{0:T(128)} %bitcast.106, bf16[32,128,128]{2,1,0:T(8,128)(2,1)} %bitcast.92, ...), custom_call_target="tpu_custom_call" | custom-call | flops 805306368 | bytes 11862016 | tf_op jit(solution)/shard_map/pallas_call | solution.py:140
  74.2 15.7 %shard_map.120 = (bf16[32,128,128]{2,1,0:T(8,128)(2,1)}, bf16[32,128,128]{2,1,0:T(8,128)(2,1)}) custom-call(s32[32]{0:T(128)} %bitcast.103, s32[32]{0:T(128)} %bitcast.105, s32[32]{0:T(128)} %bitcast.107, bf16[14,128,128]{2,1,0:T(8,128)(2,1)} %get-tuple-element.11.hid, bf16[14,128,128]{2,1,0:T(8,128)(2,1)} %get-tuple-element.12.gdel, ...), custom_call_target="tpu_custom_call" | custom-call | flops 402653184 | bytes 6619136 | tf_op jit(solution)/shard_map/pallas_call | solution.py:164
  89.9 1.1 fusion.24
  91.0 0.0 collective-permute-start.6
  91.1 0.2 copy-done
  91.2 0.3 copy-done.1
  91.6 1.2 fusion.23
  92.8 0.9 collective-permute-start.5
  93.7 0.4 collective-permute-start.4
  94.1 1.7 collective-permute-start.3
  95.8 1.8 %collective-permute-start.2 = (bf16[2,4,128,128]{3,2,1,0:T(8,128)(2,1)}, bf16[2,4,128,128]{3,2,1,0:T(8,128)(2,1)}, u32[]{:S(2)}, u32[]{:S(2)}) collective-permute-start(bf16[2,4,128,128]{3,2,1,0:T(8,128)(2,1)} %get-tuple-element.32), channel_id=1, source_target_pairs={{0,3},{1,4},{2,5},{3,6},{4,7},{5,0},{6,1},{7,2},{8,11},{9,12},{10,... | collective-permute-start | bytes 786440 | tf_op jit(solution)/shard_map/ppermute | solution.py:202
  97.6 3.1 %dynamic-slice_bitcast_fusion.2 = (bf16[8,3,128,128]{3,2,1,0:T(8,128)(2,1)}, bf16[8,3,128,128]{3,2,1,0:T(8,128)(2,1)}, bf16[8,3,128,128]{3,2,1,0:T(8,128)(2,1)}) fusion(bf16[4,8,3,128,128]{4,3,2,1,0:T(8,128)(2,1)} %get-tuple-element.16, s32[]{:T(128)S(6)} %select_n.151, s32[]{:T(128)S(6)} %select_n.155, s32[]{:T(128)S(6)} %select_n.153), kind=kLoop, calls=%fused_computation.24 | loop fusion | bytes 4718604 | tf_op jit(solution)/shard_map/jit(dynamic_index_in_dim)/squeeze | solution.py:212
  100.7 1.8 %collective-permute-start.9 = (bf16[8,3,128,128]{3,2,1,0:T(8,128)(2,1)}, bf16[8,3,128,128]{3,2,1,0:T(8,128)(2,1)S(1)}, u32[]{:S(2)}, u32[]{:S(2)}) collective-permute-start(bf16[8,3,128,128]{3,2,1,0:T(8,128)(2,1)} %get-tuple-element.28), channel_id=1, source_target_pairs={{0,24},{8,0},{16,8},{24,16},{1,25},{9,1},{17,9},{25,17},{2,26},{10... | collective-permute-start | bytes 2359304 | tf_op jit(solution)/shard_map/ppermute | solution.py:214
  102.5 0.7 collective-permute-start.8
  103.3 1.2 collective-permute-done.4
  104.5 0.4 collective-permute-start.7
  104.8 7.9 %collective-permute-start.1 = (bf16[2,4,128,128]{3,2,1,0:T(8,128)(2,1)}, bf16[2,4,128,128]{3,2,1,0:T(8,128)(2,1)}, u32[]{:S(2)}, u32[]{:S(2)}) collective-permute-start(bf16[2,4,128,128]{3,2,1,0:T(8,128)(2,1)} %get-tuple-element.31), channel_id=1, source_target_pairs={{0,2},{1,3},{2,4},{3,5},{4,6},{5,7},{6,0},{7,1},{8,10},{9,11},{10,... | collective-permute-start | bytes 786440 | tf_op jit(solution)/shard_map/ppermute | solution.py:202
  112.7 4.6 %collective-permute-start = (bf16[2,4,128,128]{3,2,1,0:T(8,128)(2,1)}, bf16[2,4,128,128]{3,2,1,0:T(8,128)(2,1)}, u32[]{:S(2)}, u32[]{:S(2)}) collective-permute-start(bf16[2,4,128,128]{3,2,1,0:T(8,128)(2,1)} %get-tuple-element.30), channel_id=1, source_target_pairs={{0,1},{1,2},{2,3},{3,4},{4,5},{5,6},{6,7},{7,0},{8,9},{9,10},{10,1... | collective-permute-start | bytes 786440 | tf_op jit(solution)/shard_map/ppermute | solution.py:202
  117.3 2.1 %collective-permute-done.1 = bf16[2,4,128,128]{3,2,1,0:T(8,128)(2,1)} collective-permute-done((bf16[2,4,128,128]{3,2,1,0:T(8,128)(2,1)}, bf16[2,4,128,128]{3,2,1,0:T(8,128)(2,1)}, u32[]{:S(2)}, u32[]{:S(2)}) %collective-permute-start.1) | collective-permute-done | bytes 262176 | tf_op jit(solution)/shard_map/ppermute | solution.py:202
  119.4 3.7 %collective-permute-done = bf16[2,4,128,128]{3,2,1,0:T(8,128)(2,1)} collective-permute-done((bf16[2,4,128,128]{3,2,1,0:T(8,128)(2,1)}, bf16[2,4,128,128]{3,2,1,0:T(8,128)(2,1)}, u32[]{:S(2)}, u32[]{:S(2)}) %collective-permute-start) | collective-permute-done | bytes 262176 | tf_op jit(solution)/shard_map/ppermute | solution.py:202
  123.1 1.6 fusion.9
  124.7 16.0 %collective-permute-done.7 = bf16[8,3,128,128]{3,2,1,0:T(8,128)(2,1)} collective-permute-done((bf16[8,3,128,128]{3,2,1,0:T(8,128)(2,1)}, bf16[8,3,128,128]{3,2,1,0:T(8,128)(2,1)}, u32[]{:S(2)}, u32[]{:S(2)}) %collective-permute-start.7) | collective-permute-done | bytes 786464 | tf_op jit(solution)/shard_map/ppermute | solution.py:214
  140.7 2.1 %fusion.2 = bf16[8,3,128,128]{3,2,1,0:T(8,128)(2,1)S(1)} fusion(bf16[8,3,128,128]{3,2,1,0:T(8,128)(2,1)S(1)} %collective-permute-done.9, bf16[8,3,128,128]{3,2,1,0:T(8,128)(2,1)} %collective-permute-done.8, bf16[8,3,128,128]{3,2,1,0:T(8,128)(2,1)} %collective-permute-done.7, bf16[4,8,3,128,128]{4,3,2,1,0:T(8,128)(2,1)} %get-tuple-element.16, s32[]{:T(128)S(6)} %select_n.149), kind=kLoop, calls=%fused_computation.19 | loop fusion | flops 3145728 | bytes 3932164 | tf_op jit(solution)/shard_map/convert_element_type | solution.py:215
  142.8 0.1 dynamic-slice_bitcast_fusion.9
  142.9 5.8 %collective-permute-start.16 = (bf16[3,128,128]{2,1,0:T(8,128)(2,1)S(1)}, bf16[3,128,128]{2,1,0:T(8,128)(2,1)S(1)}, u32[]{:S(2)}, u32[]{:S(2)}) collective-permute-start(bf16[3,128,128]{2,1,0:T(8,128)(2,1)S(1)} %get-tuple-element.41), channel_id=1, source_target_pairs={{0,224},{32,0},{64,32},{96,64},{128,96},{160,128},{192,160},{224,1... | collective-permute-start | bytes 294920 | tf_op jit(solution)/shard_map/ppermute | solution.py:225
  148.7 1.2 collective-permute-start.15
  149.9 0.5 collective-permute-start.14
  150.4 4.5 %collective-permute-start.13 = (bf16[3,128,128]{2,1,0:T(8,128)(2,1)S(1)}, bf16[3,128,128]{2,1,0:T(8,128)(2,1)S(1)}, u32[]{:S(2)}, u32[]{:S(2)}) collective-permute-start(bf16[3,128,128]{2,1,0:T(8,128)(2,1)S(1)} %get-tuple-element.44), channel_id=1, source_target_pairs={{0,128},{32,160},{64,192},{96,224},{128,0},{160,32},{192,64},{224,... | collective-permute-start | bytes 294920 | tf_op jit(solution)/shard_map/ppermute | solution.py:225
  154.9 2.2 %collective-permute-start.11 = (bf16[3,128,128]{2,1,0:T(8,128)(2,1)S(1)}, bf16[3,128,128]{2,1,0:T(8,128)(2,1)S(1)}, u32[]{:S(2)}, u32[]{:S(2)}) collective-permute-start(bf16[3,128,128]{2,1,0:T(8,128)(2,1)S(1)} %get-tuple-element.46), channel_id=1, source_target_pairs={{0,64},{32,96},{64,128},{96,160},{128,192},{160,224},{192,0},{224,... | collective-permute-start | bytes 294920 | tf_op jit(solution)/shard_map/ppermute | solution.py:225
  157.1 1.4 collective-permute-start.10
  158.5 0.7 copy_bitcast_fusion
  159.2 1.6 collective-permute-done.13
  160.8 3.5 %collective-permute-done.12 = bf16[3,128,128]{2,1,0:T(8,128)(2,1)S(1)} collective-permute-done((bf16[3,128,128]{2,1,0:T(8,128)(2,1)S(1)}, bf16[3,128,128]{2,1,0:T(8,128)(2,1)S(1)}, u32[]{:S(2)}, u32[]{:S(2)}) %collective-permute-start.12) | collective-permute-done | bytes 98336 | tf_op jit(solution)/shard_map/ppermute | solution.py:225
  164.3 7.0 %collective-permute-done.11 = bf16[3,128,128]{2,1,0:T(8,128)(2,1)S(1)} collective-permute-done((bf16[3,128,128]{2,1,0:T(8,128)(2,1)S(1)}, bf16[3,128,128]{2,1,0:T(8,128)(2,1)S(1)}, u32[]{:S(2)}, u32[]{:S(2)}) %collective-permute-start.11) | collective-permute-done | bytes 98336 | tf_op jit(solution)/shard_map/ppermute | solution.py:225
  171.3 1.9 %collective-permute-done.10 = bf16[3,128,128]{2,1,0:T(8,128)(2,1)S(1)} collective-permute-done((bf16[3,128,128]{2,1,0:T(8,128)(2,1)S(1)}, bf16[3,128,128]{2,1,0:T(8,128)(2,1)S(1)}, u32[]{:S(2)}, u32[]{:S(2)}) %collective-permute-start.10) | collective-permute-done | bytes 98336 | tf_op jit(solution)/shard_map/ppermute | solution.py:225
  173.2 0.1 fusion.31
  173.3 0.7 slice_bitcast_fusion.4
  174.0 0.7 copy.26
  (16 shorter events, 0.1 us)
Async XLA Ops:
  4.6 32.9 %all-to-all-start = ((bf16[8,2,4,128,128]{3,4,2,1,0:T(8,128)(2,1)}), bf16[8,2,4,128,128]{3,4,2,1,0:T(8,128)(2,1)S(1)}, u32[]{:S(2)}, u32[]{:S(2)}) async-start(bf16[8,2,4,128,128]{3,4,2,1,0:T(8,128)(2,1)} %broadcast_in_dim.4), calls=%async_computation | async-start | bytes 4194304 | tf_op jit(solution)/shard_map/all_to_all | solution.py:188
  40.3 3.7 %copy-start.2 = (bf16[2,8,4,128,128]{3,4,2,1,0:T(8,128)(2,1)S(1)}, bf16[2,8,4,128,128]{3,4,2,1,0:T(8,128)(2,1)}, u32[]{:S(2)}) copy-start(bf16[2,8,4,128,128]{3,4,2,1,0:T(8,128)(2,1)} %copy.23) | copy-start | bytes 6291460
  89.9 1.4 copy-start
  89.9 1.7 copy-start.1
  91.0 9.7 %collective-permute-start.6 = (bf16[2,4,128,128]{3,2,1,0:T(8,128)(2,1)S(1)}, bf16[2,4,128,128]{3,2,1,0:T(8,128)(2,1)S(1)}, u32[]{:S(2)}, u32[]{:S(2)}) collective-permute-start(bf16[2,4,128,128]{3,2,1,0:T(8,128)(2,1)S(1)} %fusion.24), channel_id=1, source_target_pairs={{0,7},{1,0},{2,1},{3,2},{4,3},{5,4},{6,5},{7,6},{8,15},{9,8},{10,9... | collective-permute-start | bytes 786440 | tf_op jit(solution)/shard_map/ppermute | solution.py:202
  92.8 9.8 %collective-permute-start.5 = (bf16[2,4,128,128]{3,2,1,0:T(8,128)(2,1)}, bf16[2,4,128,128]{3,2,1,0:T(8,128)(2,1)S(1)}, u32[]{:S(2)}, u32[]{:S(2)}) collective-permute-start(bf16[2,4,128,128]{3,2,1,0:T(8,128)(2,1)} %get-tuple-element.35), channel_id=1, source_target_pairs={{0,6},{1,7},{2,0},{3,1},{4,2},{5,3},{6,4},{7,5},{8,14},{9,15},{10,... | collective-permute-start | bytes 786440 | tf_op jit(solution)/shard_map/ppermute | solution.py:202
  93.7 10.8 %collective-permute-start.4 = (bf16[2,4,128,128]{3,2,1,0:T(8,128)(2,1)}, bf16[2,4,128,128]{3,2,1,0:T(8,128)(2,1)}, u32[]{:S(2)}, u32[]{:S(2)}) collective-permute-start(bf16[2,4,128,128]{3,2,1,0:T(8,128)(2,1)} %get-tuple-element.34), channel_id=1, source_target_pairs={{0,5},{1,6},{2,7},{3,0},{4,1},{5,2},{6,3},{7,4},{8,13},{9,14},{10,... | collective-permute-start | bytes 786440 | tf_op jit(solution)/shard_map/ppermute | solution.py:202
  94.1 10.7 %collective-permute-start.3 = (bf16[2,4,128,128]{3,2,1,0:T(8,128)(2,1)}, bf16[2,4,128,128]{3,2,1,0:T(8,128)(2,1)}, u32[]{:S(2)}, u32[]{:S(2)}) collective-permute-start(bf16[2,4,128,128]{3,2,1,0:T(8,128)(2,1)} %get-tuple-element.33), channel_id=1, source_target_pairs={{0,4},{1,5},{2,6},{3,7},{4,0},{5,1},{6,2},{7,3},{8,12},{9,13},{10,... | collective-permute-start | bytes 786440 | tf_op jit(solution)/shard_map/ppermute | solution.py:202
  95.8 16.9 %collective-permute-start.2 = (bf16[2,4,128,128]{3,2,1,0:T(8,128)(2,1)}, bf16[2,4,128,128]{3,2,1,0:T(8,128)(2,1)}, u32[]{:S(2)}, u32[]{:S(2)}) collective-permute-start(bf16[2,4,128,128]{3,2,1,0:T(8,128)(2,1)} %get-tuple-element.32), channel_id=1, source_target_pairs={{0,3},{1,4},{2,5},{3,6},{4,7},{5,0},{6,1},{7,2},{8,11},{9,12},{10,... | collective-permute-start | bytes 786440 | tf_op jit(solution)/shard_map/ppermute | solution.py:202
  100.7 23.9 %collective-permute-start.9 = (bf16[8,3,128,128]{3,2,1,0:T(8,128)(2,1)}, bf16[8,3,128,128]{3,2,1,0:T(8,128)(2,1)S(1)}, u32[]{:S(2)}, u32[]{:S(2)}) collective-permute-start(bf16[8,3,128,128]{3,2,1,0:T(8,128)(2,1)} %get-tuple-element.28), channel_id=1, source_target_pairs={{0,24},{8,0},{16,8},{24,16},{1,25},{9,1},{17,9},{25,17},{2,26},{10... | collective-permute-start | bytes 2359304 | tf_op jit(solution)/shard_map/ppermute | solution.py:214
  102.5 22.1 %collective-permute-start.8 = (bf16[8,3,128,128]{3,2,1,0:T(8,128)(2,1)}, bf16[8,3,128,128]{3,2,1,0:T(8,128)(2,1)}, u32[]{:S(2)}, u32[]{:S(2)}) collective-permute-start(bf16[8,3,128,128]{3,2,1,0:T(8,128)(2,1)} %get-tuple-element.29), channel_id=1, source_target_pairs={{0,16},{8,24},{16,0},{24,8},{1,17},{9,25},{17,1},{25,9},{2,18},{10... | collective-permute-start | bytes 2359304 | tf_op jit(solution)/shard_map/ppermute | solution.py:214
  104.5 36.2 %collective-permute-start.7 = (bf16[8,3,128,128]{3,2,1,0:T(8,128)(2,1)}, bf16[8,3,128,128]{3,2,1,0:T(8,128)(2,1)}, u32[]{:S(2)}, u32[]{:S(2)}) collective-permute-start(bf16[8,3,128,128]{3,2,1,0:T(8,128)(2,1)} %get-tuple-element.27), channel_id=1, source_target_pairs={{0,8},{8,16},{16,24},{24,0},{1,9},{9,17},{17,25},{25,1},{2,10},{10... | collective-permute-start | bytes 2359304 | tf_op jit(solution)/shard_map/ppermute | solution.py:214
  104.8 14.6 %collective-permute-start.1 = (bf16[2,4,128,128]{3,2,1,0:T(8,128)(2,1)}, bf16[2,4,128,128]{3,2,1,0:T(8,128)(2,1)}, u32[]{:S(2)}, u32[]{:S(2)}) collective-permute-start(bf16[2,4,128,128]{3,2,1,0:T(8,128)(2,1)} %get-tuple-element.31), channel_id=1, source_target_pairs={{0,2},{1,3},{2,4},{3,5},{4,6},{5,7},{6,0},{7,1},{8,10},{9,11},{10,... | collective-permute-start | bytes 786440 | tf_op jit(solution)/shard_map/ppermute | solution.py:202
  112.7 10.4 %collective-permute-start = (bf16[2,4,128,128]{3,2,1,0:T(8,128)(2,1)}, bf16[2,4,128,128]{3,2,1,0:T(8,128)(2,1)}, u32[]{:S(2)}, u32[]{:S(2)}) collective-permute-start(bf16[2,4,128,128]{3,2,1,0:T(8,128)(2,1)} %get-tuple-element.30), channel_id=1, source_target_pairs={{0,1},{1,2},{2,3},{3,4},{4,5},{5,6},{6,7},{7,0},{8,9},{9,10},{10,1... | collective-permute-start | bytes 786440 | tf_op jit(solution)/shard_map/ppermute | solution.py:202
  142.9 12.0 %collective-permute-start.16 = (bf16[3,128,128]{2,1,0:T(8,128)(2,1)S(1)}, bf16[3,128,128]{2,1,0:T(8,128)(2,1)S(1)}, u32[]{:S(2)}, u32[]{:S(2)}) collective-permute-start(bf16[3,128,128]{2,1,0:T(8,128)(2,1)S(1)} %get-tuple-element.41), channel_id=1, source_target_pairs={{0,224},{32,0},{64,32},{96,64},{128,96},{160,128},{192,160},{224,1... | collective-permute-start | bytes 294920 | tf_op jit(solution)/shard_map/ppermute | solution.py:225
  148.7 8.4 %collective-permute-start.15 = (bf16[3,128,128]{2,1,0:T(8,128)(2,1)S(1)}, bf16[3,128,128]{2,1,0:T(8,128)(2,1)S(1)}, u32[]{:S(2)}, u32[]{:S(2)}) collective-permute-start(bf16[3,128,128]{2,1,0:T(8,128)(2,1)S(1)} %get-tuple-element.42), channel_id=1, source_target_pairs={{0,192},{32,224},{64,0},{96,32},{128,64},{160,96},{192,128},{224,1... | collective-permute-start | bytes 294920 | tf_op jit(solution)/shard_map/ppermute | solution.py:225
  149.9 9.3 %collective-permute-start.14 = (bf16[3,128,128]{2,1,0:T(8,128)(2,1)S(1)}, bf16[3,128,128]{2,1,0:T(8,128)(2,1)S(1)}, u32[]{:S(2)}, u32[]{:S(2)}) collective-permute-start(bf16[3,128,128]{2,1,0:T(8,128)(2,1)S(1)} %get-tuple-element.43), channel_id=1, source_target_pairs={{0,160},{32,192},{64,224},{96,0},{128,32},{160,64},{192,96},{224,1... | collective-permute-start | bytes 294920 | tf_op jit(solution)/shard_map/ppermute | solution.py:225
  150.4 10.4 %collective-permute-start.13 = (bf16[3,128,128]{2,1,0:T(8,128)(2,1)S(1)}, bf16[3,128,128]{2,1,0:T(8,128)(2,1)S(1)}, u32[]{:S(2)}, u32[]{:S(2)}) collective-permute-start(bf16[3,128,128]{2,1,0:T(8,128)(2,1)S(1)} %get-tuple-element.44), channel_id=1, source_target_pairs={{0,128},{32,160},{64,192},{96,224},{128,0},{160,32},{192,64},{224,... | collective-permute-start | bytes 294920 | tf_op jit(solution)/shard_map/ppermute | solution.py:225
  154.9 9.4 %collective-permute-start.12 = (bf16[3,128,128]{2,1,0:T(8,128)(2,1)S(1)}, bf16[3,128,128]{2,1,0:T(8,128)(2,1)S(1)}, u32[]{:S(2)}, u32[]{:S(2)}) collective-permute-start(bf16[3,128,128]{2,1,0:T(8,128)(2,1)S(1)} %get-tuple-element.45), channel_id=1, source_target_pairs={{0,96},{32,128},{64,160},{96,192},{128,224},{160,0},{192,32},{224,... | collective-permute-start | bytes 294920 | tf_op jit(solution)/shard_map/ppermute | solution.py:225
  154.9 16.4 %collective-permute-start.11 = (bf16[3,128,128]{2,1,0:T(8,128)(2,1)S(1)}, bf16[3,128,128]{2,1,0:T(8,128)(2,1)S(1)}, u32[]{:S(2)}, u32[]{:S(2)}) collective-permute-start(bf16[3,128,128]{2,1,0:T(8,128)(2,1)S(1)} %get-tuple-element.46), channel_id=1, source_target_pairs={{0,64},{32,96},{64,128},{96,160},{128,192},{160,224},{192,0},{224,... | collective-permute-start | bytes 294920 | tf_op jit(solution)/shard_map/ppermute | solution.py:225
  157.1 16.1 %collective-permute-start.10 = (bf16[3,128,128]{2,1,0:T(8,128)(2,1)S(1)}, bf16[3,128,128]{2,1,0:T(8,128)(2,1)S(1)}, u32[]{:S(2)}, u32[]{:S(2)}) collective-permute-start(bf16[3,128,128]{2,1,0:T(8,128)(2,1)S(1)} %get-tuple-element.40), channel_id=1, source_target_pairs={{0,32},{32,64},{64,96},{96,128},{128,160},{160,192},{192,224},{224... | collective-permute-start | bytes 294920 | tf_op jit(solution)/shard_map/ppermute | solution.py:225

commit v8 on v6

--- a/solution.py
+++ b/solution.py
@@ -24,7 +24,7 @@
     upre[...] = jnp.zeros(upre.shape, jnp.float32)
     hgrad[...] = jnp.zeros(hgrad.shape, jnp.float32)
 
-    @pl.loop(0, slots, unroll=8)
+    @pl.loop(0, slots, unroll=4)
     def _(s):
         bg = gate_at[s]
 
@@ -56,7 +56,7 @@
     gdel[...] = (hg * u * sig * (1.0 + g * (1.0 - sig))).astype(gdel.dtype)
     udel[...] = (hg * act).astype(udel.dtype)
 
-    @pl.loop(0, slots, unroll=8)
+    @pl.loop(0, slots, unroll=4)
     def _(s):
         bg = gate_at[s]
 
@@ -99,7 +99,7 @@
     macc[...] = jnp.zeros(macc.shape, jnp.float32)
     iacc[...] = jnp.zeros(iacc.shape, jnp.float32)
 
-    @pl.loop(0, slots, unroll=8)
+    @pl.loop(0, slots, unroll=4)
     def _(s):
         bd = down_at[s]
 

time: 173 us -> 173 us (level)
  no operation moved by 1% of the time
where the time goes in v8:
time: 173 us
  waiting for transfers between devices  63.5 us (37%)
  Pallas kernels  44.3 us (26%)
  starting transfers between devices  42.3 us (24%)
  local copies, waits for them, and re-layouts  14.9 us (9%)
  other arithmetic  7.17 us (4%)
    pallas_call x1, Pallas kernels, front(): pl.pallas_call(_front_kernel, out_shape=(jax.ShapeDtypeStruct((inner, slo...  28.6 us
    all_to_all x1, waiting for transfers between devices, gather_blocks(): pieces = lax.all_to_all(spread_out, axis, 0, 0, tiled=True)  26.2 us
    ppermute x7, starting transfers between devices, scatter_blocks(): total = total + lax.ppermute(outgoing, axis, pairs).astype(jnp.float32)  17.3 us
    ppermute x3, waiting for transfers between devices, reduce_inner(): total = total + lax.ppermute(outgoing, inner, pairs).astype(jnp.float32)  16 us
    pallas_call x1, Pallas kernels, back(): pl.pallas_call(_back_kernel, out_shape=(jax.ShapeDtypeStruct(fshape, jnp....  15.7 us
    ppermute x7, starting transfers between devices, reduce_outer(): total = total + lax.ppermute(outgoing, outer, pairs).astype(jnp.float32)  15.4 us
    ppermute x7, waiting for transfers between devices, reduce_outer(): total = total + lax.ppermute(outgoing, outer, pairs).astype(jnp.float32)  14.3 us
    ppermute x7, waiting for transfers between devices, scatter_blocks(): total = total + lax.ppermute(outgoing, axis, pairs).astype(jnp.float32)  6.95 us
  transfers between devices with their start and end apart: 18, of which 9 were waited for; matrix products, arithmetic and copies ran while one was open for 4% of the time, Pallas kernels for 0%

profile of v8, /device:TPU:1, one launch (start us, length us, event | category | flops | bytes accessed | tf_op | source)
XLA Modules:
  0.0 172.8 jit_solution(1986554663701563694)
XLA Ops:
  0.6 1.0 pad_maximum_fusion
  1.6 0.2 copy.19
  1.8 1.8 %broadcast_in_dim.4 = bf16[8,2,128,512]{2,3,1,0:T(8,128)(2,1)} broadcast(bf16[2,128,512]{1,2,0:T(8,128)(2,1)S(1)} %copy.19), dimensions={1,2,3} | broadcast | bytes 2359296 | tf_op jit(solution)/shard_map/broadcast_in_dim | solution.py:185
  3.6 6.7 %all-to-all-start = ((bf16[8,2,128,512]{2,3,1,0:T(8,128)(2,1)}), bf16[8,2,128,512]{2,3,1,0:T(8,128)(2,1)S(1)}, u32[]{:S(2)}, u32[]{:S(2)}) async-start(bf16[8,2,128,512]{2,3,1,0:T(8,128)(2,1)} %broadcast_in_dim.4), calls=%async_computation | async-start | bytes 4194304 | tf_op jit(solution)/shard_map/all_to_all | solution.py:186
  10.3 26.2 %all-to-all-done = bf16[8,2,128,512]{2,3,1,0:T(8,128)(2,1)S(1)} async-done(((bf16[8,2,128,512]{2,3,1,0:T(8,128)(2,1)}), bf16[8,2,128,512]{2,3,1,0:T(8,128)(2,1)S(1)}, u32[]{:S(2)}, u32[]{:S(2)}) %all-to-all-start) | async-done | bytes 2097184 | tf_op jit(solution)/shard_map/all_to_all | solution.py:186
  36.5 2.6 %copy.20 = bf16[8,2,128,4,128]{4,2,3,0,1:T(8,128)(2,1)} copy(bf16[8,2,128,4,128]{2,4,3,1,0:T(8,128)(2,1)S(1)} %bitcast.80) | data formatting | bytes 4194304 | tf_op jit(solution)/shard_map/reshape | solution.py:188
  39.1 0.1 copy.30
  39.2 1.4 copy-done.2
  40.7 1.5 fusion.33
  42.2 1.5 fusion.32
  43.6 28.6 %shard_map.119 = (bf16[4,8,3,128,128]{4,3,2,1,0:T(8,128)(2,1)}, bf16[14,128,128]{2,1,0:T(8,128)(2,1)}, bf16[14,128,128]{2,1,0:T(8,128)(2,1)}, bf16[14,128,128]{2,1,0:T(8,128)(2,1)}) custom-call(s32[32]{0:T(128)} %bitcast.102, s32[32]{0:T(128)} %bitcast.104, s32[32]{0:T(128)} %bitcast.106, bf16[32,128,128]{2,1,0:T(8,128)(2,1)} %bitcast.97, ...), custom_call_target="tpu_custom_call" | custom-call | flops 805306368 | bytes 11862016 | tf_op jit(solution)/shard_map/pallas_call | solution.py:140
  72.2 15.7 %shard_map.120 = (bf16[32,128,128]{2,1,0:T(8,128)(2,1)}, bf16[32,128,128]{2,1,0:T(8,128)(2,1)}) custom-call(s32[32]{0:T(128)} %bitcast.103, s32[32]{0:T(128)} %bitcast.105, s32[32]{0:T(128)} %bitcast.107, bf16[14,128,128]{2,1,0:T(8,128)(2,1)} %get-tuple-element.11.hid, bf16[14,128,128]{2,1,0:T(8,128)(2,1)} %get-tuple-element.12.gdel, ...), custom_call_target="tpu_custom_call" | custom-call | flops 402653184 | bytes 6619136 | tf_op jit(solution)/shard_map/pallas_call | solution.py:164
  87.9 1.1 fusion.24
  89.0 0.0 collective-permute-start.6
  89.1 0.2 copy-done
  89.2 0.3 copy-done.1
  89.6 1.2 fusion.23
  90.8 0.9 collective-permute-start.5
  91.7 0.4 collective-permute-start.4
  92.1 1.7 %collective-permute-start.3 = (bf16[2,4,128,128]{3,2,1,0:T(8,128)(2,1)}, bf16[2,4,128,128]{3,2,1,0:T(8,128)(2,1)}, u32[]{:S(2)}, u32[]{:S(2)}) collective-permute-start(bf16[2,4,128,128]{3,2,1,0:T(8,128)(2,1)} %get-tuple-element.33), channel_id=1, source_target_pairs={{0,4},{1,5},{2,6},{3,7},{4,0},{5,1},{6,2},{7,3},{8,12},{9,13},{10,... | collective-permute-start | bytes 786440 | tf_op jit(solution)/shard_map/ppermute | solution.py:203
  93.8 1.8 %collective-permute-start.2 = (bf16[2,4,128,128]{3,2,1,0:T(8,128)(2,1)}, bf16[2,4,128,128]{3,2,1,0:T(8,128)(2,1)}, u32[]{:S(2)}, u32[]{:S(2)}) collective-permute-start(bf16[2,4,128,128]{3,2,1,0:T(8,128)(2,1)} %get-tuple-element.32), channel_id=1, source_target_pairs={{0,3},{1,4},{2,5},{3,6},{4,7},{5,0},{6,1},{7,2},{8,11},{9,12},{10,... | collective-permute-start | bytes 786440 | tf_op jit(solution)/shard_map/ppermute | solution.py:203
  95.6 3.1 %dynamic-slice_bitcast_fusion.2 = (bf16[8,3,128,128]{3,2,1,0:T(8,128)(2,1)}, bf16[8,3,128,128]{3,2,1,0:T(8,128)(2,1)}, bf16[8,3,128,128]{3,2,1,0:T(8,128)(2,1)}) fusion(bf16[4,8,3,128,128]{4,3,2,1,0:T(8,128)(2,1)} %get-tuple-element.16, s32[]{:T(128)S(6)} %select_n.151, s32[]{:T(128)S(6)} %select_n.155, s32[]{:T(128)S(6)} %select_n.153), kind=kLoop, calls=%fused_computation.23 | loop fusion | bytes 4718604 | tf_op jit(solution)/shard_map/jit(dynamic_index_in_dim)/squeeze | solution.py:213
  98.8 1.8 %collective-permute-start.9 = (bf16[8,3,128,128]{3,2,1,0:T(8,128)(2,1)}, bf16[8,3,128,128]{3,2,1,0:T(8,128)(2,1)S(1)}, u32[]{:S(2)}, u32[]{:S(2)}) collective-permute-start(bf16[8,3,128,128]{3,2,1,0:T(8,128)(2,1)} %get-tuple-element.28), channel_id=1, source_target_pairs={{0,24},{8,0},{16,8},{24,16},{1,25},{9,1},{17,9},{25,17},{2,26},{10... | collective-permute-start | bytes 2359304 | tf_op jit(solution)/shard_map/ppermute | solution.py:215
  100.6 0.7 collective-permute-start.8
  101.3 1.2 collective-permute-done.4
  102.5 0.4 collective-permute-start.7
  102.8 7.9 %collective-permute-start.1 = (bf16[2,4,128,128]{3,2,1,0:T(8,128)(2,1)}, bf16[2,4,128,128]{3,2,1,0:T(8,128)(2,1)}, u32[]{:S(2)}, u32[]{:S(2)}) collective-permute-start(bf16[2,4,128,128]{3,2,1,0:T(8,128)(2,1)} %get-tuple-element.31), channel_id=1, source_target_pairs={{0,2},{1,3},{2,4},{3,5},{4,6},{5,7},{6,0},{7,1},{8,10},{9,11},{10,... | collective-permute-start | bytes 786440 | tf_op jit(solution)/shard_map/ppermute | solution.py:203
  110.7 4.6 %collective-permute-start = (bf16[2,4,128,128]{3,2,1,0:T(8,128)(2,1)}, bf16[2,4,128,128]{3,2,1,0:T(8,128)(2,1)}, u32[]{:S(2)}, u32[]{:S(2)}) collective-permute-start(bf16[2,4,128,128]{3,2,1,0:T(8,128)(2,1)} %get-tuple-element.30), channel_id=1, source_target_pairs={{0,1},{1,2},{2,3},{3,4},{4,5},{5,6},{6,7},{7,0},{8,9},{9,10},{10,1... | collective-permute-start | bytes 786440 | tf_op jit(solution)/shard_map/ppermute | solution.py:203
  115.3 2.1 %collective-permute-done.1 = bf16[2,4,128,128]{3,2,1,0:T(8,128)(2,1)} collective-permute-done((bf16[2,4,128,128]{3,2,1,0:T(8,128)(2,1)}, bf16[2,4,128,128]{3,2,1,0:T(8,128)(2,1)}, u32[]{:S(2)}, u32[]{:S(2)}) %collective-permute-start.1) | collective-permute-done | bytes 262176 | tf_op jit(solution)/shard_map/ppermute | solution.py:203
  117.4 3.7 %collective-permute-done = bf16[2,4,128,128]{3,2,1,0:T(8,128)(2,1)} collective-permute-done((bf16[2,4,128,128]{3,2,1,0:T(8,128)(2,1)}, bf16[2,4,128,128]{3,2,1,0:T(8,128)(2,1)}, u32[]{:S(2)}, u32[]{:S(2)}) %collective-permute-start) | collective-permute-done | bytes 262176 | tf_op jit(solution)/shard_map/ppermute | solution.py:203
  121.1 1.6 fusion.9
  122.7 16.0 %collective-permute-done.7 = bf16[8,3,128,128]{3,2,1,0:T(8,128)(2,1)} collective-permute-done((bf16[8,3,128,128]{3,2,1,0:T(8,128)(2,1)}, bf16[8,3,128,128]{3,2,1,0:T(8,128)(2,1)}, u32[]{:S(2)}, u32[]{:S(2)}) %collective-permute-start.7) | collective-permute-done | bytes 786464 | tf_op jit(solution)/shard_map/ppermute | solution.py:215
  138.7 2.1 %fusion.2 = bf16[8,3,128,128]{3,2,1,0:T(8,128)(2,1)S(1)} fusion(bf16[8,3,128,128]{3,2,1,0:T(8,128)(2,1)S(1)} %collective-permute-done.9, bf16[8,3,128,128]{3,2,1,0:T(8,128)(2,1)} %collective-permute-done.8, bf16[8,3,128,128]{3,2,1,0:T(8,128)(2,1)} %collective-permute-done.7, bf16[4,8,3,128,128]{4,3,2,1,0:T(8,128)(2,1)} %get-tuple-element.16, s32[]{:T(128)S(6)} %select_n.149), kind=kLoop, calls=%fused_computation.20 | loop fusion | flops 3145728 | bytes 3932164 | tf_op jit(solution)/shard_map/convert_element_type | solution.py:216
  140.8 0.1 dynamic-slice_bitcast_fusion.9
  140.9 5.7 %collective-permute-start.16 = (bf16[3,128,128]{2,1,0:T(8,128)(2,1)S(1)}, bf16[3,128,128]{2,1,0:T(8,128)(2,1)S(1)}, u32[]{:S(2)}, u32[]{:S(2)}) collective-permute-start(bf16[3,128,128]{2,1,0:T(8,128)(2,1)S(1)} %get-tuple-element.41), channel_id=1, source_target_pairs={{0,224},{32,0},{64,32},{96,64},{128,96},{160,128},{192,160},{224,1... | collective-permute-start | bytes 294920 | tf_op jit(solution)/shard_map/ppermute | solution.py:226
  146.6 1.2 collective-permute-start.15
  147.8 0.5 collective-permute-start.14
  148.3 4.5 %collective-permute-start.13 = (bf16[3,128,128]{2,1,0:T(8,128)(2,1)S(1)}, bf16[3,128,128]{2,1,0:T(8,128)(2,1)S(1)}, u32[]{:S(2)}, u32[]{:S(2)}) collective-permute-start(bf16[3,128,128]{2,1,0:T(8,128)(2,1)S(1)} %get-tuple-element.44), channel_id=1, source_target_pairs={{0,128},{32,160},{64,192},{96,224},{128,0},{160,32},{192,64},{224,... | collective-permute-start | bytes 294920 | tf_op jit(solution)/shard_map/ppermute | solution.py:226
  152.8 2.3 %collective-permute-start.11 = (bf16[3,128,128]{2,1,0:T(8,128)(2,1)S(1)}, bf16[3,128,128]{2,1,0:T(8,128)(2,1)S(1)}, u32[]{:S(2)}, u32[]{:S(2)}) collective-permute-start(bf16[3,128,128]{2,1,0:T(8,128)(2,1)S(1)} %get-tuple-element.46), channel_id=1, source_target_pairs={{0,64},{32,96},{64,128},{96,160},{128,192},{160,224},{192,0},{224,... | collective-permute-start | bytes 294920 | tf_op jit(solution)/shard_map/ppermute | solution.py:226
  155.1 1.2 collective-permute-start.10
  156.3 0.7 copy_bitcast_fusion.1
  157.0 1.6 collective-permute-done.13
  158.6 3.8 %collective-permute-done.12 = bf16[3,128,128]{2,1,0:T(8,128)(2,1)S(1)} collective-permute-done((bf16[3,128,128]{2,1,0:T(8,128)(2,1)S(1)}, bf16[3,128,128]{2,1,0:T(8,128)(2,1)S(1)}, u32[]{:S(2)}, u32[]{:S(2)}) %collective-permute-start.12) | collective-permute-done | bytes 98336 | tf_op jit(solution)/shard_map/ppermute | solution.py:226
  162.4 6.8 %collective-permute-done.11 = bf16[3,128,128]{2,1,0:T(8,128)(2,1)S(1)} collective-permute-done((bf16[3,128,128]{2,1,0:T(8,128)(2,1)S(1)}, bf16[3,128,128]{2,1,0:T(8,128)(2,1)S(1)}, u32[]{:S(2)}, u32[]{:S(2)}) %collective-permute-start.11) | collective-permute-done | bytes 98336 | tf_op jit(solution)/shard_map/ppermute | solution.py:226
  169.2 2.1 %collective-permute-done.10 = bf16[3,128,128]{2,1,0:T(8,128)(2,1)S(1)} collective-permute-done((bf16[3,128,128]{2,1,0:T(8,128)(2,1)S(1)}, bf16[3,128,128]{2,1,0:T(8,128)(2,1)S(1)}, u32[]{:S(2)}, u32[]{:S(2)}) %collective-permute-start.10) | collective-permute-done | bytes 98336 | tf_op jit(solution)/shard_map/ppermute | solution.py:226
  171.3 0.1 fusion.31
  171.4 0.7 slice_bitcast_fusion.2
  172.1 0.7 copy.24
  (14 shorter events, 0.0 us)
Async XLA Ops:
  3.6 32.9 %all-to-all-start = ((bf16[8,2,128,512]{2,3,1,0:T(8,128)(2,1)}), bf16[8,2,128,512]{2,3,1,0:T(8,128)(2,1)S(1)}, u32[]{:S(2)}, u32[]{:S(2)}) async-start(bf16[8,2,128,512]{2,3,1,0:T(8,128)(2,1)} %broadcast_in_dim.4), calls=%async_computation | async-start | bytes 4194304 | tf_op jit(solution)/shard_map/all_to_all | solution.py:186
  39.1 1.6 copy-start.2
  87.9 1.4 copy-start
  87.9 1.7 copy-start.1
  89.0 9.7 %collective-permute-start.6 = (bf16[2,4,128,128]{3,2,1,0:T(8,128)(2,1)S(1)}, bf16[2,4,128,128]{3,2,1,0:T(8,128)(2,1)S(1)}, u32[]{:S(2)}, u32[]{:S(2)}) collective-permute-start(bf16[2,4,128,128]{3,2,1,0:T(8,128)(2,1)S(1)} %fusion.24), channel_id=1, source_target_pairs={{0,7},{1,0},{2,1},{3,2},{4,3},{5,4},{6,5},{7,6},{8,15},{9,8},{10,9... | collective-permute-start | bytes 786440 | tf_op jit(solution)/shard_map/ppermute | solution.py:203
  90.8 9.8 %collective-permute-start.5 = (bf16[2,4,128,128]{3,2,1,0:T(8,128)(2,1)}, bf16[2,4,128,128]{3,2,1,0:T(8,128)(2,1)S(1)}, u32[]{:S(2)}, u32[]{:S(2)}) collective-permute-start(bf16[2,4,128,128]{3,2,1,0:T(8,128)(2,1)} %get-tuple-element.35), channel_id=1, source_target_pairs={{0,6},{1,7},{2,0},{3,1},{4,2},{5,3},{6,4},{7,5},{8,14},{9,15},{10,... | collective-permute-start | bytes 786440 | tf_op jit(solution)/shard_map/ppermute | solution.py:203
  91.7 10.8 %collective-permute-start.4 = (bf16[2,4,128,128]{3,2,1,0:T(8,128)(2,1)}, bf16[2,4,128,128]{3,2,1,0:T(8,128)(2,1)}, u32[]{:S(2)}, u32[]{:S(2)}) collective-permute-start(bf16[2,4,128,128]{3,2,1,0:T(8,128)(2,1)} %get-tuple-element.34), channel_id=1, source_target_pairs={{0,5},{1,6},{2,7},{3,0},{4,1},{5,2},{6,3},{7,4},{8,13},{9,14},{10,... | collective-permute-start | bytes 786440 | tf_op jit(solution)/shard_map/ppermute | solution.py:203
  92.1 10.7 %collective-permute-start.3 = (bf16[2,4,128,128]{3,2,1,0:T(8,128)(2,1)}, bf16[2,4,128,128]{3,2,1,0:T(8,128)(2,1)}, u32[]{:S(2)}, u32[]{:S(2)}) collective-permute-start(bf16[2,4,128,128]{3,2,1,0:T(8,128)(2,1)} %get-tuple-element.33), channel_id=1, source_target_pairs={{0,4},{1,5},{2,6},{3,7},{4,0},{5,1},{6,2},{7,3},{8,12},{9,13},{10,... | collective-permute-start | bytes 786440 | tf_op jit(solution)/shard_map/ppermute | solution.py:203
  93.8 16.9 %collective-permute-start.2 = (bf16[2,4,128,128]{3,2,1,0:T(8,128)(2,1)}, bf16[2,4,128,128]{3,2,1,0:T(8,128)(2,1)}, u32[]{:S(2)}, u32[]{:S(2)}) collective-permute-start(bf16[2,4,128,128]{3,2,1,0:T(8,128)(2,1)} %get-tuple-element.32), channel_id=1, source_target_pairs={{0,3},{1,4},{2,5},{3,6},{4,7},{5,0},{6,1},{7,2},{8,11},{9,12},{10,... | collective-permute-start | bytes 786440 | tf_op jit(solution)/shard_map/ppermute | solution.py:203
  98.8 23.9 %collective-permute-start.9 = (bf16[8,3,128,128]{3,2,1,0:T(8,128)(2,1)}, bf16[8,3,128,128]{3,2,1,0:T(8,128)(2,1)S(1)}, u32[]{:S(2)}, u32[]{:S(2)}) collective-permute-start(bf16[8,3,128,128]{3,2,1,0:T(8,128)(2,1)} %get-tuple-element.28), channel_id=1, source_target_pairs={{0,24},{8,0},{16,8},{24,16},{1,25},{9,1},{17,9},{25,17},{2,26},{10... | collective-permute-start | bytes 2359304 | tf_op jit(solution)/shard_map/ppermute | solution.py:215
  100.6 22.1 %collective-permute-start.8 = (bf16[8,3,128,128]{3,2,1,0:T(8,128)(2,1)}, bf16[8,3,128,128]{3,2,1,0:T(8,128)(2,1)}, u32[]{:S(2)}, u32[]{:S(2)}) collective-permute-start(bf16[8,3,128,128]{3,2,1,0:T(8,128)(2,1)} %get-tuple-element.29), channel_id=1, source_target_pairs={{0,16},{8,24},{16,0},{24,8},{1,17},{9,25},{17,1},{25,9},{2,18},{10... | collective-permute-start | bytes 2359304 | tf_op jit(solution)/shard_map/ppermute | solution.py:215
  102.5 36.2 %collective-permute-start.7 = (bf16[8,3,128,128]{3,2,1,0:T(8,128)(2,1)}, bf16[8,3,128,128]{3,2,1,0:T(8,128)(2,1)}, u32[]{:S(2)}, u32[]{:S(2)}) collective-permute-start(bf16[8,3,128,128]{3,2,1,0:T(8,128)(2,1)} %get-tuple-element.27), channel_id=1, source_target_pairs={{0,8},{8,16},{16,24},{24,0},{1,9},{9,17},{17,25},{25,1},{2,10},{10... | collective-permute-start | bytes 2359304 | tf_op jit(solution)/shard_map/ppermute | solution.py:215
  102.8 14.6 %collective-permute-start.1 = (bf16[2,4,128,128]{3,2,1,0:T(8,128)(2,1)}, bf16[2,4,128,128]{3,2,1,0:T(8,128)(2,1)}, u32[]{:S(2)}, u32[]{:S(2)}) collective-permute-start(bf16[2,4,128,128]{3,2,1,0:T(8,128)(2,1)} %get-tuple-element.31), channel_id=1, source_target_pairs={{0,2},{1,3},{2,4},{3,5},{4,6},{5,7},{6,0},{7,1},{8,10},{9,11},{10,... | collective-permute-start | bytes 786440 | tf_op jit(solution)/shard_map/ppermute | solution.py:203
  110.7 10.4 %collective-permute-start = (bf16[2,4,128,128]{3,2,1,0:T(8,128)(2,1)}, bf16[2,4,128,128]{3,2,1,0:T(8,128)(2,1)}, u32[]{:S(2)}, u32[]{:S(2)}) collective-permute-start(bf16[2,4,128,128]{3,2,1,0:T(8,128)(2,1)} %get-tuple-element.30), channel_id=1, source_target_pairs={{0,1},{1,2},{2,3},{3,4},{4,5},{5,6},{6,7},{7,0},{8,9},{9,10},{10,1... | collective-permute-start | bytes 786440 | tf_op jit(solution)/shard_map/ppermute | solution.py:203
  140.9 11.9 %collective-permute-start.16 = (bf16[3,128,128]{2,1,0:T(8,128)(2,1)S(1)}, bf16[3,128,128]{2,1,0:T(8,128)(2,1)S(1)}, u32[]{:S(2)}, u32[]{:S(2)}) collective-permute-start(bf16[3,128,128]{2,1,0:T(8,128)(2,1)S(1)} %get-tuple-element.41), channel_id=1, source_target_pairs={{0,224},{32,0},{64,32},{96,64},{128,96},{160,128},{192,160},{224,1... | collective-permute-start | bytes 294920 | tf_op jit(solution)/shard_map/ppermute | solution.py:226
  146.6 8.6 %collective-permute-start.15 = (bf16[3,128,128]{2,1,0:T(8,128)(2,1)S(1)}, bf16[3,128,128]{2,1,0:T(8,128)(2,1)S(1)}, u32[]{:S(2)}, u32[]{:S(2)}) collective-permute-start(bf16[3,128,128]{2,1,0:T(8,128)(2,1)S(1)} %get-tuple-element.42), channel_id=1, source_target_pairs={{0,192},{32,224},{64,0},{96,32},{128,64},{160,96},{192,128},{224,1... | collective-permute-start | bytes 294920 | tf_op jit(solution)/shard_map/ppermute | solution.py:226
  147.8 9.3 %collective-permute-start.14 = (bf16[3,128,128]{2,1,0:T(8,128)(2,1)S(1)}, bf16[3,128,128]{2,1,0:T(8,128)(2,1)S(1)}, u32[]{:S(2)}, u32[]{:S(2)}) collective-permute-start(bf16[3,128,128]{2,1,0:T(8,128)(2,1)S(1)} %get-tuple-element.43), channel_id=1, source_target_pairs={{0,160},{32,192},{64,224},{96,0},{128,32},{160,64},{192,96},{224,1... | collective-permute-start | bytes 294920 | tf_op jit(solution)/shard_map/ppermute | solution.py:226
  148.3 10.4 %collective-permute-start.13 = (bf16[3,128,128]{2,1,0:T(8,128)(2,1)S(1)}, bf16[3,128,128]{2,1,0:T(8,128)(2,1)S(1)}, u32[]{:S(2)}, u32[]{:S(2)}) collective-permute-start(bf16[3,128,128]{2,1,0:T(8,128)(2,1)S(1)} %get-tuple-element.44), channel_id=1, source_target_pairs={{0,128},{32,160},{64,192},{96,224},{128,0},{160,32},{192,64},{224,... | collective-permute-start | bytes 294920 | tf_op jit(solution)/shard_map/ppermute | solution.py:226
  152.8 9.7 %collective-permute-start.12 = (bf16[3,128,128]{2,1,0:T(8,128)(2,1)S(1)}, bf16[3,128,128]{2,1,0:T(8,128)(2,1)S(1)}, u32[]{:S(2)}, u32[]{:S(2)}) collective-permute-start(bf16[3,128,128]{2,1,0:T(8,128)(2,1)S(1)} %get-tuple-element.45), channel_id=1, source_target_pairs={{0,96},{32,128},{64,160},{96,192},{128,224},{160,0},{192,32},{224,... | collective-permute-start | bytes 294920 | tf_op jit(solution)/shard_map/ppermute | solution.py:226
  152.8 16.5 %collective-permute-start.11 = (bf16[3,128,128]{2,1,0:T(8,128)(2,1)S(1)}, bf16[3,128,128]{2,1,0:T(8,128)(2,1)S(1)}, u32[]{:S(2)}, u32[]{:S(2)}) collective-permute-start(bf16[3,128,128]{2,1,0:T(8,128)(2,1)S(1)} %get-tuple-element.46), channel_id=1, source_target_pairs={{0,64},{32,96},{64,128},{96,160},{128,192},{160,224},{192,0},{224,... | collective-permute-start | bytes 294920 | tf_op jit(solution)/shard_map/ppermute | solution.py:226
  155.1 16.2 %collective-permute-start.10 = (bf16[3,128,128]{2,1,0:T(8,128)(2,1)S(1)}, bf16[3,128,128]{2,1,0:T(8,128)(2,1)S(1)}, u32[]{:S(2)}, u32[]{:S(2)}) collective-permute-start(bf16[3,128,128]{2,1,0:T(8,128)(2,1)S(1)} %get-tuple-element.40), channel_id=1, source_target_pairs={{0,32},{32,64},{64,96},{96,128},{128,160},{160,192},{192,224},{224... | collective-permute-start | bytes 294920 | tf_op jit(solution)/shard_map/ppermute | solution.py:226
